TPU v7x, 128 devices: a whole 4x4x4 slice. The times are simulated.
128 devices in a mesh: gx: 4 (over z_lo, core), gy: 32 (over z_hi, x, y).
Axes of the slice: x: 4, y: 4, z: 4 (z_hi: 2, z_lo: 2; z = z_hi * 2 + z_lo), core: 2. Of those that a mesh axis runs over, the one named last changes fastest.
Arguments:
- hidden: bfloat16 [1024, 16384], P('gy'), may hold values from -6 to 6
- norm_gain: bfloat16 [16384], replicated, may hold values from 0.099609375 to 1.8984375
- w_query: bfloat16 [16384, 16384], P('gx', 'gy'), may hold values from -0.046875 to 0.046875
- w_keyval: bfloat16 [16384, 2048], P('gx', 'gy'), may hold values from -0.046875 to 0.046875
- key_cache: bfloat16 [1024, 256, 8, 128], P(('gx', 'gy')), may hold values from -1000 to 1000
- value_cache: bfloat16 [1024, 256, 8, 128], P(('gx', 'gy')), may hold values from -16 to 16
- lengths: int32 [1024], P(('gx', 'gy')), may hold values from 1 to 256, as said below
- w_out: bfloat16 [16384, 16384], P('gy', 'gx'), may hold values from -0.046875 to 0.046875
Outputs:
- mixed: bfloat16 [1024, 16384], P('gy', 'gx')
Inputs may be any that keep to these rules, and one draw needn't show every extreme that they name: Slots 0 to lengths - 1 of a row are filled; some row fills all 256.
All inputs are finite; a program needn't handle non-finite values.
Results may differ from a plain program's by a relative error of at most 0.024.
Values may be sent and summed in bfloat16 or wider, within the bound.
No kernel may reach another device: no remote copies, remote signals or barrier semaphores. Data moves between devices by JAX's collectives and lax.ppermute only.
A program may use at most 128 MiB of HBM per device.

v0:
```python
import math

import jax
import jax.numpy as jnp
from jax import lax
from jax.sharding import PartitionSpec as P

GY = ("zh", "x", "y")
ALL = ("gx",) + GY


def rotate_heads(values, position, head_dim):
    half = head_dim // 2
    freq = jnp.exp(-(jnp.arange(half, dtype=jnp.float32) * 2.0 / head_dim) * math.log(500000.0))
    angle = position[:, None] * freq[None, :]
    cosine = jnp.cos(angle)[:, None, :]
    sine = jnp.sin(angle)[:, None, :]
    first = values[..., :half]
    second = values[..., half:]
    return jnp.concatenate(
        [first * cosine - second * sine, second * cosine + first * sine], axis=-1
    )


def attend_rows(query, keyval, key_cache, value_cache, lengths):
    rows, cache_len, kv_heads, head_dim = key_cache.shape
    heads = query.shape[1] // head_dim
    group = heads // kv_heads
    scale = 1.0 / math.sqrt(head_dim)
    position = lengths.astype(jnp.float32)
    rotated = rotate_heads(
        query.astype(jnp.float32).reshape(rows, heads, head_dim), position, head_dim
    ).astype(jnp.bfloat16)
    pairs = keyval.reshape(rows, 2, kv_heads, head_dim)
    new_key = rotate_heads(pairs[:, 0].astype(jnp.float32), position, head_dim).astype(jnp.bfloat16)
    new_value = pairs[:, 1].astype(jnp.float32)
    grouped = rotated.reshape(rows, kv_heads, group, head_dim)
    scores = (
        jnp.einsum("rgqd,rtgd->rgqt", grouped, key_cache, preferred_element_type=jnp.float32)
        * scale
    )
    own = jnp.einsum("rgqd,rgd->rgq", grouped, new_key, preferred_element_type=jnp.float32) * scale
    valid = jnp.arange(cache_len)[None, None, None, :] < lengths[:, None, None, None]
    scores = jnp.where(valid, scores, -jnp.inf)
    top = jnp.maximum(jnp.max(scores, axis=-1), own)
    weights = jnp.exp(scores - top[..., None])
    own_weight = jnp.exp(own - top)
    total = jnp.sum(weights, axis=-1) + own_weight
    probs = (weights / total[..., None]).astype(jnp.bfloat16)
    own_prob = (own_weight / total).astype(jnp.bfloat16)
    result = jnp.einsum("rgqt,rtgd->rgqd", probs, value_cache, preferred_element_type=jnp.float32)
    result = result + own_prob.astype(jnp.float32)[..., None] * new_value[:, :, None, :]
    return result.astype(jnp.bfloat16).reshape(rows, heads * head_dim)


def ring_all_gather(blk, axis, n, dim):
    idx = lax.axis_index(axis)
    fwd = [(i, (i + 1) % n) for i in range(n)]
    bwd = [(i, (i - 1) % n) for i in range(n)]
    out = jnp.zeros(blk.shape[:dim] + (n,) + blk.shape[dim:], blk.dtype)
    out = lax.dynamic_update_index_in_dim(out, blk, idx, dim)
    from_left = lax.ppermute(blk, axis, fwd)
    out = lax.dynamic_update_index_in_dim(out, from_left, (idx - 1) % n, dim)
    if n == 2:
        return out
    from_right = lax.ppermute(blk, axis, bwd)
    out = lax.dynamic_update_index_in_dim(out, from_right, (idx + 1) % n, dim)
    half = blk.shape[-1] // 2
    first = lax.ppermute(from_left[..., :half], axis, fwd)
    second = lax.ppermute(from_right[..., half:], axis, bwd)
    opposite = jnp.concatenate([first, second], axis=-1)
    return lax.dynamic_update_index_in_dim(out, opposite, (idx + 2) % n, dim)


def ring_reduce_scatter(arr, axis, dim):
    n = arr.shape[dim]
    idx = lax.axis_index(axis)

    def take(k):
        return lax.dynamic_index_in_dim(arr, k % n, dim, keepdims=False)

    fwd = [(i, (i + 1) % n) for i in range(n)]
    bwd = [(i, (i - 1) % n) for i in range(n)]
    if n == 2:
        return take(idx) + lax.ppermute(take(idx + 1), axis, fwd)
    half = arr.shape[-1] // 2
    opposite = take(idx + 2)
    from_right = lax.ppermute(opposite[..., :half], axis, bwd)
    from_left = lax.ppermute(opposite[..., half:], axis, fwd)
    to_left = take(idx - 1)
    to_left = jnp.concatenate([to_left[..., :half] + from_right, to_left[..., half:]], axis=-1)
    to_right = take(idx + 1)
    to_right = jnp.concatenate([to_right[..., :half], to_right[..., half:] + from_left], axis=-1)
    got_right = lax.ppermute(to_left, axis, bwd)
    got_left = lax.ppermute(to_right, axis, fwd)
    return take(idx) + got_right + got_left


def shards(hidden, norm_gain, w_query, w_keyval, key_cache, value_cache, lengths, w_out):
    width_part = w_query.shape[0]
    query_cols = w_query.shape[1]
    pair_cols = w_keyval.shape[1]
    peers = 32
    values = hidden.astype(jnp.float32)
    inverse = lax.rsqrt(jnp.mean(values * values, axis=1, keepdims=True) + 1e-05)
    normed = (values * inverse * norm_gain.astype(jnp.float32)).astype(jnp.bfloat16)
    own_cols = lax.dynamic_slice_in_dim(normed, lax.axis_index("gx") * width_part, width_part, 1)
    pair = lax.all_gather(own_cols, "zh", axis=0, tiled=False)
    first = pair[..., : width_part // 2]
    second = pair[..., width_part // 2 :]
    first = ring_all_gather(first, "y", 4, 0)
    second = ring_all_gather(second, "x", 4, 0)
    first = ring_all_gather(first, "x", 4, 0)
    second = ring_all_gather(second, "y", 4, 1)
    gathered = jnp.concatenate([first, second], axis=-1).reshape(-1, width_part)
    projected = jnp.concatenate(
        [
            jnp.dot(gathered, w_query, preferred_element_type=jnp.float32),
            jnp.dot(gathered, w_keyval, preferred_element_type=jnp.float32),
        ],
        axis=1,
    )
    projected = projected.reshape(4, 4, 2, -1, projected.shape[1]).transpose(2, 0, 1, 3, 4)
    projected = projected.reshape(-1, projected.shape[-1])
    arrived = lax.all_to_all(projected.astype(jnp.bfloat16), ALL, split_axis=0, concat_axis=0, tiled=True)
    rows_dev = arrived.shape[0] // 128
    summed = arrived.reshape(4, peers, rows_dev, query_cols + pair_cols).astype(jnp.float32).sum(axis=0)
    split_cols = summed.astype(jnp.bfloat16).transpose(1, 0, 2)
    query = split_cols[:, :, :query_cols].reshape(rows_dev, peers * query_cols)
    keyval = split_cols[:, :, query_cols:].reshape(rows_dev, peers * pair_cols)
    attended = attend_rows(query, keyval, key_cache, value_cache, lengths)
    heads_first = attended.reshape(rows_dev, peers, query_cols).transpose(1, 0, 2)
    sent = jnp.broadcast_to(heads_first[None], (4,) + heads_first.shape).reshape(-1, query_cols)
    full_rows = lax.all_to_all(sent, ALL, split_axis=0, concat_axis=0, tiled=True)
    partial_out = jnp.dot(full_rows, w_out, preferred_element_type=jnp.float32)
    part = partial_out.astype(jnp.bfloat16)
    rows, cols = part.shape
    part = part.reshape(2, 4, 4, rows // peers, cols)
    first, second = part[..., : cols // 2], part[..., cols // 2 :]
    first = ring_reduce_scatter(first, "y", 2)
    second = ring_reduce_scatter(second, "x", 1)
    first = ring_reduce_scatter(first, "x", 1)
    second = ring_reduce_scatter(second, "y", 1)
    first = ring_reduce_scatter(first, "zh", 0)
    second = ring_reduce_scatter(second, "zh", 0)
    return jnp.concatenate([first, second], axis=-1)


def solution(mesh):
    from jax.sharding import Mesh
    mesh = Mesh(mesh.devices.reshape(4, 2, 4, 4), ("gx", "zh", "x", "y"))
    in_specs = (
        P(GY, None),
        P(),
        P("gx", GY),
        P("gx", GY),
        P(("gx",) + GY, None, None, None),
        P(("gx",) + GY, None, None, None),
        P(("gx",) + GY),
        P(GY, "gx"),
    )
    out_specs = P(GY, "gx")
    return jax.shard_map(shards, mesh=mesh, in_specs=in_specs, out_specs=out_specs, check_vma=False)
```

profile of v0, /device:TPU:0, one launch (start us, length us, event | category | flops | bytes accessed | tf_op | source)
XLA Modules:
  0.0 238.6 jit_solution(11296145136008691083)
XLA Ops:
  0.0 1.4 convert_element_type.66
  1.4 1.5 multiply_reduce_fusion
  3.1 11.0 %all-gather = bf16[64,4096]{1,0:T(8,128)(2,1)S(1)} all-gather(bf16[32,4096]{1,0:T(8,128)(2,1)S(1)} %fusion.23), channel_id=2, replica_groups=mesh['gx'=4,'zh'=2,'x'=4,'y'=4] {'zh'}, dimensions={0}, use_global_device_ids=true | all-gather | bytes 786432 | tf_op jit(solution)/shard_map/all_gather | solution.py:108
  14.8 1.6 collective-permute-start
  16.4 1.7 collective-permute-start.1
  18.1 1.5 collective-permute-start.8
  19.6 1.7 collective-permute-start.9
  21.6 2.1 collective-permute-done
  24.2 3.0 %collective-permute-start.3 = (bf16[2,32,1024]{2,1,0:T(8,128)(2,1)S(1)}, bf16[2,32,1024]{2,1,0:T(8,128)(2,1)S(1)}, u32[]{:S(2)}, u32[]{:S(2)}) collective-permute-start(bf16[2,32,1024]{2,1,0:T(8,128)(2,1)S(1)} %slice.178), channel_id=1, source_target_pairs={{0,3},{1,0},{2,1},{3,2},{4,7},{5,4},{6,5},{7,6},{8,11},{9,8},{10,9... | collective-permute-start | bytes 393224 | tf_op jit(solution)/shard_map/ppermute | solution.py:70
  27.2 1.6 collective-permute-start.10
  28.8 1.8 collective-permute-start.11
  31.6 2.4 %collective-permute-start.5 = (bf16[4,2,32,2048]{3,2,1,0:T(8,128)(2,1)S(1)}, bf16[4,2,32,2048]{3,2,1,0:T(8,128)(2,1)S(1)}, u32[]{:S(2)}, u32[]{:S(2)}) collective-permute-start(bf16[4,2,32,2048]{3,2,1,0:T(8,128)(2,1)S(1)} %fusion.26), channel_id=1, source_target_pairs={{0,12},{4,0},{8,4},{12,8},{1,13},{5,1},{9,5},{13,9},{2,14},{6,2},{... | collective-permute-start | bytes 3145736 | tf_op jit(solution)/shard_map/ppermute | solution.py:66
  35.3 3.2 %collective-permute-start.13 = (bf16[4,2,32,2048]{3,2,1,0:T(8,128)(2,1)S(1)}, bf16[4,2,32,2048]{3,2,1,0:T(8,128)(2,1)S(1)}, u32[]{:S(2)}, u32[]{:S(2)}) collective-permute-start(bf16[4,2,32,2048]{3,2,1,0:T(8,128)(2,1)S(1)} %fusion.27), channel_id=1, source_target_pairs={{0,3},{1,0},{2,1},{3,2},{4,7},{5,4},{6,5},{7,6},{8,11},{9,8},{10,9... | collective-permute-start | bytes 3145736 | tf_op jit(solution)/shard_map/ppermute | solution.py:66
  38.6 2.5 %broadcast.89.clone.1 = bf16[4,4,2,32,2048]{4,3,2,1,0:T(8,128)(2,1)} broadcast(bf16[]{:T(256)} %constant.213.clone.1), dimensions={} | broadcast | bytes 4194306 | tf_op jit(solution)/shard_map/broadcast.8
  41.0 1.0 bitcast_dynamic-update-slice_fusion.5
  42.1 2.6 %broadcast.89.clone = bf16[4,4,2,32,2048]{4,3,2,1,0:T(8,128)(2,1)} broadcast(bf16[]{:T(256)} %constant.213.clone.1), dimensions={} | broadcast | bytes 4194306 | tf_op jit(solution)/shard_map/broadcast.8
  44.7 1.0 bitcast_dynamic-update-slice_fusion.2
  45.7 10.2 %collective-permute-done.4 = bf16[4,2,32,2048]{3,2,1,0:T(8,128)(2,1)S(1)} collective-permute-done((bf16[4,2,32,2048]{3,2,1,0:T(8,128)(2,1)S(1)}, bf16[4,2,32,2048]{3,2,1,0:T(8,128)(2,1)S(1)}, u32[]{:S(2)}, u32[]{:S(2)}) %collective-permute-start.4) | collective-permute-done | bytes 1048608 | tf_op jit(solution)/shard_map/ppermute | solution.py:62
  56.1 3.3 %collective-permute-start.7 = (bf16[4,2,32,1024]{3,2,1,0:T(8,128)(2,1)S(1)}, bf16[4,2,32,1024]{3,2,1,0:T(8,128)(2,1)S(1)}, u32[]{:S(2)}, u32[]{:S(2)}) collective-permute-start(bf16[4,2,32,1024]{3,2,1,0:T(8,128)(2,1)S(1)} %slice.180), channel_id=1, source_target_pairs={{0,12},{4,0},{8,4},{12,8},{1,13},{5,1},{9,5},{13,9},{2,14},{6,2},{... | collective-permute-start | bytes 1572872 | tf_op jit(solution)/shard_map/ppermute | solution.py:70
  59.5 3.5 %collective-permute-start.15 = (bf16[4,2,32,1024]{3,2,1,0:T(8,128)(2,1)S(1)}, bf16[4,2,32,1024]{3,2,1,0:T(8,128)(2,1)S(1)}, u32[]{:S(2)}, u32[]{:S(2)}) collective-permute-start(bf16[4,2,32,1024]{3,2,1,0:T(8,128)(2,1)S(1)} %slice.185), channel_id=1, source_target_pairs={{0,3},{1,0},{2,1},{3,2},{4,7},{5,4},{6,5},{7,6},{8,11},{9,8},{10,9... | collective-permute-start | bytes 1572872 | tf_op jit(solution)/shard_map/ppermute | solution.py:70
  63.0 1.0 bitcast_dynamic-update-slice_fusion.4
  64.0 1.0 bitcast_dynamic-update-slice_fusion.3
  65.1 1.0 bitcast_dynamic-update-slice_fusion.1
  66.1 1.0 bitcast_dynamic-update-slice_fusion
  67.2 1.8 collective-permute-done.6
  68.9 1.1 fusion.16
  70.0 1.8 collective-permute-done.14
  71.8 1.1 fusion.17
  72.9 7.9 %pad_maximum_fusion = bf16[4,4,2,32,4096]{4,3,2,1,0:T(8,128)(2,1)} fusion(bf16[4,4,2,32,2048]{4,3,2,1,0:T(8,128)(2,1)} %fusion.17, bf16[4,4,2,32,2048]{4,3,2,1,0:T(8,128)(2,1)} %fusion.16), kind=kLoop, calls=%fused_computation | loop fusion | flops 16777216 | bytes 16777216 | tf_op jit(solution)/shard_map/concatenate | solution.py:115
  80.8 9.2 %convolution_convert_fusion.1 = bf16[1024,512]{0,1:T(8,128)(2,1)S(1)} fusion(bf16[1024,4096]{1,0:T(8,128)(2,1)} %bitcast.131, bf16[4096,512]{1,0:T(8,128)(2,1)} %param.10), kind=kOutput, calls=%fused_computation.7 | convolution fusion | flops 4295491584 | bytes 13631488 | tf_op jit(solution)/shard_map/dot_general | solution.py:118
  90.1 2.7 %convolution_convert_fusion.2 = bf16[1024,64]{0,1:T(8,128)(2,1)S(1)} fusion(bf16[1024,4096]{1,0:T(8,128)(2,1)S(1)} %bitcast.132, bf16[4096,64]{0,1:T(8,128)(2,1)S(1)} %copy-done), kind=kOutput, calls=%fused_computation.13 | convolution fusion | flops 536936448 | bytes 9043968 | tf_op jit(solution)/shard_map/dot_general | solution.py:119
  93.6 1.3 copy.37
  94.8 7.4 %all-to-all-start = ((bf16[128,8,576]{2,1,0:T(8,128)(2,1)}), bf16[128,8,576]{2,1,0:T(8,128)(2,1)S(1)}, u32[]{:S(2)}, u32[]{:S(2)}) async-start(bf16[128,8,576]{2,1,0:T(8,128)(2,1)} %bitcast.23), calls=%async_computation | async-start | bytes 2621440 | tf_op jit(solution)/shard_map/all_to_all | solution.py:125
  102.4 20.3 %all-to-all-done = bf16[128,8,576]{2,1,0:T(8,128)(2,1)S(1)} async-done(((bf16[128,8,576]{2,1,0:T(8,128)(2,1)}), bf16[128,8,576]{2,1,0:T(8,128)(2,1)S(1)}, u32[]{:S(2)}, u32[]{:S(2)}) %all-to-all-start) | async-done | bytes 1179680 | tf_op jit(solution)/shard_map/all_to_all | solution.py:125
  124.4 3.7 %fusion.48 = (f32[8,8,16]{2,1,0:T(8,128)S(1)}, f32[8,8,16,256]{3,2,1,0:T(8,128)S(1)}) fusion(bf16[8,256,8,128]{3,2,1,0:T(8,128)(2,1)} %param.12, bf16[8,8,16,64]{3,2,1,0:T(8,128)(2,1)S(1)} %bitcast.146, bf16[8,8,16,64]{3,2,1,0:T(8,128)(2,1)S(1)} %bitcast.144, pred[8,256]{1,0:T(8,128)(4,1)S(1)} %iota_compare_fusion), kind=kOutput, calls=%fused_computation.119 | convolution fusion | flops 68418560 | bytes 5511168 | tf_op jit(solution)/shard_map/rgqd,rtgd->rgqt/dot_general | solution.py:39
  128.6 1.0 fusion.13
  130.1 23.0 %all_to_all.18 = bf16[128,8,512]{2,1,0:T(8,128)(2,1)S(1)} all-to-all(bf16[128,8,512]{2,1,0:T(8,128)(2,1)S(1)} %bitcast.139), channel_id=1, replica_groups=mesh['gx'=4,'zh'=2,'x'=4,'y'=4] {'gx','zh','x','y'}, dimensions={0} | all-to-all | bytes 2097152 | tf_op jit(solution)/shard_map/all_to_all | solution.py:134
  153.1 6.9 %convolution_convert_fusion = bf16[1024,4096]{1,0:T(8,128)(2,1)S(1)} fusion(bf16[512,4096]{1,0:T(8,128)(2,1)} %param.15, bf16[128,8,512]{2,1,0:T(8,128)(2,1)S(1)} %all_to_all.18), kind=kOutput, calls=%fused_computation.1 | convolution fusion | flops 4299161600 | bytes 13631488 | tf_op jit(solution)/shard_map/dot_general | solution.py:135
  161.1 1.7 copy-done.3
  162.7 2.5 %collective-permute-start.16 = (bf16[2,4,32,1024]{3,2,1,0:T(8,128)(2,1)S(1)}, bf16[2,4,32,1024]{3,2,1,0:T(8,128)(2,1)S(1)}, u32[]{:S(2)}, u32[]{:S(2)}) collective-permute-start(bf16[2,4,32,1024]{3,2,1,0:T(8,128)(2,1)S(1)} %get-tuple-element.18), channel_id=1, source_target_pairs={{0,3},{1,0},{2,1},{3,2},{4,7},{5,4},{6,5},{7,6},{8,11},{9,8},{10,9... | collective-permute-start | bytes 1572872 | tf_op jit(solution)/shard_map/ppermute | solution.py:88
  165.5 2.2 collective-permute-start.25
  167.7 8.9 %collective-permute-done.16 = bf16[2,4,32,1024]{3,2,1,0:T(8,128)(2,1)S(1)} collective-permute-done((bf16[2,4,32,1024]{3,2,1,0:T(8,128)(2,1)S(1)}, bf16[2,4,32,1024]{3,2,1,0:T(8,128)(2,1)S(1)}, u32[]{:S(2)}, u32[]{:S(2)}) %collective-permute-start.16) | collective-permute-done | bytes 524320 | tf_op jit(solution)/shard_map/ppermute | solution.py:88
  176.7 1.1 pad_maximum_fusion.2
  177.8 2.8 %collective-permute-start.17 = (bf16[2,4,32,2048]{3,2,1,0:T(8,128)(2,1)}, bf16[2,4,32,2048]{3,2,1,0:T(8,128)(2,1)S(1)}, u32[]{:S(2)}, u32[]{:S(2)}) collective-permute-start(bf16[2,4,32,2048]{3,2,1,0:T(8,128)(2,1)} %pad_maximum_fusion.2), channel_id=1, source_target_pairs={{0,3},{1,0},{2,1},{3,2},{4,7},{5,4},{6,5},{7,6},{8,11},{9,8},{10,9... | collective-permute-start | bytes 3145736 | tf_op jit(solution)/shard_map/ppermute | solution.py:94
  180.7 1.1 pad_maximum_fusion.3
  181.9 1.1 pad_maximum_fusion.4
  183.0 0.9 collective-permute-start.26
  184.0 1.1 pad_maximum_fusion.5
  185.0 1.2 collective-permute-start.28
  186.2 16.1 %collective-permute-done.17 = bf16[2,4,32,2048]{3,2,1,0:T(8,128)(2,1)S(1)} collective-permute-done((bf16[2,4,32,2048]{3,2,1,0:T(8,128)(2,1)}, bf16[2,4,32,2048]{3,2,1,0:T(8,128)(2,1)S(1)}, u32[]{:S(2)}, u32[]{:S(2)}) %collective-permute-start.17) | collective-permute-done | bytes 1048608 | tf_op jit(solution)/shard_map/ppermute | solution.py:94
  202.3 4.1 %collective-permute-done.19 = bf16[2,4,32,2048]{3,2,1,0:T(8,128)(2,1)S(1)} collective-permute-done((bf16[2,4,32,2048]{3,2,1,0:T(8,128)(2,1)}, bf16[2,4,32,2048]{3,2,1,0:T(8,128)(2,1)S(1)}, u32[]{:S(2)}, u32[]{:S(2)}) %collective-permute-start.19) | collective-permute-done | bytes 1048608 | tf_op jit(solution)/shard_map/ppermute | solution.py:95
  206.4 2.7 %collective-permute-done.28 = bf16[2,4,32,2048]{3,2,1,0:T(8,128)(2,1)} collective-permute-done((bf16[2,4,32,2048]{3,2,1,0:T(8,128)(2,1)}, bf16[2,4,32,2048]{3,2,1,0:T(8,128)(2,1)}, u32[]{:S(2)}, u32[]{:S(2)}) %collective-permute-start.28) | collective-permute-done | bytes 1048608 | tf_op jit(solution)/shard_map/ppermute | solution.py:95
  209.1 2.5 %fusion.18 = (bf16[2,4,32,2048]{3,2,1,0:T(8,128)(2,1)S(1)}, bf16[2,4,32,2048]{3,2,1,0:T(8,128)(2,1)S(1)}) fusion(bf16[2,4,32,2048]{3,2,1,0:T(8,128)(2,1)} %collective-permute-done.28, bf16[2,4,32,2048]{3,2,1,0:T(8,128)(2,1)} %collective-permute-done.26, bf16[2,4,4,32,2048]{4,3,2,1,0:T(8,128)(2,1)} %copy-done.4, s32[]{:T(128)S(6)} %select_n.180, ...), kind=kLoop, calls=%fused_computation.26 | loop fusion | flops 2097152 | bytes 8388616 | tf_op jit(solution)/shard_map/add | solution.py:96
  212.4 1.4 collective-permute-start.22
  213.9 2.7 %collective-permute-start.29 = (bf16[2,32,1024]{2,1,0:T(8,128)(2,1)S(1)}, bf16[2,32,1024]{2,1,0:T(8,128)(2,1)S(1)}, u32[]{:S(2)}, u32[]{:S(2)}) collective-permute-start(bf16[2,32,1024]{2,1,0:T(8,128)(2,1)S(1)} %get-tuple-element.43), channel_id=1, source_target_pairs={{0,3},{1,0},{2,1},{3,2},{4,7},{5,4},{6,5},{7,6},{8,11},{9,8},{10,9... | collective-permute-start | bytes 393224 | tf_op jit(solution)/shard_map/ppermute | solution.py:88
  216.6 1.5 collective-permute-done.20
  219.0 1.4 collective-permute-start.23
  220.5 3.0 %collective-permute-start.30 = (bf16[2,32,2048]{2,1,0:T(8,128)(2,1)S(1)}, bf16[2,32,2048]{2,1,0:T(8,128)(2,1)S(1)}, u32[]{:S(2)}, u32[]{:S(2)}) collective-permute-start(bf16[2,32,2048]{2,1,0:T(8,128)(2,1)S(1)} %pad_maximum_fusion.9), channel_id=1, source_target_pairs={{0,3},{1,0},{2,1},{3,2},{4,7},{5,4},{6,5},{7,6},{8,11},{9,8},{10,9... | collective-permute-start | bytes 786440 | tf_op jit(solution)/shard_map/ppermute | solution.py:94
  223.7 1.0 collective-permute-done.21
  224.6 2.0 collective-permute-done.23
  226.7 2.7 %collective-permute-start.24 = (bf16[32,2048]{1,0:T(8,128)(2,1)S(1)}, bf16[32,2048]{1,0:T(8,128)(2,1)S(1)}, u32[]{:S(2)}, u32[]{:S(2)}) collective-permute-start(bf16[32,2048]{1,0:T(8,128)(2,1)S(1)} %dynamic-slice_bitcast_fusion.13), channel_id=1, source_target_pairs={{0,16},{16,0},{1,17},{17,1},{2,18},{18,2},{3,19},{19,3},{4,20},{20... | collective-permute-start | bytes 393224 | tf_op jit(solution)/shard_map/ppermute | solution.py:85
  229.4 1.8 collective-permute-done.32
  231.3 3.2 %collective-permute-start.33 = (bf16[32,2048]{1,0:T(8,128)(2,1)S(1)}, bf16[32,2048]{1,0:T(8,128)(2,1)S(1)}, u32[]{:S(2)}, u32[]{:S(2)}) collective-permute-start(bf16[32,2048]{1,0:T(8,128)(2,1)S(1)} %dynamic-slice_bitcast_fusion.12), channel_id=1, source_target_pairs={{0,16},{16,0},{1,17},{17,1},{2,18},{18,2},{3,19},{19,3},{4,20},{20... | collective-permute-start | bytes 393224 | tf_op jit(solution)/shard_map/ppermute | solution.py:85
  234.5 3.4 %collective-permute-done.33 = bf16[32,2048]{1,0:T(8,128)(2,1)S(1)} collective-permute-done((bf16[32,2048]{1,0:T(8,128)(2,1)S(1)}, bf16[32,2048]{1,0:T(8,128)(2,1)S(1)}, u32[]{:S(2)}, u32[]{:S(2)}) %collective-permute-start.33) | collective-permute-done | bytes 131104 | tf_op jit(solution)/shard_map/ppermute | solution.py:85
  (122 shorter events, 12.1 us)
Async XLA Ops:
  0.0 90.1 %copy-start = (bf16[4096,64]{0,1:T(8,128)(2,1)S(1)}, bf16[4096,64]{0,1:T(8,128)(2,1)}, u32[]{:S(2)}) copy-start(bf16[4096,64]{0,1:T(8,128)(2,1)} %param.11) | copy-start | bytes 1572868
  0.0 3.0 %copy-start.5 = (bf16[16384]{0:T(1024)(128)(2,1)S(1)}, bf16[16384]{0:T(1024)(128)(2,1)}, u32[]{:S(2)}) copy-start(bf16[16384]{0:T(1024)(128)(2,1)} %param.9) | copy-start | bytes 98308
  14.8 9.0 %collective-permute-start = (bf16[2,32,2048]{2,1,0:T(8,128)(2,1)}, bf16[2,32,2048]{2,1,0:T(8,128)(2,1)S(1)}, u32[]{:S(2)}, u32[]{:S(2)}) collective-permute-start(bf16[2,32,2048]{2,1,0:T(8,128)(2,1)} %get-tuple-element.33), channel_id=1, source_target_pairs={{0,1},{1,2},{2,3},{3,0},{4,5},{5,6},{6,7},{7,4},{8,9},{9,10},{10,1... | collective-permute-start | bytes 786440 | tf_op jit(solution)/shard_map/ppermute | solution.py:62
  16.4 7.8 %collective-permute-start.1 = (bf16[2,32,2048]{2,1,0:T(8,128)(2,1)}, bf16[2,32,2048]{2,1,0:T(8,128)(2,1)S(1)}, u32[]{:S(2)}, u32[]{:S(2)}) collective-permute-start(bf16[2,32,2048]{2,1,0:T(8,128)(2,1)} %get-tuple-element.33), channel_id=1, source_target_pairs={{0,3},{1,0},{2,1},{3,2},{4,7},{5,4},{6,5},{7,6},{8,11},{9,8},{10,9... | collective-permute-start | bytes 786440 | tf_op jit(solution)/shard_map/ppermute | solution.py:66
  18.1 9.1 %collective-permute-start.8 = (bf16[2,32,2048]{2,1,0:T(8,128)(2,1)S(1)}, bf16[2,32,2048]{2,1,0:T(8,128)(2,1)S(1)}, u32[]{:S(2)}, u32[]{:S(2)}) collective-permute-start(bf16[2,32,2048]{2,1,0:T(8,128)(2,1)S(1)} %get-tuple-element.34), channel_id=1, source_target_pairs={{0,4},{4,8},{8,12},{12,0},{1,5},{5,9},{9,13},{13,1},{2,6},{6,10},{... | collective-permute-start | bytes 786440 | tf_op jit(solution)/shard_map/ppermute | solution.py:62
  19.6 9.2 %collective-permute-start.9 = (bf16[2,32,2048]{2,1,0:T(8,128)(2,1)S(1)}, bf16[2,32,2048]{2,1,0:T(8,128)(2,1)S(1)}, u32[]{:S(2)}, u32[]{:S(2)}) collective-permute-start(bf16[2,32,2048]{2,1,0:T(8,128)(2,1)S(1)} %get-tuple-element.34), channel_id=1, source_target_pairs={{0,12},{4,0},{8,4},{12,8},{1,13},{5,1},{9,5},{13,9},{2,14},{6,2},{... | collective-permute-start | bytes 786440 | tf_op jit(solution)/shard_map/ppermute | solution.py:66
  23.8 6.9 %collective-permute-start.2 = (bf16[2,32,1024]{2,1,0:T(8,128)(2,1)S(1)}, bf16[2,32,1024]{2,1,0:T(8,128)(2,1)S(1)}, u32[]{:S(2)}, u32[]{:S(2)}) collective-permute-start(bf16[2,32,1024]{2,1,0:T(8,128)(2,1)S(1)} %slice.177), channel_id=1, source_target_pairs={{0,1},{1,2},{2,3},{3,0},{4,5},{5,6},{6,7},{7,4},{8,9},{9,10},{10,1... | collective-permute-start | bytes 393224 | tf_op jit(solution)/shard_map/ppermute | solution.py:69
  24.2 6.5 %collective-permute-start.3 = (bf16[2,32,1024]{2,1,0:T(8,128)(2,1)S(1)}, bf16[2,32,1024]{2,1,0:T(8,128)(2,1)S(1)}, u32[]{:S(2)}, u32[]{:S(2)}) collective-permute-start(bf16[2,32,1024]{2,1,0:T(8,128)(2,1)S(1)} %slice.178), channel_id=1, source_target_pairs={{0,3},{1,0},{2,1},{3,2},{4,7},{5,4},{6,5},{7,6},{8,11},{9,8},{10,9... | collective-permute-start | bytes 393224 | tf_op jit(solution)/shard_map/ppermute | solution.py:70
  27.2 7.7 %collective-permute-start.10 = (bf16[2,32,1024]{2,1,0:T(8,128)(2,1)S(1)}, bf16[2,32,1024]{2,1,0:T(8,128)(2,1)S(1)}, u32[]{:S(2)}, u32[]{:S(2)}) collective-permute-start(bf16[2,32,1024]{2,1,0:T(8,128)(2,1)S(1)} %slice.182), channel_id=1, source_target_pairs={{0,4},{4,8},{8,12},{12,0},{1,5},{5,9},{9,13},{13,1},{2,6},{6,10},{... | collective-permute-start | bytes 393224 | tf_op jit(solution)/shard_map/ppermute | solution.py:69
  28.8 6.4 %collective-permute-start.11 = (bf16[2,32,1024]{2,1,0:T(8,128)(2,1)S(1)}, bf16[2,32,1024]{2,1,0:T(8,128)(2,1)S(1)}, u32[]{:S(2)}, u32[]{:S(2)}) collective-permute-start(bf16[2,32,1024]{2,1,0:T(8,128)(2,1)S(1)} %slice.183), channel_id=1, source_target_pairs={{0,12},{4,0},{8,4},{12,8},{1,13},{5,1},{9,5},{13,9},{2,14},{6,2},{... | collective-permute-start | bytes 393224 | tf_op jit(solution)/shard_map/ppermute | solution.py:70
  30.8 25.1 %collective-permute-start.4 = (bf16[4,2,32,2048]{3,2,1,0:T(8,128)(2,1)S(1)}, bf16[4,2,32,2048]{3,2,1,0:T(8,128)(2,1)S(1)}, u32[]{:S(2)}, u32[]{:S(2)}) collective-permute-start(bf16[4,2,32,2048]{3,2,1,0:T(8,128)(2,1)S(1)} %fusion.26), channel_id=1, source_target_pairs={{0,4},{4,8},{8,12},{12,0},{1,5},{5,9},{9,13},{13,1},{2,6},{6,10},{... | collective-permute-start | bytes 3145736 | tf_op jit(solution)/shard_map/ppermute | solution.py:62
  31.6 24.4 %collective-permute-start.5 = (bf16[4,2,32,2048]{3,2,1,0:T(8,128)(2,1)S(1)}, bf16[4,2,32,2048]{3,2,1,0:T(8,128)(2,1)S(1)}, u32[]{:S(2)}, u32[]{:S(2)}) collective-permute-start(bf16[4,2,32,2048]{3,2,1,0:T(8,128)(2,1)S(1)} %fusion.26), channel_id=1, source_target_pairs={{0,12},{4,0},{8,4},{12,8},{1,13},{5,1},{9,5},{13,9},{2,14},{6,2},{... | collective-permute-start | bytes 3145736 | tf_op jit(solution)/shard_map/ppermute | solution.py:66
  35.3 24.1 %collective-permute-start.12 = (bf16[4,2,32,2048]{3,2,1,0:T(8,128)(2,1)S(1)}, bf16[4,2,32,2048]{3,2,1,0:T(8,128)(2,1)S(1)}, u32[]{:S(2)}, u32[]{:S(2)}) collective-permute-start(bf16[4,2,32,2048]{3,2,1,0:T(8,128)(2,1)S(1)} %fusion.27), channel_id=1, source_target_pairs={{0,1},{1,2},{2,3},{3,0},{4,5},{5,6},{6,7},{7,4},{8,9},{9,10},{10,1... | collective-permute-start | bytes 3145736 | tf_op jit(solution)/shard_map/ppermute | solution.py:62
  35.3 24.1 %collective-permute-start.13 = (bf16[4,2,32,2048]{3,2,1,0:T(8,128)(2,1)S(1)}, bf16[4,2,32,2048]{3,2,1,0:T(8,128)(2,1)S(1)}, u32[]{:S(2)}, u32[]{:S(2)}) collective-permute-start(bf16[4,2,32,2048]{3,2,1,0:T(8,128)(2,1)S(1)} %fusion.27), channel_id=1, source_target_pairs={{0,3},{1,0},{2,1},{3,2},{4,7},{5,4},{6,5},{7,6},{8,11},{9,8},{10,9... | collective-permute-start | bytes 3145736 | tf_op jit(solution)/shard_map/ppermute | solution.py:66
  55.9 13.0 %collective-permute-start.6 = (bf16[4,2,32,1024]{3,2,1,0:T(8,128)(2,1)S(1)}, bf16[4,2,32,1024]{3,2,1,0:T(8,128)(2,1)S(1)}, u32[]{:S(2)}, u32[]{:S(2)}) collective-permute-start(bf16[4,2,32,1024]{3,2,1,0:T(8,128)(2,1)S(1)} %slice.179), channel_id=1, source_target_pairs={{0,4},{4,8},{8,12},{12,0},{1,5},{5,9},{9,13},{13,1},{2,6},{6,10},{... | collective-permute-start | bytes 1572872 | tf_op jit(solution)/shard_map/ppermute | solution.py:69
  56.1 12.9 %collective-permute-start.7 = (bf16[4,2,32,1024]{3,2,1,0:T(8,128)(2,1)S(1)}, bf16[4,2,32,1024]{3,2,1,0:T(8,128)(2,1)S(1)}, u32[]{:S(2)}, u32[]{:S(2)}) collective-permute-start(bf16[4,2,32,1024]{3,2,1,0:T(8,128)(2,1)S(1)} %slice.180), channel_id=1, source_target_pairs={{0,12},{4,0},{8,4},{12,8},{1,13},{5,1},{9,5},{13,9},{2,14},{6,2},{... | collective-permute-start | bytes 1572872 | tf_op jit(solution)/shard_map/ppermute | solution.py:70
  59.4 12.4 %collective-permute-start.14 = (bf16[4,2,32,1024]{3,2,1,0:T(8,128)(2,1)S(1)}, bf16[4,2,32,1024]{3,2,1,0:T(8,128)(2,1)S(1)}, u32[]{:S(2)}, u32[]{:S(2)}) collective-permute-start(bf16[4,2,32,1024]{3,2,1,0:T(8,128)(2,1)S(1)} %slice.184), channel_id=1, source_target_pairs={{0,1},{1,2},{2,3},{3,0},{4,5},{5,6},{6,7},{7,4},{8,9},{9,10},{10,1... | collective-permute-start | bytes 1572872 | tf_op jit(solution)/shard_map/ppermute | solution.py:69
  59.5 12.3 %collective-permute-start.15 = (bf16[4,2,32,1024]{3,2,1,0:T(8,128)(2,1)S(1)}, bf16[4,2,32,1024]{3,2,1,0:T(8,128)(2,1)S(1)}, u32[]{:S(2)}, u32[]{:S(2)}) collective-permute-start(bf16[4,2,32,1024]{3,2,1,0:T(8,128)(2,1)S(1)} %slice.185), channel_id=1, source_target_pairs={{0,3},{1,0},{2,1},{3,2},{4,7},{5,4},{6,5},{7,6},{8,11},{9,8},{10,9... | collective-permute-start | bytes 1572872 | tf_op jit(solution)/shard_map/ppermute | solution.py:70
  80.8 9.3 %copy-start.2 = (bf16[4,4,2,32,4096]{4,3,2,1,0:T(8,128)(2,1)S(1)}, bf16[4,4,2,32,4096]{4,3,2,1,0:T(8,128)(2,1)}, u32[]{:S(2)}) copy-start(bf16[4,4,2,32,4096]{4,3,2,1,0:T(8,128)(2,1)} %pad_maximum_fusion) | copy-start | bytes 25165828
  92.8 9.4 %copy-start.6 = (s32[8]{0:T(128)S(1)}, s32[8]{0:T(128)}, u32[]{:S(2)}) copy-start(s32[8]{0:T(128)} %param.14) | copy-start | bytes 100
  94.8 27.9 %all-to-all-start = ((bf16[128,8,576]{2,1,0:T(8,128)(2,1)}), bf16[128,8,576]{2,1,0:T(8,128)(2,1)S(1)}, u32[]{:S(2)}, u32[]{:S(2)}) async-start(bf16[128,8,576]{2,1,0:T(8,128)(2,1)} %bitcast.23), calls=%async_computation | async-start | bytes 2621440 | tf_op jit(solution)/shard_map/all_to_all | solution.py:125
  124.0 4.6 %copy-start.7 = (bf16[8,256,8,128]{3,2,1,0:T(8,128)(2,1)S(1)}, bf16[8,256,8,128]{3,2,1,0:T(8,128)(2,1)}, u32[]{:S(2)}) copy-start(bf16[8,256,8,128]{3,2,1,0:T(8,128)(2,1)} %param.13) | copy-start | bytes 12582916
  160.7 2.0 copy-start.3
  160.7 4.5 %copy-start.4 = (bf16[2,4,4,32,2048]{4,3,2,1,0:T(8,128)(2,1)}, bf16[2,4,4,32,2048]{4,3,2,1,0:T(8,128)(2,1)S(1)}, u32[]{:S(2)}) copy-start(bf16[2,4,4,32,2048]{4,3,2,1,0:T(8,128)(2,1)S(1)} %get-tuple-element.6) | copy-start | bytes 12582916
  162.7 13.9 %collective-permute-start.16 = (bf16[2,4,32,1024]{3,2,1,0:T(8,128)(2,1)S(1)}, bf16[2,4,32,1024]{3,2,1,0:T(8,128)(2,1)S(1)}, u32[]{:S(2)}, u32[]{:S(2)}) collective-permute-start(bf16[2,4,32,1024]{3,2,1,0:T(8,128)(2,1)S(1)} %get-tuple-element.18), channel_id=1, source_target_pairs={{0,3},{1,0},{2,1},{3,2},{4,7},{5,4},{6,5},{7,6},{8,11},{9,8},{10,9... | collective-permute-start | bytes 1572872 | tf_op jit(solution)/shard_map/ppermute | solution.py:88
  165.2 15.4 %collective-permute-start.18 = (bf16[2,4,32,1024]{3,2,1,0:T(8,128)(2,1)S(1)}, bf16[2,4,32,1024]{3,2,1,0:T(8,128)(2,1)S(1)}, u32[]{:S(2)}, u32[]{:S(2)}) collective-permute-start(bf16[2,4,32,1024]{3,2,1,0:T(8,128)(2,1)S(1)} %get-tuple-element.19), channel_id=1, source_target_pairs={{0,1},{1,2},{2,3},{3,0},{4,5},{5,6},{6,7},{7,4},{8,9},{9,10},{10,1... | collective-permute-start | bytes 1572872 | tf_op jit(solution)/shard_map/ppermute | solution.py:89
  165.5 16.3 %collective-permute-start.25 = (bf16[2,4,32,1024]{3,2,1,0:T(8,128)(2,1)S(1)}, bf16[2,4,32,1024]{3,2,1,0:T(8,128)(2,1)S(1)}, u32[]{:S(2)}, u32[]{:S(2)}) collective-permute-start(bf16[2,4,32,1024]{3,2,1,0:T(8,128)(2,1)S(1)} %get-tuple-element.27), channel_id=1, source_target_pairs={{0,12},{4,0},{8,4},{12,8},{1,13},{5,1},{9,5},{13,9},{2,14},{6,2},{... | collective-permute-start | bytes 1572872 | tf_op jit(solution)/shard_map/ppermute | solution.py:88
  167.7 16.2 %collective-permute-start.27 = (bf16[2,4,32,1024]{3,2,1,0:T(8,128)(2,1)S(1)}, bf16[2,4,32,1024]{3,2,1,0:T(8,128)(2,1)S(1)}, u32[]{:S(2)}, u32[]{:S(2)}) collective-permute-start(bf16[2,4,32,1024]{3,2,1,0:T(8,128)(2,1)S(1)} %get-tuple-element.28), channel_id=1, source_target_pairs={{0,4},{4,8},{8,12},{12,0},{1,5},{5,9},{9,13},{13,1},{2,6},{6,10},{... | collective-permute-start | bytes 1572872 | tf_op jit(solution)/shard_map/ppermute | solution.py:89
  177.8 24.5 %collective-permute-start.17 = (bf16[2,4,32,2048]{3,2,1,0:T(8,128)(2,1)}, bf16[2,4,32,2048]{3,2,1,0:T(8,128)(2,1)S(1)}, u32[]{:S(2)}, u32[]{:S(2)}) collective-permute-start(bf16[2,4,32,2048]{3,2,1,0:T(8,128)(2,1)} %pad_maximum_fusion.2), channel_id=1, source_target_pairs={{0,3},{1,0},{2,1},{3,2},{4,7},{5,4},{6,5},{7,6},{8,11},{9,8},{10,9... | collective-permute-start | bytes 3145736 | tf_op jit(solution)/shard_map/ppermute | solution.py:94
  181.8 24.5 %collective-permute-start.19 = (bf16[2,4,32,2048]{3,2,1,0:T(8,128)(2,1)}, bf16[2,4,32,2048]{3,2,1,0:T(8,128)(2,1)S(1)}, u32[]{:S(2)}, u32[]{:S(2)}) collective-permute-start(bf16[2,4,32,2048]{3,2,1,0:T(8,128)(2,1)} %pad_maximum_fusion.3), channel_id=1, source_target_pairs={{0,1},{1,2},{2,3},{3,0},{4,5},{5,6},{6,7},{7,4},{8,9},{9,10},{10,1... | collective-permute-start | bytes 3145736 | tf_op jit(solution)/shard_map/ppermute | solution.py:95
  183.0 23.4 %collective-permute-start.26 = (bf16[2,4,32,2048]{3,2,1,0:T(8,128)(2,1)}, bf16[2,4,32,2048]{3,2,1,0:T(8,128)(2,1)}, u32[]{:S(2)}, u32[]{:S(2)}) collective-permute-start(bf16[2,4,32,2048]{3,2,1,0:T(8,128)(2,1)} %pad_maximum_fusion.4), channel_id=1, source_target_pairs={{0,12},{4,0},{8,4},{12,8},{1,13},{5,1},{9,5},{13,9},{2,14},{6,2},{... | collective-permute-start | bytes 3145736 | tf_op jit(solution)/shard_map/ppermute | solution.py:94
  185.0 24.1 %collective-permute-start.28 = (bf16[2,4,32,2048]{3,2,1,0:T(8,128)(2,1)}, bf16[2,4,32,2048]{3,2,1,0:T(8,128)(2,1)}, u32[]{:S(2)}, u32[]{:S(2)}) collective-permute-start(bf16[2,4,32,2048]{3,2,1,0:T(8,128)(2,1)} %pad_maximum_fusion.5), channel_id=1, source_target_pairs={{0,4},{4,8},{8,12},{12,0},{1,5},{5,9},{9,13},{13,1},{2,6},{6,10},{... | collective-permute-start | bytes 3145736 | tf_op jit(solution)/shard_map/ppermute | solution.py:95
  211.7 6.4 %collective-permute-start.20 = (bf16[2,32,1024]{2,1,0:T(8,128)(2,1)S(1)}, bf16[2,32,1024]{2,1,0:T(8,128)(2,1)S(1)}, u32[]{:S(2)}, u32[]{:S(2)}) collective-permute-start(bf16[2,32,1024]{2,1,0:T(8,128)(2,1)S(1)} %get-tuple-element.37), channel_id=1, source_target_pairs={{0,12},{4,0},{8,4},{12,8},{1,13},{5,1},{9,5},{13,9},{2,14},{6,2},{... | collective-permute-start | bytes 393224 | tf_op jit(solution)/shard_map/ppermute | solution.py:88
  212.4 6.5 %collective-permute-start.22 = (bf16[2,32,1024]{2,1,0:T(8,128)(2,1)S(1)}, bf16[2,32,1024]{2,1,0:T(8,128)(2,1)S(1)}, u32[]{:S(2)}, u32[]{:S(2)}) collective-permute-start(bf16[2,32,1024]{2,1,0:T(8,128)(2,1)S(1)} %get-tuple-element.38), channel_id=1, source_target_pairs={{0,4},{4,8},{8,12},{12,0},{1,5},{5,9},{9,13},{13,1},{2,6},{6,10},{... | collective-permute-start | bytes 393224 | tf_op jit(solution)/shard_map/ppermute | solution.py:89
  213.9 6.5 %collective-permute-start.29 = (bf16[2,32,1024]{2,1,0:T(8,128)(2,1)S(1)}, bf16[2,32,1024]{2,1,0:T(8,128)(2,1)S(1)}, u32[]{:S(2)}, u32[]{:S(2)}) collective-permute-start(bf16[2,32,1024]{2,1,0:T(8,128)(2,1)S(1)} %get-tuple-element.43), channel_id=1, source_target_pairs={{0,3},{1,0},{2,1},{3,2},{4,7},{5,4},{6,5},{7,6},{8,11},{9,8},{10,9... | collective-permute-start | bytes 393224 | tf_op jit(solution)/shard_map/ppermute | solution.py:88
  216.6 6.9 %collective-permute-start.31 = (bf16[2,32,1024]{2,1,0:T(8,128)(2,1)S(1)}, bf16[2,32,1024]{2,1,0:T(8,128)(2,1)S(1)}, u32[]{:S(2)}, u32[]{:S(2)}) collective-permute-start(bf16[2,32,1024]{2,1,0:T(8,128)(2,1)S(1)} %get-tuple-element.44), channel_id=1, source_target_pairs={{0,1},{1,2},{2,3},{3,0},{4,5},{5,6},{6,7},{7,4},{8,9},{9,10},{10,1... | collective-permute-start | bytes 393224 | tf_op jit(solution)/shard_map/ppermute | solution.py:89
  218.1 20.5 %copy-start.1 = (bf16[4096,64]{0,1:T(8,128)(2,1)S(1)}, bf16[4096,64]{0,1:T(8,128)(2,1)}, u32[]{:S(2)}) copy-start(bf16[4096,64]{0,1:T(8,128)(2,1)} %param.11) | copy-start | bytes 1572868
  218.2 6.4 %collective-permute-start.21 = (bf16[2,32,2048]{2,1,0:T(8,128)(2,1)S(1)}, bf16[2,32,2048]{2,1,0:T(8,128)(2,1)S(1)}, u32[]{:S(2)}, u32[]{:S(2)}) collective-permute-start(bf16[2,32,2048]{2,1,0:T(8,128)(2,1)S(1)} %pad_maximum_fusion.7), channel_id=1, source_target_pairs={{0,12},{4,0},{8,4},{12,8},{1,13},{5,1},{9,5},{13,9},{2,14},{6,2},{... | collective-permute-start | bytes 786440 | tf_op jit(solution)/shard_map/ppermute | solution.py:94
  219.0 7.7 %collective-permute-start.23 = (bf16[2,32,2048]{2,1,0:T(8,128)(2,1)S(1)}, bf16[2,32,2048]{2,1,0:T(8,128)(2,1)S(1)}, u32[]{:S(2)}, u32[]{:S(2)}) collective-permute-start(bf16[2,32,2048]{2,1,0:T(8,128)(2,1)S(1)} %pad_maximum_fusion.8), channel_id=1, source_target_pairs={{0,4},{4,8},{8,12},{12,0},{1,5},{5,9},{9,13},{13,1},{2,6},{6,10},{... | collective-permute-start | bytes 786440 | tf_op jit(solution)/shard_map/ppermute | solution.py:95
  220.5 8.9 %collective-permute-start.30 = (bf16[2,32,2048]{2,1,0:T(8,128)(2,1)S(1)}, bf16[2,32,2048]{2,1,0:T(8,128)(2,1)S(1)}, u32[]{:S(2)}, u32[]{:S(2)}) collective-permute-start(bf16[2,32,2048]{2,1,0:T(8,128)(2,1)S(1)} %pad_maximum_fusion.9), channel_id=1, source_target_pairs={{0,3},{1,0},{2,1},{3,2},{4,7},{5,4},{6,5},{7,6},{8,11},{9,8},{10,9... | collective-permute-start | bytes 786440 | tf_op jit(solution)/shard_map/ppermute | solution.py:94
  223.6 7.7 %collective-permute-start.32 = (bf16[2,32,2048]{2,1,0:T(8,128)(2,1)S(1)}, bf16[2,32,2048]{2,1,0:T(8,128)(2,1)S(1)}, u32[]{:S(2)}, u32[]{:S(2)}) collective-permute-start(bf16[2,32,2048]{2,1,0:T(8,128)(2,1)S(1)} %pad_maximum_fusion.10), channel_id=1, source_target_pairs={{0,1},{1,2},{2,3},{3,0},{4,5},{5,6},{6,7},{7,4},{8,9},{9,10},{10,1... | collective-permute-start | bytes 786440 | tf_op jit(solution)/shard_map/ppermute | solution.py:95
  226.7 7.8 %collective-permute-start.24 = (bf16[32,2048]{1,0:T(8,128)(2,1)S(1)}, bf16[32,2048]{1,0:T(8,128)(2,1)S(1)}, u32[]{:S(2)}, u32[]{:S(2)}) collective-permute-start(bf16[32,2048]{1,0:T(8,128)(2,1)S(1)} %dynamic-slice_bitcast_fusion.13), channel_id=1, source_target_pairs={{0,16},{16,0},{1,17},{17,1},{2,18},{18,2},{3,19},{19,3},{4,20},{20... | collective-permute-start | bytes 393224 | tf_op jit(solution)/shard_map/ppermute | solution.py:85
  231.3 6.6 %collective-permute-start.33 = (bf16[32,2048]{1,0:T(8,128)(2,1)S(1)}, bf16[32,2048]{1,0:T(8,128)(2,1)S(1)}, u32[]{:S(2)}, u32[]{:S(2)}) collective-permute-start(bf16[32,2048]{1,0:T(8,128)(2,1)S(1)} %dynamic-slice_bitcast_fusion.12), channel_id=1, source_target_pairs={{0,16},{16,0},{1,17},{17,1},{2,18},{18,2},{3,19},{19,3},{4,20},{20... | collective-permute-start | bytes 393224 | tf_op jit(solution)/shard_map/ppermute | solution.py:85
where the time goes:
time: 239 us
  waiting for transfers between devices  79 us (33%)
  starting transfers between devices  59.6 us (25%)
  blocking collectives  34 us (14%)
  matrix products  23.9 us (10%)
  other arithmetic  22.9 us (10%)
  local copies, waits for them, and re-layouts  18.6 us (8%)
    all_to_all x1, blocking collectives, shards(): lax.all_to_all(sent, ALL, split_axis=0, concat_axis=0, tiled=True)  23 us
    all_to_all x1, waiting for transfers between devices, shards(): lax.all_to_all(projected.astype(jnp.bfloat16), ALL, split_axis=0, concat_...  20.3 us
    ppermute x4, waiting for transfers between devices, ring_reduce_scatter(): got_right = lax.ppermute(to_left, axis, bwd)  17.1 us
    ppermute x4, waiting for transfers between devices, ring_all_gather(): from_left = lax.ppermute(blk, axis, fwd)  12.3 us
    ppermute x4, starting transfers between devices, ring_all_gather(): second = lax.ppermute(from_right[..., half:], axis, bwd)  11.6 us
    all_gather x1, blocking collectives, shards(): pair = lax.all_gather(own_cols, 'zh', axis=0, tiled=False)  11 us
    ppermute x4, waiting for transfers between devices, ring_reduce_scatter(): got_left = lax.ppermute(to_right, axis, fwd)  10.6 us
    ppermute x4, waiting for transfers between devices, ring_reduce_scatter(): from_right = lax.ppermute(opposite[..., :half], axis, bwd)  10.5 us
  transfers between devices with their start and end apart: 35, of which 16 were waited for; matrix products, arithmetic and copies ran while one was open for 8% of the time, Pallas kernels for 0%

commit v1 on v0

--- a/solution.py
+++ b/solution.py
@@ -72,19 +72,40 @@
     return lax.dynamic_update_index_in_dim(out, opposite, (idx + 2) % n, dim)
 
 
-def ring_reduce_scatter(arr, axis, dim):
-    n = arr.shape[dim]
+def ring_all_gather_apply(blk, axis, n, dim, fn):
+    idx = lax.axis_index(axis)
+    fwd = [(i, (i + 1) % n) for i in range(n)]
+    bwd = [(i, (i - 1) % n) for i in range(n)]
+    from_left = lax.ppermute(blk, axis, fwd)
+    from_right = lax.ppermute(blk, axis, bwd)
+    own = fn(blk)
+    out = jnp.zeros(own.shape[:dim] + (n,) + own.shape[dim:], own.dtype)
+    out = lax.dynamic_update_index_in_dim(out, own, idx, dim)
+    half = blk.shape[-1] // 2
+    first = lax.ppermute(from_left[..., :half], axis, fwd)
+    second = lax.ppermute(from_right[..., half:], axis, bwd)
+    out = lax.dynamic_update_index_in_dim(out, fn(from_left), (idx - 1) % n, dim)
+    out = lax.dynamic_update_index_in_dim(out, fn(from_right), (idx + 1) % n, dim)
+    opposite = jnp.concatenate([first, second], axis=-1)
+    return lax.dynamic_update_index_in_dim(out, fn(opposite), (idx + 2) % n, dim)
+
+
+def blocks_of(arr, dim):
+    return lambda k: lax.dynamic_index_in_dim(arr, k, dim, keepdims=False)
+
+
+def ring_reduce_scatter(make, axis, n):
     idx = lax.axis_index(axis)
 
     def take(k):
-        return lax.dynamic_index_in_dim(arr, k % n, dim, keepdims=False)
+        return make(k % n)
 
     fwd = [(i, (i + 1) % n) for i in range(n)]
     bwd = [(i, (i - 1) % n) for i in range(n)]
     if n == 2:
         return take(idx) + lax.ppermute(take(idx + 1), axis, fwd)
-    half = arr.shape[-1] // 2
     opposite = take(idx + 2)
+    half = opposite.shape[-1] // 2
     from_right = lax.ppermute(opposite[..., :half], axis, bwd)
     from_left = lax.ppermute(opposite[..., half:], axis, fwd)
     to_left = take(idx - 1)
@@ -110,16 +131,20 @@
     second = pair[..., width_part // 2 :]
     first = ring_all_gather(first, "y", 4, 0)
     second = ring_all_gather(second, "x", 4, 0)
-    first = ring_all_gather(first, "x", 4, 0)
-    second = ring_all_gather(second, "y", 4, 1)
-    gathered = jnp.concatenate([first, second], axis=-1).reshape(-1, width_part)
-    projected = jnp.concatenate(
-        [
-            jnp.dot(gathered, w_query, preferred_element_type=jnp.float32),
-            jnp.dot(gathered, w_keyval, preferred_element_type=jnp.float32),
-        ],
-        axis=1,
-    )
+    half = width_part // 2
+
+    def project(lo, hi):
+        return lambda piece: jnp.concatenate(
+            [
+                jnp.dot(piece, w_query[lo:hi], preferred_element_type=jnp.float32),
+                jnp.dot(piece, w_keyval[lo:hi], preferred_element_type=jnp.float32),
+            ],
+            axis=-1,
+        )
+
+    projected = ring_all_gather_apply(first, "x", 4, 0, project(0, half))
+    projected = projected + ring_all_gather_apply(second, "y", 4, 1, project(half, width_part))
+    projected = projected.reshape(-1, query_cols + pair_cols)
     projected = projected.reshape(4, 4, 2, -1, projected.shape[1]).transpose(2, 0, 1, 3, 4)
     projected = projected.reshape(-1, projected.shape[-1])
     arrived = lax.all_to_all(projected.astype(jnp.bfloat16), ALL, split_axis=0, concat_axis=0, tiled=True)
@@ -132,17 +157,22 @@
     heads_first = attended.reshape(rows_dev, peers, query_cols).transpose(1, 0, 2)
     sent = jnp.broadcast_to(heads_first[None], (4,) + heads_first.shape).reshape(-1, query_cols)
     full_rows = lax.all_to_all(sent, ALL, split_axis=0, concat_axis=0, tiled=True)
-    partial_out = jnp.dot(full_rows, w_out, preferred_element_type=jnp.float32)
-    part = partial_out.astype(jnp.bfloat16)
-    rows, cols = part.shape
-    part = part.reshape(2, 4, 4, rows // peers, cols)
-    first, second = part[..., : cols // 2], part[..., cols // 2 :]
-    first = ring_reduce_scatter(first, "y", 2)
-    second = ring_reduce_scatter(second, "x", 1)
-    first = ring_reduce_scatter(first, "x", 1)
-    second = ring_reduce_scatter(second, "y", 1)
-    first = ring_reduce_scatter(first, "zh", 0)
-    second = ring_reduce_scatter(second, "zh", 0)
+    cols = w_out.shape[1]
+    by_row = full_rows.reshape(2, 4, 4, rows_dev * 4, query_cols)
+
+    def partial_out(dim, lo, hi):
+        return lambda k: jnp.dot(
+            lax.dynamic_index_in_dim(by_row, k, dim, keepdims=False),
+            w_out[:, lo:hi],
+            preferred_element_type=jnp.float32,
+        ).astype(jnp.bfloat16)
+
+    first = ring_reduce_scatter(partial_out(2, 0, cols // 2), "y", 4)
+    second = ring_reduce_scatter(partial_out(1, cols // 2, cols), "x", 4)
+    first = ring_reduce_scatter(blocks_of(first, 1), "x", 4)
+    second = ring_reduce_scatter(blocks_of(second, 1), "y", 4)
+    first = ring_reduce_scatter(blocks_of(first, 0), "zh", 2)
+    second = ring_reduce_scatter(blocks_of(second, 0), "zh", 2)
     return jnp.concatenate([first, second], axis=-1)
 
 

time: 239 us -> 218 us (0.912)
  waiting for transfers between devices: 79 us -> 108 us
  blocking collectives: 34 us -> 11 us
  local copies, waits for them, and re-layouts: 18.6 us -> 3.6 us
  other arithmetic: 22.9 us -> 8.57 us
    all_to_all x1 -> x0, blocking collectives: 23 us -> none  [shards(): lax.all_to_all(sent, ALL, split_axis=0, concat_axis=0, tiled=True)]
    ppermute x0 -> x8, waiting for transfers between devices: none -> 20.7 us  [the longest x2 15.2 us: ring_all_gather_apply(): from_right = lax.ppermute(blk, axis, bwd)]
    all_to_all x0 -> x1, waiting for transfers between devices: none -> 17.6 us  [shards(): lax.all_to_all(sent, ALL, split_axis=0, concat_axis=0, tiled=True)]
    ppermute x4 -> x2, waiting for transfers between devices: 12.3 us -> 1.9 us  [ring_all_gather(): from_left = lax.ppermute(blk, axis, fwd)]
    ppermute x0 -> x8, starting transfers between devices: none -> 10.4 us  [the longest x2 3.44 us: ring_all_gather_apply(): second = lax.ppermute(from_right[..., half:], axis, bwd)]
    concatenate x2 -> x0, other arithmetic: 7.97 us -> none  [the longest x1 7.88 us: shards(): gathered = jnp.concatenate([first, second], axis=-1).reshape(-1, width_part)]
    ppermute x4 -> x2, starting transfers between devices: 11.6 us -> 4.75 us  [ring_all_gather(): second = lax.ppermute(from_right[..., half:], axis, bwd)]
    ppermute x4 -> x2, starting transfers between devices: 9.07 us -> 3.41 us  [ring_all_gather(): from_right = lax.ppermute(blk, axis, bwd)]
  transfers between devices with their start and end apart: 35 -> 36, of which waited for: 16 -> 16; matrix products, arithmetic and copies ran while one was open for 8% -> 6% of each run, Pallas kernels for 0% -> 0%
where the time goes in v1:
time: 218 us; the launch traced here: 217 us
  waiting for transfers between devices  108 us (50%)
  starting transfers between devices  61.9 us (28%)
  matrix products  23 us (11%)
  blocking collectives  11 us (5%)
  other arithmetic  8.57 us (4%)
  local copies, waits for them, and re-layouts  3.6 us (2%)
    all_to_all x1, waiting for transfers between devices, shards(): lax.all_to_all(projected.astype(jnp.bfloat16), ALL, split_axis=0, concat_...  20.6 us
    all_to_all x1, waiting for transfers between devices, shards(): lax.all_to_all(sent, ALL, split_axis=0, concat_axis=0, tiled=True)  17.6 us
    ppermute x4, waiting for transfers between devices, ring_reduce_scatter(): got_right = lax.ppermute(to_left, axis, bwd)  16.8 us
    ppermute x2, waiting for transfers between devices, ring_all_gather_apply(): from_right = lax.ppermute(blk, axis, bwd)  15.2 us
    ppermute x4, starting transfers between devices, ring_reduce_scatter(): got_right = lax.ppermute(to_left, axis, bwd)  11.6 us
    all_gather x1, blocking collectives, shards(): pair = lax.all_gather(own_cols, 'zh', axis=0, tiled=False)  11 us
    ppermute x4, starting transfers between devices, ring_reduce_scatter(): from_right = lax.ppermute(opposite[..., :half], axis, bwd)  9.86 us
    ppermute x4, waiting for transfers between devices, ring_reduce_scatter(): from_right = lax.ppermute(opposite[..., :half], axis, bwd)  9.35 us
  transfers between devices with their start and end apart: 36, of which 16 were waited for; matrix products, arithmetic and copies ran while one was open for 6% of the time, Pallas kernels for 0%

profile of v1, /device:TPU:0, one launch (start us, length us, event | category | flops | bytes accessed | tf_op | source)
XLA Modules:
  0.0 217.3 jit_solution(15945161871442385323)
XLA Ops:
  0.0 1.5 multiply_reduce_fusion
  1.5 1.4 convert_element_type.86
  3.1 11.0 %all-gather = bf16[64,4096]{1,0:T(8,128)(2,1)S(1)} all-gather(bf16[32,4096]{1,0:T(8,128)(2,1)S(1)} %fusion.58), channel_id=2, replica_groups=mesh['gx'=4,'zh'=2,'x'=4,'y'=4] {'zh'}, dimensions={0}, use_global_device_ids=true | all-gather | bytes 786432 | tf_op jit(solution)/shard_map/all_gather | solution.py:129
  14.1 1.6 collective-permute-start.8
  15.7 1.7 collective-permute-start.9
  17.4 1.6 collective-permute-start
  19.0 1.7 collective-permute-start.1
  21.0 1.9 collective-permute-done.8
  23.2 3.0 %collective-permute-start.11 = (bf16[2,32,1024]{2,1,0:T(8,128)(2,1)S(1)}, bf16[2,32,1024]{2,1,0:T(8,128)(2,1)S(1)}, u32[]{:S(2)}, u32[]{:S(2)}) collective-permute-start(bf16[2,32,1024]{2,1,0:T(8,128)(2,1)S(1)} %slice.217), channel_id=1, source_target_pairs={{0,12},{4,0},{8,4},{12,8},{1,13},{5,1},{9,5},{13,9},{2,14},{6,2},{... | collective-permute-start | bytes 393224 | tf_op jit(solution)/shard_map/ppermute | solution.py:70
  26.3 1.6 collective-permute-start.2
  27.9 1.7 collective-permute-start.3
  29.8 2.7 %collective-permute-done.2 = bf16[2,32,1024]{2,1,0:T(8,128)(2,1)S(1)} collective-permute-done((bf16[2,32,1024]{2,1,0:T(8,128)(2,1)S(1)}, bf16[2,32,1024]{2,1,0:T(8,128)(2,1)S(1)}, u32[]{:S(2)}, u32[]{:S(2)}) %collective-permute-start.2) | collective-permute-done | bytes 131104 | tf_op jit(solution)/shard_map/ppermute | solution.py:69
  33.0 0.5 collective-permute-start.5
  33.5 1.6 collective-permute-start.4
  35.1 2.9 %collective-permute-start.13 = (bf16[4,2,32,2048]{3,2,1,0:T(8,128)(2,1)S(1)}, bf16[4,2,32,2048]{3,2,1,0:T(8,128)(2,1)S(1)}, u32[]{:S(2)}, u32[]{:S(2)}) collective-permute-start(bf16[4,2,32,2048]{3,2,1,0:T(8,128)(2,1)S(1)} %fusion.62), channel_id=1, source_target_pairs={{0,3},{1,0},{2,1},{3,2},{4,7},{5,4},{6,5},{7,6},{8,11},{9,8},{10,9... | collective-permute-start | bytes 3145736 | tf_op jit(solution)/shard_map/ppermute | solution.py:80
  38.1 0.7 fusion.26
  40.0 0.7 fusion.18
  41.1 15.2 %collective-permute-done.5 = bf16[4,2,32,2048]{3,2,1,0:T(8,128)(2,1)S(1)} collective-permute-done((bf16[4,2,32,2048]{3,2,1,0:T(8,128)(2,1)S(1)}, bf16[4,2,32,2048]{3,2,1,0:T(8,128)(2,1)S(1)}, u32[]{:S(2)}, u32[]{:S(2)}) %collective-permute-start.5) | collective-permute-done | bytes 1048608 | tf_op jit(solution)/shard_map/ppermute | solution.py:80
  56.3 0.5 collective-permute-start.7
  56.9 1.7 collective-permute-start.6
  58.6 2.9 %collective-permute-start.15 = (bf16[4,2,32,1024]{3,2,1,0:T(8,128)(2,1)S(1)}, bf16[4,2,32,1024]{3,2,1,0:T(8,128)(2,1)S(1)}, u32[]{:S(2)}, u32[]{:S(2)}) collective-permute-start(bf16[4,2,32,1024]{3,2,1,0:T(8,128)(2,1)S(1)} %slice.219), channel_id=1, source_target_pairs={{0,3},{1,0},{2,1},{3,2},{4,7},{5,4},{6,5},{7,6},{8,11},{9,8},{10,9... | collective-permute-start | bytes 1572872 | tf_op jit(solution)/shard_map/ppermute | solution.py:86
  62.3 0.7 fusion.22
  63.4 0.7 fusion.24
  64.5 0.7 fusion.14
  65.3 0.7 fusion.16
  66.7 0.8 collective-permute-done.6
  67.5 4.7 %collective-permute-done.14 = bf16[4,2,32,1024]{3,2,1,0:T(8,128)(2,1)S(1)} collective-permute-done((bf16[4,2,32,1024]{3,2,1,0:T(8,128)(2,1)S(1)}, bf16[4,2,32,1024]{3,2,1,0:T(8,128)(2,1)S(1)}, u32[]{:S(2)}, u32[]{:S(2)}) %collective-permute-start.14) | collective-permute-done | bytes 524320 | tf_op jit(solution)/shard_map/ppermute | solution.py:85
  72.8 0.7 fusion.20
  73.9 0.7 fusion.12
  74.8 1.6 add_convert_fusion
  76.4 6.6 %all-to-all-start = ((bf16[128,8,576]{2,1,0:T(8,128)(2,1)}), bf16[128,8,576]{2,1,0:T(8,128)(2,1)S(1)}, u32[]{:S(2)}, u32[]{:S(2)}) async-start(bf16[128,8,576]{2,1,0:T(8,128)(2,1)} %bitcast.30), calls=%async_computation | async-start | bytes 2621440 | tf_op jit(solution)/shard_map/all_to_all | solution.py:150
  83.2 20.6 %all-to-all-done = bf16[128,8,576]{2,1,0:T(8,128)(2,1)S(1)} async-done(((bf16[128,8,576]{2,1,0:T(8,128)(2,1)}), bf16[128,8,576]{2,1,0:T(8,128)(2,1)S(1)}, u32[]{:S(2)}, u32[]{:S(2)}) %all-to-all-start) | async-done | bytes 1179680 | tf_op jit(solution)/shard_map/all_to_all | solution.py:150
  105.4 3.7 %fusion.130 = (f32[8,8,16]{2,1,0:T(8,128)S(1)}, f32[8,8,16,256]{3,2,1,0:T(8,128)S(1)}) fusion(bf16[8,256,8,128]{3,2,1,0:T(8,128)(2,1)} %param.12, bf16[8,8,16,64]{3,2,1,0:T(8,128)(2,1)S(1)} %bitcast.223, bf16[8,8,16,64]{3,2,1,0:T(8,128)(2,1)S(1)} %bitcast.221, pred[8,256]{1,0:T(8,128)(4,1)S(1)} %iota_compare_fusion), kind=kOutput, calls=%fused_computation.211 | convolution fusion | flops 68418560 | bytes 5511168 | tf_op jit(solution)/shard_map/rgqd,rtgd->rgqt/dot_general | solution.py:39
  109.5 1.0 fusion.53
  110.9 1.1 broadcast_in_dim.103
  112.0 5.6 %all-to-all-start.1 = ((bf16[128,8,512]{2,1,0:T(8,128)(2,1)}), bf16[128,8,512]{2,1,0:T(8,128)(2,1)S(1)}, u32[]{:S(2)}, u32[]{:S(2)}) async-start(bf16[128,8,512]{2,1,0:T(8,128)(2,1)} %bitcast.42), calls=%async_computation.1 | async-start | bytes 2097152 | tf_op jit(solution)/shard_map/all_to_all | solution.py:159
  117.6 17.6 %all-to-all-done.1 = bf16[128,8,512]{2,1,0:T(8,128)(2,1)S(1)} async-done(((bf16[128,8,512]{2,1,0:T(8,128)(2,1)}), bf16[128,8,512]{2,1,0:T(8,128)(2,1)S(1)}, u32[]{:S(2)}, u32[]{:S(2)}) %all-to-all-start.1) | async-done | bytes 1048608 | tf_op jit(solution)/shard_map/all_to_all | solution.py:159
  135.2 2.5 %convolution_convert_fusion = bf16[2,4,32,2048]{3,2,1,0:T(8,128)(2,1)S(1)} fusion(bf16[512,4096]{1,0:T(8,128)(2,1)} %param.15, bf16[2,4,4,32,512]{4,3,2,1,0:T(8,128)(2,1)S(1)} %bitcast.211, s32[]{:T(128)S(6)} %select_n.173), kind=kOutput, calls=%fused_computation.5 | convolution fusion | flops 537395200 | bytes 3407876 | tf_op jit(solution)/shard_map/dot_general | solution.py:164
  137.7 2.3 %convolution_convert_fusion.1 = bf16[2,4,32,2048]{3,2,1,0:T(8,128)(2,1)S(1)} fusion(bf16[512,4096]{1,0:T(8,128)(2,1)} %param.15, bf16[2,4,4,32,512]{4,3,2,1,0:T(8,128)(2,1)S(1)} %bitcast.212, s32[]{:T(128)S(6)} %select_n.175), kind=kOutput, calls=%fused_computation.6 | convolution fusion | flops 537395200 | bytes 3407876 | tf_op jit(solution)/shard_map/dot_general | solution.py:164
  140.0 0.7 convolution_convert_fusion.2
  140.7 0.7 convolution_convert_fusion.4
  141.4 0.7 convolution_convert_fusion.5
  142.3 2.6 %collective-permute-start.25 = (bf16[2,4,32,1024]{3,2,1,0:T(8,128)(2,1)S(1)}, bf16[2,4,32,1024]{3,2,1,0:T(8,128)(2,1)S(1)}, u32[]{:S(2)}, u32[]{:S(2)}) collective-permute-start(bf16[2,4,32,1024]{3,2,1,0:T(8,128)(2,1)S(1)} %get-tuple-element.19), channel_id=1, source_target_pairs={{0,12},{4,0},{8,4},{12,8},{1,13},{5,1},{9,5},{13,9},{2,14},{6,2},{... | collective-permute-start | bytes 1572872 | tf_op jit(solution)/shard_map/ppermute | solution.py:109
  145.0 2.0 collective-permute-start.16
  147.1 0.7 convolution_convert_fusion.6
  147.8 0.7 convolution_convert_fusion.3
  148.5 9.3 %collective-permute-done.16 = bf16[2,4,32,1024]{3,2,1,0:T(8,128)(2,1)S(1)} collective-permute-done((bf16[2,4,32,1024]{3,2,1,0:T(8,128)(2,1)S(1)}, bf16[2,4,32,1024]{3,2,1,0:T(8,128)(2,1)S(1)}, u32[]{:S(2)}, u32[]{:S(2)}) %collective-permute-start.16) | collective-permute-done | bytes 524320 | tf_op jit(solution)/shard_map/ppermute | solution.py:109
  158.1 2.9 %collective-permute-start.17 = (bf16[2,4,32,2048]{3,2,1,0:T(8,128)(2,1)S(1)}, bf16[2,4,32,2048]{3,2,1,0:T(8,128)(2,1)S(1)}, u32[]{:S(2)}, u32[]{:S(2)}) collective-permute-start(bf16[2,4,32,2048]{3,2,1,0:T(8,128)(2,1)S(1)} %pad_maximum_fusion), channel_id=1, source_target_pairs={{0,3},{1,0},{2,1},{3,2},{4,7},{5,4},{6,5},{7,6},{8,11},{9,8},{10,9... | collective-permute-start | bytes 3145736 | tf_op jit(solution)/shard_map/ppermute | solution.py:115
  161.4 2.1 collective-permute-start.26
  163.8 0.7 convolution_convert_fusion.7
  164.5 16.8 %collective-permute-done.17 = bf16[2,4,32,2048]{3,2,1,0:T(8,128)(2,1)S(1)} collective-permute-done((bf16[2,4,32,2048]{3,2,1,0:T(8,128)(2,1)S(1)}, bf16[2,4,32,2048]{3,2,1,0:T(8,128)(2,1)S(1)}, u32[]{:S(2)}, u32[]{:S(2)}) %collective-permute-start.17) | collective-permute-done | bytes 1048608 | tf_op jit(solution)/shard_map/ppermute | solution.py:115
  181.3 3.7 %collective-permute-done.19 = bf16[2,4,32,2048]{3,2,1,0:T(8,128)(2,1)S(1)} collective-permute-done((bf16[2,4,32,2048]{3,2,1,0:T(8,128)(2,1)S(1)}, bf16[2,4,32,2048]{3,2,1,0:T(8,128)(2,1)S(1)}, u32[]{:S(2)}, u32[]{:S(2)}) %collective-permute-start.19) | collective-permute-done | bytes 1048608 | tf_op jit(solution)/shard_map/ppermute | solution.py:116
  185.2 1.5 collective-permute-start.20
  186.7 0.6 collective-permute-start.22
  187.6 3.7 %collective-permute-start.29 = (bf16[2,32,1024]{2,1,0:T(8,128)(2,1)S(1)}, bf16[2,32,1024]{2,1,0:T(8,128)(2,1)S(1)}, u32[]{:S(2)}, u32[]{:S(2)}) collective-permute-start(bf16[2,32,1024]{2,1,0:T(8,128)(2,1)S(1)} %get-tuple-element.35), channel_id=1, source_target_pairs={{0,3},{1,0},{2,1},{3,2},{4,7},{5,4},{6,5},{7,6},{8,11},{9,8},{10,9... | collective-permute-start | bytes 393224 | tf_op jit(solution)/shard_map/ppermute | solution.py:109
  191.3 2.4 %collective-permute-done.22 = bf16[2,32,1024]{2,1,0:T(8,128)(2,1)S(1)} collective-permute-done((bf16[2,32,1024]{2,1,0:T(8,128)(2,1)S(1)}, bf16[2,32,1024]{2,1,0:T(8,128)(2,1)S(1)}, u32[]{:S(2)}, u32[]{:S(2)}) %collective-permute-start.22) | collective-permute-done | bytes 131104 | tf_op jit(solution)/shard_map/ppermute | solution.py:110
  193.9 3.3 %collective-permute-start.21 = (bf16[2,32,2048]{2,1,0:T(8,128)(2,1)S(1)}, bf16[2,32,2048]{2,1,0:T(8,128)(2,1)S(1)}, u32[]{:S(2)}, u32[]{:S(2)}) collective-permute-start(bf16[2,32,2048]{2,1,0:T(8,128)(2,1)S(1)} %pad_maximum_fusion.5), channel_id=1, source_target_pairs={{0,12},{4,0},{8,4},{12,8},{1,13},{5,1},{9,5},{13,9},{2,14},{6,2},{... | collective-permute-start | bytes 786440 | tf_op jit(solution)/shard_map/ppermute | solution.py:115
  197.2 1.7 collective-permute-done.31
  199.1 3.3 %collective-permute-start.30 = (bf16[2,32,2048]{2,1,0:T(8,128)(2,1)S(1)}, bf16[2,32,2048]{2,1,0:T(8,128)(2,1)S(1)}, u32[]{:S(2)}, u32[]{:S(2)}) collective-permute-start(bf16[2,32,2048]{2,1,0:T(8,128)(2,1)S(1)} %pad_maximum_fusion.7), channel_id=1, source_target_pairs={{0,3},{1,0},{2,1},{3,2},{4,7},{5,4},{6,5},{7,6},{8,11},{9,8},{10,9... | collective-permute-start | bytes 786440 | tf_op jit(solution)/shard_map/ppermute | solution.py:115
  202.4 4.2 %collective-permute-done.32 = bf16[2,32,2048]{2,1,0:T(8,128)(2,1)S(1)} collective-permute-done((bf16[2,32,2048]{2,1,0:T(8,128)(2,1)S(1)}, bf16[2,32,2048]{2,1,0:T(8,128)(2,1)S(1)}, u32[]{:S(2)}, u32[]{:S(2)}) %collective-permute-start.32) | collective-permute-done | bytes 262176 | tf_op jit(solution)/shard_map/ppermute | solution.py:116
  206.7 3.4 %collective-permute-start.33 = (bf16[32,2048]{1,0:T(8,128)(2,1)S(1)}, bf16[32,2048]{1,0:T(8,128)(2,1)S(1)}, u32[]{:S(2)}, u32[]{:S(2)}) collective-permute-start(bf16[32,2048]{1,0:T(8,128)(2,1)S(1)} %get-tuple-element.49), channel_id=1, source_target_pairs={{0,16},{16,0},{1,17},{17,1},{2,18},{18,2},{3,19},{19,3},{4,20},{20... | collective-permute-start | bytes 393224 | tf_op jit(solution)/shard_map/ppermute | solution.py:106
  210.3 2.9 %collective-permute-done.33 = bf16[32,2048]{1,0:T(8,128)(2,1)S(1)} collective-permute-done((bf16[32,2048]{1,0:T(8,128)(2,1)S(1)}, bf16[32,2048]{1,0:T(8,128)(2,1)S(1)}, u32[]{:S(2)}, u32[]{:S(2)}) %collective-permute-start.33) | collective-permute-done | bytes 131104 | tf_op jit(solution)/shard_map/ppermute | solution.py:106
  213.3 3.3 %collective-permute-done.24 = bf16[32,2048]{1,0:T(8,128)(2,1)S(1)} collective-permute-done((bf16[32,2048]{1,0:T(8,128)(2,1)S(1)}, bf16[32,2048]{1,0:T(8,128)(2,1)S(1)}, u32[]{:S(2)}, u32[]{:S(2)}) %collective-permute-start.24) | collective-permute-done | bytes 131104 | tf_op jit(solution)/shard_map/ppermute | solution.py:106
  216.6 0.7 pad_maximum_fusion.9
  (138 shorter events, 11.3 us)
Async XLA Ops:
  0.0 2.9 %copy-start = (bf16[16384]{0:T(1024)(128)(2,1)S(1)}, bf16[16384]{0:T(1024)(128)(2,1)}, u32[]{:S(2)}) copy-start(bf16[16384]{0:T(1024)(128)(2,1)} %param.9) | copy-start | bytes 98308
  14.1 8.8 %collective-permute-start.8 = (bf16[2,32,2048]{2,1,0:T(8,128)(2,1)S(1)}, bf16[2,32,2048]{2,1,0:T(8,128)(2,1)S(1)}, u32[]{:S(2)}, u32[]{:S(2)}) collective-permute-start(bf16[2,32,2048]{2,1,0:T(8,128)(2,1)S(1)} %get-tuple-element.25), channel_id=1, source_target_pairs={{0,4},{4,8},{8,12},{12,0},{1,5},{5,9},{9,13},{13,1},{2,6},{6,10},{... | collective-permute-start | bytes 786440 | tf_op jit(solution)/shard_map/ppermute | solution.py:62
  15.7 7.6 %collective-permute-start.9 = (bf16[2,32,2048]{2,1,0:T(8,128)(2,1)S(1)}, bf16[2,32,2048]{2,1,0:T(8,128)(2,1)S(1)}, u32[]{:S(2)}, u32[]{:S(2)}) collective-permute-start(bf16[2,32,2048]{2,1,0:T(8,128)(2,1)S(1)} %get-tuple-element.25), channel_id=1, source_target_pairs={{0,12},{4,0},{8,4},{12,8},{1,13},{5,1},{9,5},{13,9},{2,14},{6,2},{... | collective-permute-start | bytes 786440 | tf_op jit(solution)/shard_map/ppermute | solution.py:66
  17.4 8.9 %collective-permute-start = (bf16[2,32,2048]{2,1,0:T(8,128)(2,1)S(1)}, bf16[2,32,2048]{2,1,0:T(8,128)(2,1)S(1)}, u32[]{:S(2)}, u32[]{:S(2)}) collective-permute-start(bf16[2,32,2048]{2,1,0:T(8,128)(2,1)S(1)} %get-tuple-element.26), channel_id=1, source_target_pairs={{0,1},{1,2},{2,3},{3,0},{4,5},{5,6},{6,7},{7,4},{8,9},{9,10},{10,1... | collective-permute-start | bytes 786440 | tf_op jit(solution)/shard_map/ppermute | solution.py:62
  19.0 8.9 %collective-permute-start.1 = (bf16[2,32,2048]{2,1,0:T(8,128)(2,1)S(1)}, bf16[2,32,2048]{2,1,0:T(8,128)(2,1)S(1)}, u32[]{:S(2)}, u32[]{:S(2)}) collective-permute-start(bf16[2,32,2048]{2,1,0:T(8,128)(2,1)S(1)} %get-tuple-element.26), channel_id=1, source_target_pairs={{0,3},{1,0},{2,1},{3,2},{4,7},{5,4},{6,5},{7,6},{8,11},{9,8},{10,9... | collective-permute-start | bytes 786440 | tf_op jit(solution)/shard_map/ppermute | solution.py:66
  20.9 17.2 %copy-start.2 = (bf16[4096,512]{1,0:T(8,128)(2,1)S(1)}, bf16[4096,512]{1,0:T(8,128)(2,1)}, u32[]{:S(2)}) copy-start(bf16[4096,512]{1,0:T(8,128)(2,1)} %param.10) | copy-start | bytes 12582916
  22.9 12.2 %collective-permute-start.10 = (bf16[2,32,1024]{2,1,0:T(8,128)(2,1)S(1)}, bf16[2,32,1024]{2,1,0:T(8,128)(2,1)S(1)}, u32[]{:S(2)}, u32[]{:S(2)}) collective-permute-start(bf16[2,32,1024]{2,1,0:T(8,128)(2,1)S(1)} %slice.216), channel_id=1, source_target_pairs={{0,4},{4,8},{8,12},{12,0},{1,5},{5,9},{9,13},{13,1},{2,6},{6,10},{... | collective-permute-start | bytes 393224 | tf_op jit(solution)/shard_map/ppermute | solution.py:69
  23.2 11.9 %collective-permute-start.11 = (bf16[2,32,1024]{2,1,0:T(8,128)(2,1)S(1)}, bf16[2,32,1024]{2,1,0:T(8,128)(2,1)S(1)}, u32[]{:S(2)}, u32[]{:S(2)}) collective-permute-start(bf16[2,32,1024]{2,1,0:T(8,128)(2,1)S(1)} %slice.217), channel_id=1, source_target_pairs={{0,12},{4,0},{8,4},{12,8},{1,13},{5,1},{9,5},{13,9},{2,14},{6,2},{... | collective-permute-start | bytes 393224 | tf_op jit(solution)/shard_map/ppermute | solution.py:70
  26.3 6.2 %collective-permute-start.2 = (bf16[2,32,1024]{2,1,0:T(8,128)(2,1)S(1)}, bf16[2,32,1024]{2,1,0:T(8,128)(2,1)S(1)}, u32[]{:S(2)}, u32[]{:S(2)}) collective-permute-start(bf16[2,32,1024]{2,1,0:T(8,128)(2,1)S(1)} %slice.211), channel_id=1, source_target_pairs={{0,1},{1,2},{2,3},{3,0},{4,5},{5,6},{6,7},{7,4},{8,9},{9,10},{10,1... | collective-permute-start | bytes 393224 | tf_op jit(solution)/shard_map/ppermute | solution.py:69
  27.9 5.0 %collective-permute-start.3 = (bf16[2,32,1024]{2,1,0:T(8,128)(2,1)S(1)}, bf16[2,32,1024]{2,1,0:T(8,128)(2,1)S(1)}, u32[]{:S(2)}, u32[]{:S(2)}) collective-permute-start(bf16[2,32,1024]{2,1,0:T(8,128)(2,1)S(1)} %slice.212), channel_id=1, source_target_pairs={{0,3},{1,0},{2,1},{3,2},{4,7},{5,4},{6,5},{7,6},{8,11},{9,8},{10,9... | collective-permute-start | bytes 393224 | tf_op jit(solution)/shard_map/ppermute | solution.py:70
  33.0 5.8 %copy-start.5 = (bf16[4096,64]{0,1:T(8,128)(2,1)S(1)}, bf16[4096,64]{0,1:T(8,128)(2,1)}, u32[]{:S(2)}) copy-start(bf16[4096,64]{0,1:T(8,128)(2,1)} %param.11) | copy-start | bytes 1572868
  33.0 23.3 %collective-permute-start.5 = (bf16[4,2,32,2048]{3,2,1,0:T(8,128)(2,1)S(1)}, bf16[4,2,32,2048]{3,2,1,0:T(8,128)(2,1)S(1)}, u32[]{:S(2)}, u32[]{:S(2)}) collective-permute-start(bf16[4,2,32,2048]{3,2,1,0:T(8,128)(2,1)S(1)} %fusion.61), channel_id=1, source_target_pairs={{0,12},{4,0},{8,4},{12,8},{1,13},{5,1},{9,5},{13,9},{2,14},{6,2},{... | collective-permute-start | bytes 3145736 | tf_op jit(solution)/shard_map/ppermute | solution.py:80
  33.5 23.3 %collective-permute-start.4 = (bf16[4,2,32,2048]{3,2,1,0:T(8,128)(2,1)S(1)}, bf16[4,2,32,2048]{3,2,1,0:T(8,128)(2,1)S(1)}, u32[]{:S(2)}, u32[]{:S(2)}) collective-permute-start(bf16[4,2,32,2048]{3,2,1,0:T(8,128)(2,1)S(1)} %fusion.61), channel_id=1, source_target_pairs={{0,4},{4,8},{8,12},{12,0},{1,5},{5,9},{9,13},{13,1},{2,6},{6,10},{... | collective-permute-start | bytes 3145736 | tf_op jit(solution)/shard_map/ppermute | solution.py:79
  35.1 23.4 %collective-permute-start.13 = (bf16[4,2,32,2048]{3,2,1,0:T(8,128)(2,1)S(1)}, bf16[4,2,32,2048]{3,2,1,0:T(8,128)(2,1)S(1)}, u32[]{:S(2)}, u32[]{:S(2)}) collective-permute-start(bf16[4,2,32,2048]{3,2,1,0:T(8,128)(2,1)S(1)} %fusion.62), channel_id=1, source_target_pairs={{0,3},{1,0},{2,1},{3,2},{4,7},{5,4},{6,5},{7,6},{8,11},{9,8},{10,9... | collective-permute-start | bytes 3145736 | tf_op jit(solution)/shard_map/ppermute | solution.py:80
  38.1 23.5 %collective-permute-start.12 = (bf16[4,2,32,2048]{3,2,1,0:T(8,128)(2,1)S(1)}, bf16[4,2,32,2048]{3,2,1,0:T(8,128)(2,1)S(1)}, u32[]{:S(2)}, u32[]{:S(2)}) collective-permute-start(bf16[4,2,32,2048]{3,2,1,0:T(8,128)(2,1)S(1)} %fusion.62), channel_id=1, source_target_pairs={{0,1},{1,2},{2,3},{3,0},{4,5},{5,6},{6,7},{7,4},{8,9},{9,10},{10,1... | collective-permute-start | bytes 3145736 | tf_op jit(solution)/shard_map/ppermute | solution.py:79
  56.3 15.9 %collective-permute-start.7 = (bf16[4,2,32,1024]{3,2,1,0:T(8,128)(2,1)S(1)}, bf16[4,2,32,1024]{3,2,1,0:T(8,128)(2,1)S(1)}, u32[]{:S(2)}, u32[]{:S(2)}) collective-permute-start(bf16[4,2,32,1024]{3,2,1,0:T(8,128)(2,1)S(1)} %slice.214), channel_id=1, source_target_pairs={{0,12},{4,0},{8,4},{12,8},{1,13},{5,1},{9,5},{13,9},{2,14},{6,2},{... | collective-permute-start | bytes 1572872 | tf_op jit(solution)/shard_map/ppermute | solution.py:86
  56.9 10.6 %collective-permute-start.6 = (bf16[4,2,32,1024]{3,2,1,0:T(8,128)(2,1)S(1)}, bf16[4,2,32,1024]{3,2,1,0:T(8,128)(2,1)S(1)}, u32[]{:S(2)}, u32[]{:S(2)}) collective-permute-start(bf16[4,2,32,1024]{3,2,1,0:T(8,128)(2,1)S(1)} %slice.213), channel_id=1, source_target_pairs={{0,4},{4,8},{8,12},{12,0},{1,5},{5,9},{9,13},{13,1},{2,6},{6,10},{... | collective-permute-start | bytes 1572872 | tf_op jit(solution)/shard_map/ppermute | solution.py:85
  58.6 14.9 %collective-permute-start.15 = (bf16[4,2,32,1024]{3,2,1,0:T(8,128)(2,1)S(1)}, bf16[4,2,32,1024]{3,2,1,0:T(8,128)(2,1)S(1)}, u32[]{:S(2)}, u32[]{:S(2)}) collective-permute-start(bf16[4,2,32,1024]{3,2,1,0:T(8,128)(2,1)S(1)} %slice.219), channel_id=1, source_target_pairs={{0,3},{1,0},{2,1},{3,2},{4,7},{5,4},{6,5},{7,6},{8,11},{9,8},{10,9... | collective-permute-start | bytes 1572872 | tf_op jit(solution)/shard_map/ppermute | solution.py:86
  61.6 10.6 %collective-permute-start.14 = (bf16[4,2,32,1024]{3,2,1,0:T(8,128)(2,1)S(1)}, bf16[4,2,32,1024]{3,2,1,0:T(8,128)(2,1)S(1)}, u32[]{:S(2)}, u32[]{:S(2)}) collective-permute-start(bf16[4,2,32,1024]{3,2,1,0:T(8,128)(2,1)S(1)} %slice.218), channel_id=1, source_target_pairs={{0,1},{1,2},{2,3},{3,0},{4,5},{5,6},{6,7},{7,4},{8,9},{9,10},{10,1... | collective-permute-start | bytes 1572872 | tf_op jit(solution)/shard_map/ppermute | solution.py:85
  76.4 6.6 %copy-start.1 = (s32[8]{0:T(128)S(1)}, s32[8]{0:T(128)}, u32[]{:S(2)}) copy-start(s32[8]{0:T(128)} %param.14) | copy-start | bytes 100
  76.4 27.4 %all-to-all-start = ((bf16[128,8,576]{2,1,0:T(8,128)(2,1)}), bf16[128,8,576]{2,1,0:T(8,128)(2,1)S(1)}, u32[]{:S(2)}, u32[]{:S(2)}) async-start(bf16[128,8,576]{2,1,0:T(8,128)(2,1)} %bitcast.30), calls=%async_computation | async-start | bytes 2621440 | tf_op jit(solution)/shard_map/all_to_all | solution.py:150
  105.4 4.1 %copy-start.3 = (bf16[8,256,8,128]{3,2,1,0:T(8,128)(2,1)S(1)}, bf16[8,256,8,128]{3,2,1,0:T(8,128)(2,1)}, u32[]{:S(2)}) copy-start(bf16[8,256,8,128]{3,2,1,0:T(8,128)(2,1)} %param.13) | copy-start | bytes 12582916
  112.0 23.2 %all-to-all-start.1 = ((bf16[128,8,512]{2,1,0:T(8,128)(2,1)}), bf16[128,8,512]{2,1,0:T(8,128)(2,1)S(1)}, u32[]{:S(2)}, u32[]{:S(2)}) async-start(bf16[128,8,512]{2,1,0:T(8,128)(2,1)} %bitcast.42), calls=%async_computation.1 | async-start | bytes 2097152 | tf_op jit(solution)/shard_map/all_to_all | solution.py:159
  135.2 4.8 %copy-start.4 = (bf16[512,4096]{1,0:T(8,128)(2,1)S(1)}, bf16[512,4096]{1,0:T(8,128)(2,1)}, u32[]{:S(2)}) copy-start(bf16[512,4096]{1,0:T(8,128)(2,1)} %param.15) | copy-start | bytes 12582916
  142.3 19.0 %collective-permute-start.25 = (bf16[2,4,32,1024]{3,2,1,0:T(8,128)(2,1)S(1)}, bf16[2,4,32,1024]{3,2,1,0:T(8,128)(2,1)S(1)}, u32[]{:S(2)}, u32[]{:S(2)}) collective-permute-start(bf16[2,4,32,1024]{3,2,1,0:T(8,128)(2,1)S(1)} %get-tuple-element.19), channel_id=1, source_target_pairs={{0,12},{4,0},{8,4},{12,8},{1,13},{5,1},{9,5},{13,9},{2,14},{6,2},{... | collective-permute-start | bytes 1572872 | tf_op jit(solution)/shard_map/ppermute | solution.py:109
  144.9 18.6 %collective-permute-start.27 = (bf16[2,4,32,1024]{3,2,1,0:T(8,128)(2,1)S(1)}, bf16[2,4,32,1024]{3,2,1,0:T(8,128)(2,1)S(1)}, u32[]{:S(2)}, u32[]{:S(2)}) collective-permute-start(bf16[2,4,32,1024]{3,2,1,0:T(8,128)(2,1)S(1)} %get-tuple-element.20), channel_id=1, source_target_pairs={{0,4},{4,8},{8,12},{12,0},{1,5},{5,9},{9,13},{13,1},{2,6},{6,10},{... | collective-permute-start | bytes 1572872 | tf_op jit(solution)/shard_map/ppermute | solution.py:110
  145.0 12.9 %collective-permute-start.16 = (bf16[2,4,32,1024]{3,2,1,0:T(8,128)(2,1)S(1)}, bf16[2,4,32,1024]{3,2,1,0:T(8,128)(2,1)S(1)}, u32[]{:S(2)}, u32[]{:S(2)}) collective-permute-start(bf16[2,4,32,1024]{3,2,1,0:T(8,128)(2,1)S(1)} %get-tuple-element.10), channel_id=1, source_target_pairs={{0,3},{1,0},{2,1},{3,2},{4,7},{5,4},{6,5},{7,6},{8,11},{9,8},{10,9... | collective-permute-start | bytes 1572872 | tf_op jit(solution)/shard_map/ppermute | solution.py:109
  147.0 13.9 %collective-permute-start.18 = (bf16[2,4,32,1024]{3,2,1,0:T(8,128)(2,1)S(1)}, bf16[2,4,32,1024]{3,2,1,0:T(8,128)(2,1)S(1)}, u32[]{:S(2)}, u32[]{:S(2)}) collective-permute-start(bf16[2,4,32,1024]{3,2,1,0:T(8,128)(2,1)S(1)} %get-tuple-element.11), channel_id=1, source_target_pairs={{0,1},{1,2},{2,3},{3,0},{4,5},{5,6},{6,7},{7,4},{8,9},{9,10},{10,1... | collective-permute-start | bytes 1572872 | tf_op jit(solution)/shard_map/ppermute | solution.py:110
  158.1 23.3 %collective-permute-start.17 = (bf16[2,4,32,2048]{3,2,1,0:T(8,128)(2,1)S(1)}, bf16[2,4,32,2048]{3,2,1,0:T(8,128)(2,1)S(1)}, u32[]{:S(2)}, u32[]{:S(2)}) collective-permute-start(bf16[2,4,32,2048]{3,2,1,0:T(8,128)(2,1)S(1)} %pad_maximum_fusion), channel_id=1, source_target_pairs={{0,3},{1,0},{2,1},{3,2},{4,7},{5,4},{6,5},{7,6},{8,11},{9,8},{10,9... | collective-permute-start | bytes 3145736 | tf_op jit(solution)/shard_map/ppermute | solution.py:115
  161.1 23.8 %collective-permute-start.19 = (bf16[2,4,32,2048]{3,2,1,0:T(8,128)(2,1)S(1)}, bf16[2,4,32,2048]{3,2,1,0:T(8,128)(2,1)S(1)}, u32[]{:S(2)}, u32[]{:S(2)}) collective-permute-start(bf16[2,4,32,2048]{3,2,1,0:T(8,128)(2,1)S(1)} %pad_maximum_fusion.1), channel_id=1, source_target_pairs={{0,1},{1,2},{2,3},{3,0},{4,5},{5,6},{6,7},{7,4},{8,9},{9,10},{10,1... | collective-permute-start | bytes 3145736 | tf_op jit(solution)/shard_map/ppermute | solution.py:116
  161.4 25.9 %collective-permute-start.26 = (bf16[2,4,32,2048]{3,2,1,0:T(8,128)(2,1)S(1)}, bf16[2,4,32,2048]{3,2,1,0:T(8,128)(2,1)S(1)}, u32[]{:S(2)}, u32[]{:S(2)}) collective-permute-start(bf16[2,4,32,2048]{3,2,1,0:T(8,128)(2,1)S(1)} %pad_maximum_fusion.2), channel_id=1, source_target_pairs={{0,12},{4,0},{8,4},{12,8},{1,13},{5,1},{9,5},{13,9},{2,14},{6,2},{... | collective-permute-start | bytes 3145736 | tf_op jit(solution)/shard_map/ppermute | solution.py:115
  163.7 23.6 %collective-permute-start.28 = (bf16[2,4,32,2048]{3,2,1,0:T(8,128)(2,1)S(1)}, bf16[2,4,32,2048]{3,2,1,0:T(8,128)(2,1)S(1)}, u32[]{:S(2)}, u32[]{:S(2)}) collective-permute-start(bf16[2,4,32,2048]{3,2,1,0:T(8,128)(2,1)S(1)} %pad_maximum_fusion.3), channel_id=1, source_target_pairs={{0,4},{4,8},{8,12},{12,0},{1,5},{5,9},{9,13},{13,1},{2,6},{6,10},{... | collective-permute-start | bytes 3145736 | tf_op jit(solution)/shard_map/ppermute | solution.py:116
  185.2 8.6 %collective-permute-start.20 = (bf16[2,32,1024]{2,1,0:T(8,128)(2,1)S(1)}, bf16[2,32,1024]{2,1,0:T(8,128)(2,1)S(1)}, u32[]{:S(2)}, u32[]{:S(2)}) collective-permute-start(bf16[2,32,1024]{2,1,0:T(8,128)(2,1)S(1)} %get-tuple-element.29), channel_id=1, source_target_pairs={{0,12},{4,0},{8,4},{12,8},{1,13},{5,1},{9,5},{13,9},{2,14},{6,2},{... | collective-permute-start | bytes 393224 | tf_op jit(solution)/shard_map/ppermute | solution.py:109
  186.7 6.9 %collective-permute-start.22 = (bf16[2,32,1024]{2,1,0:T(8,128)(2,1)S(1)}, bf16[2,32,1024]{2,1,0:T(8,128)(2,1)S(1)}, u32[]{:S(2)}, u32[]{:S(2)}) collective-permute-start(bf16[2,32,1024]{2,1,0:T(8,128)(2,1)S(1)} %get-tuple-element.30), channel_id=1, source_target_pairs={{0,4},{4,8},{8,12},{12,0},{1,5},{5,9},{9,13},{13,1},{2,6},{6,10},{... | collective-permute-start | bytes 393224 | tf_op jit(solution)/shard_map/ppermute | solution.py:110
  187.6 11.4 %collective-permute-start.29 = (bf16[2,32,1024]{2,1,0:T(8,128)(2,1)S(1)}, bf16[2,32,1024]{2,1,0:T(8,128)(2,1)S(1)}, u32[]{:S(2)}, u32[]{:S(2)}) collective-permute-start(bf16[2,32,1024]{2,1,0:T(8,128)(2,1)S(1)} %get-tuple-element.35), channel_id=1, source_target_pairs={{0,3},{1,0},{2,1},{3,2},{4,7},{5,4},{6,5},{7,6},{8,11},{9,8},{10,9... | collective-permute-start | bytes 393224 | tf_op jit(solution)/shard_map/ppermute | solution.py:109
  191.3 7.6 %collective-permute-start.31 = (bf16[2,32,1024]{2,1,0:T(8,128)(2,1)S(1)}, bf16[2,32,1024]{2,1,0:T(8,128)(2,1)S(1)}, u32[]{:S(2)}, u32[]{:S(2)}) collective-permute-start(bf16[2,32,1024]{2,1,0:T(8,128)(2,1)S(1)} %get-tuple-element.36), channel_id=1, source_target_pairs={{0,1},{1,2},{2,3},{3,0},{4,5},{5,6},{6,7},{7,4},{8,9},{9,10},{10,1... | collective-permute-start | bytes 393224 | tf_op jit(solution)/shard_map/ppermute | solution.py:110
  193.7 8.7 %collective-permute-start.23 = (bf16[2,32,2048]{2,1,0:T(8,128)(2,1)S(1)}, bf16[2,32,2048]{2,1,0:T(8,128)(2,1)S(1)}, u32[]{:S(2)}, u32[]{:S(2)}) collective-permute-start(bf16[2,32,2048]{2,1,0:T(8,128)(2,1)S(1)} %pad_maximum_fusion.6), channel_id=1, source_target_pairs={{0,4},{4,8},{8,12},{12,0},{1,5},{5,9},{9,13},{13,1},{2,6},{6,10},{... | collective-permute-start | bytes 786440 | tf_op jit(solution)/shard_map/ppermute | solution.py:116
  193.9 8.5 %collective-permute-start.21 = (bf16[2,32,2048]{2,1,0:T(8,128)(2,1)S(1)}, bf16[2,32,2048]{2,1,0:T(8,128)(2,1)S(1)}, u32[]{:S(2)}, u32[]{:S(2)}) collective-permute-start(bf16[2,32,2048]{2,1,0:T(8,128)(2,1)S(1)} %pad_maximum_fusion.5), channel_id=1, source_target_pairs={{0,12},{4,0},{8,4},{12,8},{1,13},{5,1},{9,5},{13,9},{2,14},{6,2},{... | collective-permute-start | bytes 786440 | tf_op jit(solution)/shard_map/ppermute | solution.py:115
  198.9 7.7 %collective-permute-start.32 = (bf16[2,32,2048]{2,1,0:T(8,128)(2,1)S(1)}, bf16[2,32,2048]{2,1,0:T(8,128)(2,1)S(1)}, u32[]{:S(2)}, u32[]{:S(2)}) collective-permute-start(bf16[2,32,2048]{2,1,0:T(8,128)(2,1)S(1)} %pad_maximum_fusion.8), channel_id=1, source_target_pairs={{0,1},{1,2},{2,3},{3,0},{4,5},{5,6},{6,7},{7,4},{8,9},{9,10},{10,1... | collective-permute-start | bytes 786440 | tf_op jit(solution)/shard_map/ppermute | solution.py:116
  199.1 7.5 %collective-permute-start.30 = (bf16[2,32,2048]{2,1,0:T(8,128)(2,1)S(1)}, bf16[2,32,2048]{2,1,0:T(8,128)(2,1)S(1)}, u32[]{:S(2)}, u32[]{:S(2)}) collective-permute-start(bf16[2,32,2048]{2,1,0:T(8,128)(2,1)S(1)} %pad_maximum_fusion.7), channel_id=1, source_target_pairs={{0,3},{1,0},{2,1},{3,2},{4,7},{5,4},{6,5},{7,6},{8,11},{9,8},{10,9... | collective-permute-start | bytes 786440 | tf_op jit(solution)/shard_map/ppermute | solution.py:115
  206.7 6.6 %collective-permute-start.33 = (bf16[32,2048]{1,0:T(8,128)(2,1)S(1)}, bf16[32,2048]{1,0:T(8,128)(2,1)S(1)}, u32[]{:S(2)}, u32[]{:S(2)}) collective-permute-start(bf16[32,2048]{1,0:T(8,128)(2,1)S(1)} %get-tuple-element.49), channel_id=1, source_target_pairs={{0,16},{16,0},{1,17},{17,1},{2,18},{18,2},{3,19},{19,3},{4,20},{20... | collective-permute-start | bytes 393224 | tf_op jit(solution)/shard_map/ppermute | solution.py:106
  210.1 6.5 %collective-permute-start.24 = (bf16[32,2048]{1,0:T(8,128)(2,1)S(1)}, bf16[32,2048]{1,0:T(8,128)(2,1)S(1)}, u32[]{:S(2)}, u32[]{:S(2)}) collective-permute-start(bf16[32,2048]{1,0:T(8,128)(2,1)S(1)} %get-tuple-element.50), channel_id=1, source_target_pairs={{0,16},{16,0},{1,17},{17,1},{2,18},{18,2},{3,19},{19,3},{4,20},{20... | collective-permute-start | bytes 393224 | tf_op jit(solution)/shard_map/ppermute | solution.py:106

commit v2 on v1

--- a/solution.py
+++ b/solution.py
@@ -117,6 +117,14 @@
     return take(idx) + got_right + got_left
 
 
+def neighbour_pairs():
+    pairs = []
+    for gx in range(4):
+        for gy in range(32):
+            pairs.append((gx * 32 + gy, ((gx + 2) % 4) * 32 + (gy + 16) % 32))
+    return pairs
+
+
 def shards(hidden, norm_gain, w_query, w_keyval, key_cache, value_cache, lengths, w_out):
     width_part = w_query.shape[0]
     query_cols = w_query.shape[1]
@@ -125,8 +133,15 @@
     values = hidden.astype(jnp.float32)
     inverse = lax.rsqrt(jnp.mean(values * values, axis=1, keepdims=True) + 1e-05)
     normed = (values * inverse * norm_gain.astype(jnp.float32)).astype(jnp.bfloat16)
-    own_cols = lax.dynamic_slice_in_dim(normed, lax.axis_index("gx") * width_part, width_part, 1)
-    pair = lax.all_gather(own_cols, "zh", axis=0, tiled=False)
+    gx = lax.axis_index("gx")
+    own_cols = lax.dynamic_slice_in_dim(normed, gx * width_part, width_part, 1)
+    partner_gx = (gx + 2) % 4
+    sent = lax.dynamic_slice_in_dim(normed, partner_gx * width_part, width_part, 1)
+    got = lax.ppermute(sent, ALL, neighbour_pairs())
+    zh = lax.axis_index("zh")
+    pair = jnp.zeros((2,) + own_cols.shape, own_cols.dtype)
+    pair = lax.dynamic_update_index_in_dim(pair, own_cols, zh, 0)
+    pair = lax.dynamic_update_index_in_dim(pair, got, 1 - zh, 0)
     first = pair[..., : width_part // 2]
     second = pair[..., width_part // 2 :]
     first = ring_all_gather(first, "y", 4, 0)

time: 218 us -> 217 us (level)
  blocking collectives: 11 us -> 0 us
  waiting for transfers between devices: 108 us -> 113 us
  starting transfers between devices: 61.9 us -> 66.5 us
    all_gather x1 -> x0, blocking collectives: 11 us -> none  [shards(): pair = lax.all_gather(own_cols, 'zh', axis=0, tiled=False)]
    ppermute x0 -> x1, waiting for transfers between devices: none -> 6.23 us  [shards(): got = lax.ppermute(sent, ALL, neighbour_pairs())]
    ppermute x0 -> x1, starting transfers between devices: none -> 4.23 us  [shards(): got = lax.ppermute(sent, ALL, neighbour_pairs())]
    ppermute x2, waiting for transfers between devices: 2.74 us -> 0.28 us  [ring_all_gather(): first = lax.ppermute(from_left[..., :half], axis, fwd)]
  transfers between devices with their start and end apart: 36 -> 37, of which waited for: 16 -> 17; matrix products, arithmetic and copies ran while one was open for 6% -> 6% of each run, Pallas kernels for 0% -> 0%
where the time goes in v2:
time: 217 us
  waiting for transfers between devices  113 us (52%)
  starting transfers between devices  66.5 us (31%)
  matrix products  23 us (11%)
  other arithmetic  9.38 us (4%)
  local copies, waits for them, and re-layouts  3.69 us (2%)
    all_to_all x1, waiting for transfers between devices, shards(): lax.all_to_all(projected.astype(jnp.bfloat16), ALL, split_axis=0, concat_...  20.6 us
    all_to_all x1, waiting for transfers between devices, shards(): lax.all_to_all(sent, ALL, split_axis=0, concat_axis=0, tiled=True)  17.6 us
    ppermute x4, waiting for transfers between devices, ring_reduce_scatter(): got_right = lax.ppermute(to_left, axis, bwd)  16.8 us
    ppermute x2, waiting for transfers between devices, ring_all_gather_apply(): from_right = lax.ppermute(blk, axis, bwd)  14.3 us
    ppermute x4, starting transfers between devices, ring_reduce_scatter(): got_right = lax.ppermute(to_left, axis, bwd)  11.6 us
    ppermute x4, starting transfers between devices, ring_reduce_scatter(): from_right = lax.ppermute(opposite[..., :half], axis, bwd)  9.87 us
    ppermute x4, waiting for transfers between devices, ring_reduce_scatter(): from_right = lax.ppermute(opposite[..., :half], axis, bwd)  9.35 us
    dot_general x8, matrix products, partial_out(): jnp.dot(lax.dynamic_index_in_dim(by_row, k, dim, keepdims=False), w_out[:...  9.03 us
  transfers between devices with their start and end apart: 37, of which 17 were waited for; matrix products, arithmetic and copies ran while one was open for 6% of the time, Pallas kernels for 0%

profile of v2, /device:TPU:0, one launch (start us, length us, event | category | flops | bytes accessed | tf_op | source)
XLA Modules:
  0.0 216.7 jit_solution(6212904138445602106)
XLA Ops:
  0.0 1.5 fusion.4
  1.5 0.8 convert_element_type.87
  2.3 1.5 fusion.6
  3.9 4.2 %collective-permute-start = (bf16[32,4096]{1,0:T(8,128)(2,1)S(1)}, bf16[32,4096]{1,0:T(8,128)(2,1)S(1)}, u32[]{:S(2)}, u32[]{:S(2)}) collective-permute-start(bf16[32,4096]{1,0:T(8,128)(2,1)S(1)} %constant_dynamic-slice_fusion), channel_id=1, source_target_pairs={{0,80},{1,81},{2,82},{3,83},{4,84},{5,85},{6,86},{7,87},{8,88},{9,... | collective-permute-start | bytes 786440 | tf_op jit(solution)/shard_map/ppermute | solution.py:140
  8.2 6.2 %collective-permute-done = bf16[32,4096]{1,0:T(8,128)(2,1)S(1)} collective-permute-done((bf16[32,4096]{1,0:T(8,128)(2,1)S(1)}, bf16[32,4096]{1,0:T(8,128)(2,1)S(1)}, u32[]{:S(2)}, u32[]{:S(2)}) %collective-permute-start) | collective-permute-done | bytes 262176 | tf_op jit(solution)/shard_map/ppermute | solution.py:140
  14.5 1.6 collective-permute-start.9
  16.1 1.7 collective-permute-start.10
  17.8 1.6 collective-permute-start.1
  19.4 1.7 collective-permute-start.2
  21.4 1.9 collective-permute-done.9
  23.6 3.0 %collective-permute-start.12 = (bf16[2,32,1024]{2,1,0:T(8,128)(2,1)S(1)}, bf16[2,32,1024]{2,1,0:T(8,128)(2,1)S(1)}, u32[]{:S(2)}, u32[]{:S(2)}) collective-permute-start(bf16[2,32,1024]{2,1,0:T(8,128)(2,1)S(1)} %slice.217), channel_id=1, source_target_pairs={{0,12},{4,0},{8,4},{12,8},{1,13},{5,1},{9,5},{13,9},{2,14},{6,2},{... | collective-permute-start | bytes 393224 | tf_op jit(solution)/shard_map/ppermute | solution.py:70
  26.7 1.6 collective-permute-start.3
  28.3 1.7 collective-permute-start.4
  30.2 2.4 %collective-permute-start.14 = (bf16[4,2,32,2048]{3,2,1,0:T(8,128)(2,1)S(1)}, bf16[4,2,32,2048]{3,2,1,0:T(8,128)(2,1)S(1)}, u32[]{:S(2)}, u32[]{:S(2)}) collective-permute-start(bf16[4,2,32,2048]{3,2,1,0:T(8,128)(2,1)S(1)} %fusion.63), channel_id=1, source_target_pairs={{0,3},{1,0},{2,1},{3,2},{4,7},{5,4},{6,5},{7,6},{8,11},{9,8},{10,9... | collective-permute-start | bytes 3145736 | tf_op jit(solution)/shard_map/ppermute | solution.py:80
  32.9 1.9 collective-permute-done.4
  34.8 1.3 collective-permute-start.6
  36.1 0.8 collective-permute-start.5
  36.9 0.7 fusion.29
  38.8 0.7 fusion.21
  39.9 14.3 %collective-permute-done.14 = bf16[4,2,32,2048]{3,2,1,0:T(8,128)(2,1)S(1)} collective-permute-done((bf16[4,2,32,2048]{3,2,1,0:T(8,128)(2,1)S(1)}, bf16[4,2,32,2048]{3,2,1,0:T(8,128)(2,1)S(1)}, u32[]{:S(2)}, u32[]{:S(2)}) %collective-permute-start.14) | collective-permute-done | bytes 1048608 | tf_op jit(solution)/shard_map/ppermute | solution.py:80
  54.2 3.5 %collective-permute-start.16 = (bf16[4,2,32,1024]{3,2,1,0:T(8,128)(2,1)S(1)}, bf16[4,2,32,1024]{3,2,1,0:T(8,128)(2,1)S(1)}, u32[]{:S(2)}, u32[]{:S(2)}) collective-permute-start(bf16[4,2,32,1024]{3,2,1,0:T(8,128)(2,1)S(1)} %slice.219), channel_id=1, source_target_pairs={{0,3},{1,0},{2,1},{3,2},{4,7},{5,4},{6,5},{7,6},{8,11},{9,8},{10,9... | collective-permute-start | bytes 1572872 | tf_op jit(solution)/shard_map/ppermute | solution.py:86
  57.9 2.1 collective-permute-start.8
  60.7 0.7 fusion.17
  61.8 0.7 fusion.19
  63.0 0.7 fusion.25
  63.7 0.7 fusion.27
  65.1 5.0 %collective-permute-done.15 = bf16[4,2,32,1024]{3,2,1,0:T(8,128)(2,1)S(1)} collective-permute-done((bf16[4,2,32,1024]{3,2,1,0:T(8,128)(2,1)S(1)}, bf16[4,2,32,1024]{3,2,1,0:T(8,128)(2,1)S(1)}, u32[]{:S(2)}, u32[]{:S(2)}) %collective-permute-start.15) | collective-permute-done | bytes 524320 | tf_op jit(solution)/shard_map/ppermute | solution.py:85
  70.2 1.1 collective-permute-done.7
  71.8 0.7 fusion.15
  73.0 0.7 fusion.23
  73.8 1.6 add_convert_fusion
  75.4 7.0 %all-to-all-start = ((bf16[128,8,576]{2,1,0:T(8,128)(2,1)}), bf16[128,8,576]{2,1,0:T(8,128)(2,1)S(1)}, u32[]{:S(2)}, u32[]{:S(2)}) async-start(bf16[128,8,576]{2,1,0:T(8,128)(2,1)} %bitcast.31), calls=%async_computation | async-start | bytes 2621440 | tf_op jit(solution)/shard_map/all_to_all | solution.py:165
  82.6 20.6 %all-to-all-done = bf16[128,8,576]{2,1,0:T(8,128)(2,1)S(1)} async-done(((bf16[128,8,576]{2,1,0:T(8,128)(2,1)}), bf16[128,8,576]{2,1,0:T(8,128)(2,1)S(1)}, u32[]{:S(2)}, u32[]{:S(2)}) %all-to-all-start) | async-done | bytes 1179680 | tf_op jit(solution)/shard_map/all_to_all | solution.py:165
  104.8 3.7 %fusion.131 = (f32[8,8,16]{2,1,0:T(8,128)S(1)}, f32[8,8,16,256]{3,2,1,0:T(8,128)S(1)}) fusion(bf16[8,256,8,128]{3,2,1,0:T(8,128)(2,1)} %param.12, bf16[8,8,16,64]{3,2,1,0:T(8,128)(2,1)S(1)} %bitcast.223, bf16[8,8,16,64]{3,2,1,0:T(8,128)(2,1)S(1)} %bitcast.221, pred[8,256]{1,0:T(8,128)(4,1)S(1)} %iota_compare_fusion), kind=kOutput, calls=%fused_computation.215 | convolution fusion | flops 68418560 | bytes 5511168 | tf_op jit(solution)/shard_map/rgqd,rtgd->rgqt/dot_general | solution.py:39
  109.0 1.0 fusion.56
  110.3 1.1 broadcast_in_dim.116
  111.4 5.6 %all-to-all-start.1 = ((bf16[128,8,512]{2,1,0:T(8,128)(2,1)}), bf16[128,8,512]{2,1,0:T(8,128)(2,1)S(1)}, u32[]{:S(2)}, u32[]{:S(2)}) async-start(bf16[128,8,512]{2,1,0:T(8,128)(2,1)} %bitcast.43), calls=%async_computation.1 | async-start | bytes 2097152 | tf_op jit(solution)/shard_map/all_to_all | solution.py:174
  117.0 17.6 %all-to-all-done.1 = bf16[128,8,512]{2,1,0:T(8,128)(2,1)S(1)} async-done(((bf16[128,8,512]{2,1,0:T(8,128)(2,1)}), bf16[128,8,512]{2,1,0:T(8,128)(2,1)S(1)}, u32[]{:S(2)}, u32[]{:S(2)}) %all-to-all-start.1) | async-done | bytes 1048608 | tf_op jit(solution)/shard_map/all_to_all | solution.py:174
  134.6 2.5 %convolution_convert_fusion = bf16[2,4,32,2048]{3,2,1,0:T(8,128)(2,1)S(1)} fusion(bf16[512,4096]{1,0:T(8,128)(2,1)} %param.15, bf16[2,4,4,32,512]{4,3,2,1,0:T(8,128)(2,1)S(1)} %bitcast.211, s32[]{:T(128)S(6)} %select_n.191), kind=kOutput, calls=%fused_computation.7 | convolution fusion | flops 537395200 | bytes 3407876 | tf_op jit(solution)/shard_map/dot_general | solution.py:179
  137.1 2.3 %convolution_convert_fusion.1 = bf16[2,4,32,2048]{3,2,1,0:T(8,128)(2,1)S(1)} fusion(bf16[512,4096]{1,0:T(8,128)(2,1)} %param.15, bf16[2,4,4,32,512]{4,3,2,1,0:T(8,128)(2,1)S(1)} %bitcast.212, s32[]{:T(128)S(6)} %select_n.193), kind=kOutput, calls=%fused_computation.8 | convolution fusion | flops 537395200 | bytes 3407876 | tf_op jit(solution)/shard_map/dot_general | solution.py:179
  139.4 0.7 convolution_convert_fusion.2
  140.1 0.7 convolution_convert_fusion.4
  140.9 0.7 convolution_convert_fusion.5
  141.7 2.6 %collective-permute-start.26 = (bf16[2,4,32,1024]{3,2,1,0:T(8,128)(2,1)S(1)}, bf16[2,4,32,1024]{3,2,1,0:T(8,128)(2,1)S(1)}, u32[]{:S(2)}, u32[]{:S(2)}) collective-permute-start(bf16[2,4,32,1024]{3,2,1,0:T(8,128)(2,1)S(1)} %get-tuple-element.19), channel_id=1, source_target_pairs={{0,12},{4,0},{8,4},{12,8},{1,13},{5,1},{9,5},{13,9},{2,14},{6,2},{... | collective-permute-start | bytes 1572872 | tf_op jit(solution)/shard_map/ppermute | solution.py:109
  144.4 2.0 collective-permute-start.17
  146.5 0.7 convolution_convert_fusion.6
  147.2 0.7 convolution_convert_fusion.3
  147.9 9.3 %collective-permute-done.17 = bf16[2,4,32,1024]{3,2,1,0:T(8,128)(2,1)S(1)} collective-permute-done((bf16[2,4,32,1024]{3,2,1,0:T(8,128)(2,1)S(1)}, bf16[2,4,32,1024]{3,2,1,0:T(8,128)(2,1)S(1)}, u32[]{:S(2)}, u32[]{:S(2)}) %collective-permute-start.17) | collective-permute-done | bytes 524320 | tf_op jit(solution)/shard_map/ppermute | solution.py:109
  157.5 2.9 %collective-permute-start.18 = (bf16[2,4,32,2048]{3,2,1,0:T(8,128)(2,1)S(1)}, bf16[2,4,32,2048]{3,2,1,0:T(8,128)(2,1)S(1)}, u32[]{:S(2)}, u32[]{:S(2)}) collective-permute-start(bf16[2,4,32,2048]{3,2,1,0:T(8,128)(2,1)S(1)} %pad_maximum_fusion), channel_id=1, source_target_pairs={{0,3},{1,0},{2,1},{3,2},{4,7},{5,4},{6,5},{7,6},{8,11},{9,8},{10,9... | collective-permute-start | bytes 3145736 | tf_op jit(solution)/shard_map/ppermute | solution.py:115
  160.8 2.1 collective-permute-start.27
  163.2 0.7 convolution_convert_fusion.7
  163.9 16.8 %collective-permute-done.18 = bf16[2,4,32,2048]{3,2,1,0:T(8,128)(2,1)S(1)} collective-permute-done((bf16[2,4,32,2048]{3,2,1,0:T(8,128)(2,1)S(1)}, bf16[2,4,32,2048]{3,2,1,0:T(8,128)(2,1)S(1)}, u32[]{:S(2)}, u32[]{:S(2)}) %collective-permute-start.18) | collective-permute-done | bytes 1048608 | tf_op jit(solution)/shard_map/ppermute | solution.py:115
  180.7 3.7 %collective-permute-done.20 = bf16[2,4,32,2048]{3,2,1,0:T(8,128)(2,1)S(1)} collective-permute-done((bf16[2,4,32,2048]{3,2,1,0:T(8,128)(2,1)S(1)}, bf16[2,4,32,2048]{3,2,1,0:T(8,128)(2,1)S(1)}, u32[]{:S(2)}, u32[]{:S(2)}) %collective-permute-start.20) | collective-permute-done | bytes 1048608 | tf_op jit(solution)/shard_map/ppermute | solution.py:116
  184.6 1.5 collective-permute-start.21
  187.0 3.7 %collective-permute-start.30 = (bf16[2,32,1024]{2,1,0:T(8,128)(2,1)S(1)}, bf16[2,32,1024]{2,1,0:T(8,128)(2,1)S(1)}, u32[]{:S(2)}, u32[]{:S(2)}) collective-permute-start(bf16[2,32,1024]{2,1,0:T(8,128)(2,1)S(1)} %get-tuple-element.35), channel_id=1, source_target_pairs={{0,3},{1,0},{2,1},{3,2},{4,7},{5,4},{6,5},{7,6},{8,11},{9,8},{10,9... | collective-permute-start | bytes 393224 | tf_op jit(solution)/shard_map/ppermute | solution.py:109
  190.7 2.4 %collective-permute-done.23 = bf16[2,32,1024]{2,1,0:T(8,128)(2,1)S(1)} collective-permute-done((bf16[2,32,1024]{2,1,0:T(8,128)(2,1)S(1)}, bf16[2,32,1024]{2,1,0:T(8,128)(2,1)S(1)}, u32[]{:S(2)}, u32[]{:S(2)}) %collective-permute-start.23) | collective-permute-done | bytes 131104 | tf_op jit(solution)/shard_map/ppermute | solution.py:110
  193.3 3.3 %collective-permute-start.22 = (bf16[2,32,2048]{2,1,0:T(8,128)(2,1)S(1)}, bf16[2,32,2048]{2,1,0:T(8,128)(2,1)S(1)}, u32[]{:S(2)}, u32[]{:S(2)}) collective-permute-start(bf16[2,32,2048]{2,1,0:T(8,128)(2,1)S(1)} %pad_maximum_fusion.5), channel_id=1, source_target_pairs={{0,12},{4,0},{8,4},{12,8},{1,13},{5,1},{9,5},{13,9},{2,14},{6,2},{... | collective-permute-start | bytes 786440 | tf_op jit(solution)/shard_map/ppermute | solution.py:115
  196.6 1.7 collective-permute-done.32
  198.5 3.3 %collective-permute-start.31 = (bf16[2,32,2048]{2,1,0:T(8,128)(2,1)S(1)}, bf16[2,32,2048]{2,1,0:T(8,128)(2,1)S(1)}, u32[]{:S(2)}, u32[]{:S(2)}) collective-permute-start(bf16[2,32,2048]{2,1,0:T(8,128)(2,1)S(1)} %pad_maximum_fusion.7), channel_id=1, source_target_pairs={{0,3},{1,0},{2,1},{3,2},{4,7},{5,4},{6,5},{7,6},{8,11},{9,8},{10,9... | collective-permute-start | bytes 786440 | tf_op jit(solution)/shard_map/ppermute | solution.py:115
  201.9 4.2 %collective-permute-done.33 = bf16[2,32,2048]{2,1,0:T(8,128)(2,1)S(1)} collective-permute-done((bf16[2,32,2048]{2,1,0:T(8,128)(2,1)S(1)}, bf16[2,32,2048]{2,1,0:T(8,128)(2,1)S(1)}, u32[]{:S(2)}, u32[]{:S(2)}) %collective-permute-start.33) | collective-permute-done | bytes 262176 | tf_op jit(solution)/shard_map/ppermute | solution.py:116
  206.1 3.4 %collective-permute-start.34 = (bf16[32,2048]{1,0:T(8,128)(2,1)S(1)}, bf16[32,2048]{1,0:T(8,128)(2,1)S(1)}, u32[]{:S(2)}, u32[]{:S(2)}) collective-permute-start(bf16[32,2048]{1,0:T(8,128)(2,1)S(1)} %get-tuple-element.49), channel_id=1, source_target_pairs={{0,16},{16,0},{1,17},{17,1},{2,18},{18,2},{3,19},{19,3},{4,20},{20... | collective-permute-start | bytes 393224 | tf_op jit(solution)/shard_map/ppermute | solution.py:106
  209.7 2.9 %collective-permute-done.34 = bf16[32,2048]{1,0:T(8,128)(2,1)S(1)} collective-permute-done((bf16[32,2048]{1,0:T(8,128)(2,1)S(1)}, bf16[32,2048]{1,0:T(8,128)(2,1)S(1)}, u32[]{:S(2)}, u32[]{:S(2)}) %collective-permute-start.34) | collective-permute-done | bytes 131104 | tf_op jit(solution)/shard_map/ppermute | solution.py:106
  212.7 3.3 %collective-permute-done.25 = bf16[32,2048]{1,0:T(8,128)(2,1)S(1)} collective-permute-done((bf16[32,2048]{1,0:T(8,128)(2,1)S(1)}, bf16[32,2048]{1,0:T(8,128)(2,1)S(1)}, u32[]{:S(2)}, u32[]{:S(2)}) %collective-permute-start.25) | collective-permute-done | bytes 131104 | tf_op jit(solution)/shard_map/ppermute | solution.py:106
  216.0 0.7 pad_maximum_fusion.9
  (140 shorter events, 11.8 us)
Async XLA Ops:
  3.9 10.5 %collective-permute-start = (bf16[32,4096]{1,0:T(8,128)(2,1)S(1)}, bf16[32,4096]{1,0:T(8,128)(2,1)S(1)}, u32[]{:S(2)}, u32[]{:S(2)}) collective-permute-start(bf16[32,4096]{1,0:T(8,128)(2,1)S(1)} %constant_dynamic-slice_fusion), channel_id=1, source_target_pairs={{0,80},{1,81},{2,82},{3,83},{4,84},{5,85},{6,86},{7,87},{8,88},{9,... | collective-permute-start | bytes 786440 | tf_op jit(solution)/shard_map/ppermute | solution.py:140
  14.5 8.8 %collective-permute-start.9 = (bf16[2,32,2048]{2,1,0:T(8,128)(2,1)S(1)}, bf16[2,32,2048]{2,1,0:T(8,128)(2,1)S(1)}, u32[]{:S(2)}, u32[]{:S(2)}) collective-permute-start(bf16[2,32,2048]{2,1,0:T(8,128)(2,1)S(1)} %get-tuple-element.25), channel_id=1, source_target_pairs={{0,4},{4,8},{8,12},{12,0},{1,5},{5,9},{9,13},{13,1},{2,6},{6,10},{... | collective-permute-start | bytes 786440 | tf_op jit(solution)/shard_map/ppermute | solution.py:62
  16.1 7.6 %collective-permute-start.10 = (bf16[2,32,2048]{2,1,0:T(8,128)(2,1)S(1)}, bf16[2,32,2048]{2,1,0:T(8,128)(2,1)S(1)}, u32[]{:S(2)}, u32[]{:S(2)}) collective-permute-start(bf16[2,32,2048]{2,1,0:T(8,128)(2,1)S(1)} %get-tuple-element.25), channel_id=1, source_target_pairs={{0,12},{4,0},{8,4},{12,8},{1,13},{5,1},{9,5},{13,9},{2,14},{6,2},{... | collective-permute-start | bytes 786440 | tf_op jit(solution)/shard_map/ppermute | solution.py:66
  17.8 8.9 %collective-permute-start.1 = (bf16[2,32,2048]{2,1,0:T(8,128)(2,1)S(1)}, bf16[2,32,2048]{2,1,0:T(8,128)(2,1)S(1)}, u32[]{:S(2)}, u32[]{:S(2)}) collective-permute-start(bf16[2,32,2048]{2,1,0:T(8,128)(2,1)S(1)} %get-tuple-element.26), channel_id=1, source_target_pairs={{0,1},{1,2},{2,3},{3,0},{4,5},{5,6},{6,7},{7,4},{8,9},{9,10},{10,1... | collective-permute-start | bytes 786440 | tf_op jit(solution)/shard_map/ppermute | solution.py:62
  19.4 8.9 %collective-permute-start.2 = (bf16[2,32,2048]{2,1,0:T(8,128)(2,1)S(1)}, bf16[2,32,2048]{2,1,0:T(8,128)(2,1)S(1)}, u32[]{:S(2)}, u32[]{:S(2)}) collective-permute-start(bf16[2,32,2048]{2,1,0:T(8,128)(2,1)S(1)} %get-tuple-element.26), channel_id=1, source_target_pairs={{0,3},{1,0},{2,1},{3,2},{4,7},{5,4},{6,5},{7,6},{8,11},{9,8},{10,9... | collective-permute-start | bytes 786440 | tf_op jit(solution)/shard_map/ppermute | solution.py:66
  21.3 15.6 %copy-start.1 = (bf16[4096,512]{1,0:T(8,128)(2,1)S(1)}, bf16[4096,512]{1,0:T(8,128)(2,1)}, u32[]{:S(2)}) copy-start(bf16[4096,512]{1,0:T(8,128)(2,1)} %param.10) | copy-start | bytes 12582916
  23.3 6.9 %collective-permute-start.11 = (bf16[2,32,1024]{2,1,0:T(8,128)(2,1)S(1)}, bf16[2,32,1024]{2,1,0:T(8,128)(2,1)S(1)}, u32[]{:S(2)}, u32[]{:S(2)}) collective-permute-start(bf16[2,32,1024]{2,1,0:T(8,128)(2,1)S(1)} %slice.216), channel_id=1, source_target_pairs={{0,4},{4,8},{8,12},{12,0},{1,5},{5,9},{9,13},{13,1},{2,6},{6,10},{... | collective-permute-start | bytes 393224 | tf_op jit(solution)/shard_map/ppermute | solution.py:69
  23.6 6.6 %collective-permute-start.12 = (bf16[2,32,1024]{2,1,0:T(8,128)(2,1)S(1)}, bf16[2,32,1024]{2,1,0:T(8,128)(2,1)S(1)}, u32[]{:S(2)}, u32[]{:S(2)}) collective-permute-start(bf16[2,32,1024]{2,1,0:T(8,128)(2,1)S(1)} %slice.217), channel_id=1, source_target_pairs={{0,12},{4,0},{8,4},{12,8},{1,13},{5,1},{9,5},{13,9},{2,14},{6,2},{... | collective-permute-start | bytes 393224 | tf_op jit(solution)/shard_map/ppermute | solution.py:70
  26.7 6.2 %collective-permute-start.3 = (bf16[2,32,1024]{2,1,0:T(8,128)(2,1)S(1)}, bf16[2,32,1024]{2,1,0:T(8,128)(2,1)S(1)}, u32[]{:S(2)}, u32[]{:S(2)}) collective-permute-start(bf16[2,32,1024]{2,1,0:T(8,128)(2,1)S(1)} %slice.211), channel_id=1, source_target_pairs={{0,1},{1,2},{2,3},{3,0},{4,5},{5,6},{6,7},{7,4},{8,9},{9,10},{10,1... | collective-permute-start | bytes 393224 | tf_op jit(solution)/shard_map/ppermute | solution.py:69
  28.3 6.4 %collective-permute-start.4 = (bf16[2,32,1024]{2,1,0:T(8,128)(2,1)S(1)}, bf16[2,32,1024]{2,1,0:T(8,128)(2,1)S(1)}, u32[]{:S(2)}, u32[]{:S(2)}) collective-permute-start(bf16[2,32,1024]{2,1,0:T(8,128)(2,1)S(1)} %slice.212), channel_id=1, source_target_pairs={{0,3},{1,0},{2,1},{3,2},{4,7},{5,4},{6,5},{7,6},{8,11},{9,8},{10,9... | collective-permute-start | bytes 393224 | tf_op jit(solution)/shard_map/ppermute | solution.py:70
  30.2 7.4 %copy-start.4 = (bf16[4096,64]{0,1:T(8,128)(2,1)S(1)}, bf16[4096,64]{0,1:T(8,128)(2,1)}, u32[]{:S(2)}) copy-start(bf16[4096,64]{0,1:T(8,128)(2,1)} %param.11) | copy-start | bytes 1572868
  30.2 23.9 %collective-permute-start.14 = (bf16[4,2,32,2048]{3,2,1,0:T(8,128)(2,1)S(1)}, bf16[4,2,32,2048]{3,2,1,0:T(8,128)(2,1)S(1)}, u32[]{:S(2)}, u32[]{:S(2)}) collective-permute-start(bf16[4,2,32,2048]{3,2,1,0:T(8,128)(2,1)S(1)} %fusion.63), channel_id=1, source_target_pairs={{0,3},{1,0},{2,1},{3,2},{4,7},{5,4},{6,5},{7,6},{8,11},{9,8},{10,9... | collective-permute-start | bytes 3145736 | tf_op jit(solution)/shard_map/ppermute | solution.py:80
  32.6 25.1 %collective-permute-start.13 = (bf16[4,2,32,2048]{3,2,1,0:T(8,128)(2,1)S(1)}, bf16[4,2,32,2048]{3,2,1,0:T(8,128)(2,1)S(1)}, u32[]{:S(2)}, u32[]{:S(2)}) collective-permute-start(bf16[4,2,32,2048]{3,2,1,0:T(8,128)(2,1)S(1)} %fusion.63), channel_id=1, source_target_pairs={{0,1},{1,2},{2,3},{3,0},{4,5},{5,6},{6,7},{7,4},{8,9},{9,10},{10,1... | collective-permute-start | bytes 3145736 | tf_op jit(solution)/shard_map/ppermute | solution.py:79
  34.8 23.0 %collective-permute-start.6 = (bf16[4,2,32,2048]{3,2,1,0:T(8,128)(2,1)S(1)}, bf16[4,2,32,2048]{3,2,1,0:T(8,128)(2,1)S(1)}, u32[]{:S(2)}, u32[]{:S(2)}) collective-permute-start(bf16[4,2,32,2048]{3,2,1,0:T(8,128)(2,1)S(1)} %fusion.62), channel_id=1, source_target_pairs={{0,12},{4,0},{8,4},{12,8},{1,13},{5,1},{9,5},{13,9},{2,14},{6,2},{... | collective-permute-start | bytes 3145736 | tf_op jit(solution)/shard_map/ppermute | solution.py:80
  36.1 23.9 %collective-permute-start.5 = (bf16[4,2,32,2048]{3,2,1,0:T(8,128)(2,1)S(1)}, bf16[4,2,32,2048]{3,2,1,0:T(8,128)(2,1)S(1)}, u32[]{:S(2)}, u32[]{:S(2)}) collective-permute-start(bf16[4,2,32,2048]{3,2,1,0:T(8,128)(2,1)S(1)} %fusion.62), channel_id=1, source_target_pairs={{0,4},{4,8},{8,12},{12,0},{1,5},{5,9},{9,13},{13,1},{2,6},{6,10},{... | collective-permute-start | bytes 3145736 | tf_op jit(solution)/shard_map/ppermute | solution.py:79
  54.2 17.1 %collective-permute-start.16 = (bf16[4,2,32,1024]{3,2,1,0:T(8,128)(2,1)S(1)}, bf16[4,2,32,1024]{3,2,1,0:T(8,128)(2,1)S(1)}, u32[]{:S(2)}, u32[]{:S(2)}) collective-permute-start(bf16[4,2,32,1024]{3,2,1,0:T(8,128)(2,1)S(1)} %slice.219), channel_id=1, source_target_pairs={{0,3},{1,0},{2,1},{3,2},{4,7},{5,4},{6,5},{7,6},{8,11},{9,8},{10,9... | collective-permute-start | bytes 1572872 | tf_op jit(solution)/shard_map/ppermute | solution.py:86
  57.7 12.4 %collective-permute-start.15 = (bf16[4,2,32,1024]{3,2,1,0:T(8,128)(2,1)S(1)}, bf16[4,2,32,1024]{3,2,1,0:T(8,128)(2,1)S(1)}, u32[]{:S(2)}, u32[]{:S(2)}) collective-permute-start(bf16[4,2,32,1024]{3,2,1,0:T(8,128)(2,1)S(1)} %slice.218), channel_id=1, source_target_pairs={{0,1},{1,2},{2,3},{3,0},{4,5},{5,6},{6,7},{7,4},{8,9},{9,10},{10,1... | collective-permute-start | bytes 1572872 | tf_op jit(solution)/shard_map/ppermute | solution.py:85
  57.9 14.6 %collective-permute-start.8 = (bf16[4,2,32,1024]{3,2,1,0:T(8,128)(2,1)S(1)}, bf16[4,2,32,1024]{3,2,1,0:T(8,128)(2,1)S(1)}, u32[]{:S(2)}, u32[]{:S(2)}) collective-permute-start(bf16[4,2,32,1024]{3,2,1,0:T(8,128)(2,1)S(1)} %slice.214), channel_id=1, source_target_pairs={{0,12},{4,0},{8,4},{12,8},{1,13},{5,1},{9,5},{13,9},{2,14},{6,2},{... | collective-permute-start | bytes 1572872 | tf_op jit(solution)/shard_map/ppermute | solution.py:86
  60.0 11.2 %collective-permute-start.7 = (bf16[4,2,32,1024]{3,2,1,0:T(8,128)(2,1)S(1)}, bf16[4,2,32,1024]{3,2,1,0:T(8,128)(2,1)S(1)}, u32[]{:S(2)}, u32[]{:S(2)}) collective-permute-start(bf16[4,2,32,1024]{3,2,1,0:T(8,128)(2,1)S(1)} %slice.213), channel_id=1, source_target_pairs={{0,4},{4,8},{8,12},{12,0},{1,5},{5,9},{9,13},{13,1},{2,6},{6,10},{... | collective-permute-start | bytes 1572872 | tf_op jit(solution)/shard_map/ppermute | solution.py:85
  75.4 7.0 %copy-start = (s32[8]{0:T(128)S(1)}, s32[8]{0:T(128)}, u32[]{:S(2)}) copy-start(s32[8]{0:T(128)} %param.14) | copy-start | bytes 100
  75.4 27.8 %all-to-all-start = ((bf16[128,8,576]{2,1,0:T(8,128)(2,1)}), bf16[128,8,576]{2,1,0:T(8,128)(2,1)S(1)}, u32[]{:S(2)}, u32[]{:S(2)}) async-start(bf16[128,8,576]{2,1,0:T(8,128)(2,1)} %bitcast.31), calls=%async_computation | async-start | bytes 2621440 | tf_op jit(solution)/shard_map/all_to_all | solution.py:165
  104.8 4.1 %copy-start.2 = (bf16[8,256,8,128]{3,2,1,0:T(8,128)(2,1)S(1)}, bf16[8,256,8,128]{3,2,1,0:T(8,128)(2,1)}, u32[]{:S(2)}) copy-start(bf16[8,256,8,128]{3,2,1,0:T(8,128)(2,1)} %param.13) | copy-start | bytes 12582916
  111.4 23.2 %all-to-all-start.1 = ((bf16[128,8,512]{2,1,0:T(8,128)(2,1)}), bf16[128,8,512]{2,1,0:T(8,128)(2,1)S(1)}, u32[]{:S(2)}, u32[]{:S(2)}) async-start(bf16[128,8,512]{2,1,0:T(8,128)(2,1)} %bitcast.43), calls=%async_computation.1 | async-start | bytes 2097152 | tf_op jit(solution)/shard_map/all_to_all | solution.py:174
  134.6 4.8 %copy-start.3 = (bf16[512,4096]{1,0:T(8,128)(2,1)S(1)}, bf16[512,4096]{1,0:T(8,128)(2,1)}, u32[]{:S(2)}) copy-start(bf16[512,4096]{1,0:T(8,128)(2,1)} %param.15) | copy-start | bytes 12582916
  141.7 19.0 %collective-permute-start.26 = (bf16[2,4,32,1024]{3,2,1,0:T(8,128)(2,1)S(1)}, bf16[2,4,32,1024]{3,2,1,0:T(8,128)(2,1)S(1)}, u32[]{:S(2)}, u32[]{:S(2)}) collective-permute-start(bf16[2,4,32,1024]{3,2,1,0:T(8,128)(2,1)S(1)} %get-tuple-element.19), channel_id=1, source_target_pairs={{0,12},{4,0},{8,4},{12,8},{1,13},{5,1},{9,5},{13,9},{2,14},{6,2},{... | collective-permute-start | bytes 1572872 | tf_op jit(solution)/shard_map/ppermute | solution.py:109
  144.3 18.6 %collective-permute-start.28 = (bf16[2,4,32,1024]{3,2,1,0:T(8,128)(2,1)S(1)}, bf16[2,4,32,1024]{3,2,1,0:T(8,128)(2,1)S(1)}, u32[]{:S(2)}, u32[]{:S(2)}) collective-permute-start(bf16[2,4,32,1024]{3,2,1,0:T(8,128)(2,1)S(1)} %get-tuple-element.20), channel_id=1, source_target_pairs={{0,4},{4,8},{8,12},{12,0},{1,5},{5,9},{9,13},{13,1},{2,6},{6,10},{... | collective-permute-start | bytes 1572872 | tf_op jit(solution)/shard_map/ppermute | solution.py:110
  144.4 12.9 %collective-permute-start.17 = (bf16[2,4,32,1024]{3,2,1,0:T(8,128)(2,1)S(1)}, bf16[2,4,32,1024]{3,2,1,0:T(8,128)(2,1)S(1)}, u32[]{:S(2)}, u32[]{:S(2)}) collective-permute-start(bf16[2,4,32,1024]{3,2,1,0:T(8,128)(2,1)S(1)} %get-tuple-element.10), channel_id=1, source_target_pairs={{0,3},{1,0},{2,1},{3,2},{4,7},{5,4},{6,5},{7,6},{8,11},{9,8},{10,9... | collective-permute-start | bytes 1572872 | tf_op jit(solution)/shard_map/ppermute | solution.py:109
  146.4 13.9 %collective-permute-start.19 = (bf16[2,4,32,1024]{3,2,1,0:T(8,128)(2,1)S(1)}, bf16[2,4,32,1024]{3,2,1,0:T(8,128)(2,1)S(1)}, u32[]{:S(2)}, u32[]{:S(2)}) collective-permute-start(bf16[2,4,32,1024]{3,2,1,0:T(8,128)(2,1)S(1)} %get-tuple-element.11), channel_id=1, source_target_pairs={{0,1},{1,2},{2,3},{3,0},{4,5},{5,6},{6,7},{7,4},{8,9},{9,10},{10,1... | collective-permute-start | bytes 1572872 | tf_op jit(solution)/shard_map/ppermute | solution.py:110
  157.5 23.3 %collective-permute-start.18 = (bf16[2,4,32,2048]{3,2,1,0:T(8,128)(2,1)S(1)}, bf16[2,4,32,2048]{3,2,1,0:T(8,128)(2,1)S(1)}, u32[]{:S(2)}, u32[]{:S(2)}) collective-permute-start(bf16[2,4,32,2048]{3,2,1,0:T(8,128)(2,1)S(1)} %pad_maximum_fusion), channel_id=1, source_target_pairs={{0,3},{1,0},{2,1},{3,2},{4,7},{5,4},{6,5},{7,6},{8,11},{9,8},{10,9... | collective-permute-start | bytes 3145736 | tf_op jit(solution)/shard_map/ppermute | solution.py:115
  160.5 23.8 %collective-permute-start.20 = (bf16[2,4,32,2048]{3,2,1,0:T(8,128)(2,1)S(1)}, bf16[2,4,32,2048]{3,2,1,0:T(8,128)(2,1)S(1)}, u32[]{:S(2)}, u32[]{:S(2)}) collective-permute-start(bf16[2,4,32,2048]{3,2,1,0:T(8,128)(2,1)S(1)} %pad_maximum_fusion.1), channel_id=1, source_target_pairs={{0,1},{1,2},{2,3},{3,0},{4,5},{5,6},{6,7},{7,4},{8,9},{9,10},{10,1... | collective-permute-start | bytes 3145736 | tf_op jit(solution)/shard_map/ppermute | solution.py:116
  160.8 25.9 %collective-permute-start.27 = (bf16[2,4,32,2048]{3,2,1,0:T(8,128)(2,1)S(1)}, bf16[2,4,32,2048]{3,2,1,0:T(8,128)(2,1)S(1)}, u32[]{:S(2)}, u32[]{:S(2)}) collective-permute-start(bf16[2,4,32,2048]{3,2,1,0:T(8,128)(2,1)S(1)} %pad_maximum_fusion.2), channel_id=1, source_target_pairs={{0,12},{4,0},{8,4},{12,8},{1,13},{5,1},{9,5},{13,9},{2,14},{6,2},{... | collective-permute-start | bytes 3145736 | tf_op jit(solution)/shard_map/ppermute | solution.py:115
  163.1 23.6 %collective-permute-start.29 = (bf16[2,4,32,2048]{3,2,1,0:T(8,128)(2,1)S(1)}, bf16[2,4,32,2048]{3,2,1,0:T(8,128)(2,1)S(1)}, u32[]{:S(2)}, u32[]{:S(2)}) collective-permute-start(bf16[2,4,32,2048]{3,2,1,0:T(8,128)(2,1)S(1)} %pad_maximum_fusion.3), channel_id=1, source_target_pairs={{0,4},{4,8},{8,12},{12,0},{1,5},{5,9},{9,13},{13,1},{2,6},{6,10},{... | collective-permute-start | bytes 3145736 | tf_op jit(solution)/shard_map/ppermute | solution.py:116
  184.6 8.6 %collective-permute-start.21 = (bf16[2,32,1024]{2,1,0:T(8,128)(2,1)S(1)}, bf16[2,32,1024]{2,1,0:T(8,128)(2,1)S(1)}, u32[]{:S(2)}, u32[]{:S(2)}) collective-permute-start(bf16[2,32,1024]{2,1,0:T(8,128)(2,1)S(1)} %get-tuple-element.29), channel_id=1, source_target_pairs={{0,12},{4,0},{8,4},{12,8},{1,13},{5,1},{9,5},{13,9},{2,14},{6,2},{... | collective-permute-start | bytes 393224 | tf_op jit(solution)/shard_map/ppermute | solution.py:109
  186.1 6.9 %collective-permute-start.23 = (bf16[2,32,1024]{2,1,0:T(8,128)(2,1)S(1)}, bf16[2,32,1024]{2,1,0:T(8,128)(2,1)S(1)}, u32[]{:S(2)}, u32[]{:S(2)}) collective-permute-start(bf16[2,32,1024]{2,1,0:T(8,128)(2,1)S(1)} %get-tuple-element.30), channel_id=1, source_target_pairs={{0,4},{4,8},{8,12},{12,0},{1,5},{5,9},{9,13},{13,1},{2,6},{6,10},{... | collective-permute-start | bytes 393224 | tf_op jit(solution)/shard_map/ppermute | solution.py:110
  187.0 11.4 %collective-permute-start.30 = (bf16[2,32,1024]{2,1,0:T(8,128)(2,1)S(1)}, bf16[2,32,1024]{2,1,0:T(8,128)(2,1)S(1)}, u32[]{:S(2)}, u32[]{:S(2)}) collective-permute-start(bf16[2,32,1024]{2,1,0:T(8,128)(2,1)S(1)} %get-tuple-element.35), channel_id=1, source_target_pairs={{0,3},{1,0},{2,1},{3,2},{4,7},{5,4},{6,5},{7,6},{8,11},{9,8},{10,9... | collective-permute-start | bytes 393224 | tf_op jit(solution)/shard_map/ppermute | solution.py:109
  190.7 7.6 %collective-permute-start.32 = (bf16[2,32,1024]{2,1,0:T(8,128)(2,1)S(1)}, bf16[2,32,1024]{2,1,0:T(8,128)(2,1)S(1)}, u32[]{:S(2)}, u32[]{:S(2)}) collective-permute-start(bf16[2,32,1024]{2,1,0:T(8,128)(2,1)S(1)} %get-tuple-element.36), channel_id=1, source_target_pairs={{0,1},{1,2},{2,3},{3,0},{4,5},{5,6},{6,7},{7,4},{8,9},{9,10},{10,1... | collective-permute-start | bytes 393224 | tf_op jit(solution)/shard_map/ppermute | solution.py:110
  193.1 8.7 %collective-permute-start.24 = (bf16[2,32,2048]{2,1,0:T(8,128)(2,1)S(1)}, bf16[2,32,2048]{2,1,0:T(8,128)(2,1)S(1)}, u32[]{:S(2)}, u32[]{:S(2)}) collective-permute-start(bf16[2,32,2048]{2,1,0:T(8,128)(2,1)S(1)} %pad_maximum_fusion.6), channel_id=1, source_target_pairs={{0,4},{4,8},{8,12},{12,0},{1,5},{5,9},{9,13},{13,1},{2,6},{6,10},{... | collective-permute-start | bytes 786440 | tf_op jit(solution)/shard_map/ppermute | solution.py:116
  193.3 8.5 %collective-permute-start.22 = (bf16[2,32,2048]{2,1,0:T(8,128)(2,1)S(1)}, bf16[2,32,2048]{2,1,0:T(8,128)(2,1)S(1)}, u32[]{:S(2)}, u32[]{:S(2)}) collective-permute-start(bf16[2,32,2048]{2,1,0:T(8,128)(2,1)S(1)} %pad_maximum_fusion.5), channel_id=1, source_target_pairs={{0,12},{4,0},{8,4},{12,8},{1,13},{5,1},{9,5},{13,9},{2,14},{6,2},{... | collective-permute-start | bytes 786440 | tf_op jit(solution)/shard_map/ppermute | solution.py:115
  198.4 7.7 %collective-permute-start.33 = (bf16[2,32,2048]{2,1,0:T(8,128)(2,1)S(1)}, bf16[2,32,2048]{2,1,0:T(8,128)(2,1)S(1)}, u32[]{:S(2)}, u32[]{:S(2)}) collective-permute-start(bf16[2,32,2048]{2,1,0:T(8,128)(2,1)S(1)} %pad_maximum_fusion.8), channel_id=1, source_target_pairs={{0,1},{1,2},{2,3},{3,0},{4,5},{5,6},{6,7},{7,4},{8,9},{9,10},{10,1... | collective-permute-start | bytes 786440 | tf_op jit(solution)/shard_map/ppermute | solution.py:116
  198.5 7.5 %collective-permute-start.31 = (bf16[2,32,2048]{2,1,0:T(8,128)(2,1)S(1)}, bf16[2,32,2048]{2,1,0:T(8,128)(2,1)S(1)}, u32[]{:S(2)}, u32[]{:S(2)}) collective-permute-start(bf16[2,32,2048]{2,1,0:T(8,128)(2,1)S(1)} %pad_maximum_fusion.7), channel_id=1, source_target_pairs={{0,3},{1,0},{2,1},{3,2},{4,7},{5,4},{6,5},{7,6},{8,11},{9,8},{10,9... | collective-permute-start | bytes 786440 | tf_op jit(solution)/shard_map/ppermute | solution.py:115
  206.1 6.6 %collective-permute-start.34 = (bf16[32,2048]{1,0:T(8,128)(2,1)S(1)}, bf16[32,2048]{1,0:T(8,128)(2,1)S(1)}, u32[]{:S(2)}, u32[]{:S(2)}) collective-permute-start(bf16[32,2048]{1,0:T(8,128)(2,1)S(1)} %get-tuple-element.49), channel_id=1, source_target_pairs={{0,16},{16,0},{1,17},{17,1},{2,18},{18,2},{3,19},{19,3},{4,20},{20... | collective-permute-start | bytes 393224 | tf_op jit(solution)/shard_map/ppermute | solution.py:106
  209.5 6.5 %collective-permute-start.25 = (bf16[32,2048]{1,0:T(8,128)(2,1)S(1)}, bf16[32,2048]{1,0:T(8,128)(2,1)S(1)}, u32[]{:S(2)}, u32[]{:S(2)}) collective-permute-start(bf16[32,2048]{1,0:T(8,128)(2,1)S(1)} %get-tuple-element.50), channel_id=1, source_target_pairs={{0,16},{16,0},{1,17},{17,1},{2,18},{18,2},{3,19},{19,3},{4,20},{20... | collective-permute-start | bytes 393224 | tf_op jit(solution)/shard_map/ppermute | solution.py:106

commit v3 on v2

--- a/solution.py
+++ b/solution.py
@@ -184,11 +184,11 @@
 
     first = ring_reduce_scatter(partial_out(2, 0, cols // 2), "y", 4)
     second = ring_reduce_scatter(partial_out(1, cols // 2, cols), "x", 4)
-    first = ring_reduce_scatter(blocks_of(first, 1), "x", 4)
-    second = ring_reduce_scatter(blocks_of(second, 1), "y", 4)
-    first = ring_reduce_scatter(blocks_of(first, 0), "zh", 2)
-    second = ring_reduce_scatter(blocks_of(second, 0), "zh", 2)
-    return jnp.concatenate([first, second], axis=-1)
+    first = lax.all_to_all(first.reshape((8,) + first.shape[2:]), ("zh", "x"), 0, 0, tiled=True)
+    second = lax.all_to_all(second.reshape((8,) + second.shape[2:]), ("zh", "y"), 0, 0, tiled=True)
+    first = first.astype(jnp.float32).sum(axis=0)
+    second = second.astype(jnp.float32).sum(axis=0)
+    return jnp.concatenate([first, second], axis=-1).astype(jnp.bfloat16)
 
 
 def solution(mesh):

time: 217 us -> 227 us (1.046)
  waiting for transfers between devices: 113 us -> 124 us
  starting transfers between devices: 66.5 us -> 59.3 us
  other arithmetic: 9.38 us -> 13.8 us
    all_to_all x0 -> x2, waiting for transfers between devices: none -> 26.3 us  [the longest x1 16.5 us: shards(): lax.all_to_all(second.reshape((8,) + second.shape[2:]), ('zh', 'y'), 0, 0...]
    all_to_all x0 -> x2, starting transfers between devices: none -> 8.98 us  [the longest x1 5.43 us: shards(): lax.all_to_all(first.reshape((8,) + first.shape[2:]), ('zh', 'x'), 0, 0,...]
    ppermute x4 -> x2, starting transfers between devices: 11.6 us -> 5.02 us  [ring_reduce_scatter(): got_right = lax.ppermute(to_left, axis, bwd)]
    ppermute x2 -> x0, waiting for transfers between devices: 6.22 us -> none  [ring_reduce_scatter(): return take(idx) + lax.ppermute(take(idx + 1), axis, fwd)]
    ppermute x4 -> x2, starting transfers between devices: 9.87 us -> 4.65 us  [ring_reduce_scatter(): from_right = lax.ppermute(opposite[..., :half], axis, bwd)]
    ppermute x4 -> x2, waiting for transfers between devices: 7.82 us -> 3.66 us  [ring_reduce_scatter(): got_left = lax.ppermute(to_right, axis, fwd)]
    ppermute x4 -> x2, waiting for transfers between devices: 4.09 us -> 0.01 us  [ring_reduce_scatter(): from_left = lax.ppermute(opposite[..., half:], axis, fwd)]
    ppermute x2 -> x0, starting transfers between devices: 3.61 us -> none  [ring_reduce_scatter(): return take(idx) + lax.ppermute(take(idx + 1), axis, fwd)]
  transfers between devices with their start and end apart: 37 -> 29, of which waited for: 17 -> 14; matrix products, arithmetic and copies ran while one was open for 6% -> 9% of each run, Pallas kernels for 0% -> 0%
where the time goes in v3:
time: 227 us; the launch traced here: 226 us
  waiting for transfers between devices  124 us (55%)
  starting transfers between devices  59.3 us (26%)
  matrix products  24.8 us (11%)
  other arithmetic  13.8 us (6%)
  local copies, waits for them, and re-layouts  3.47 us (2%)
    all_to_all x1, waiting for transfers between devices, shards(): lax.all_to_all(projected.astype(jnp.bfloat16), ALL, split_axis=0, concat_...  20.6 us
    all_to_all x1, waiting for transfers between devices, shards(): lax.all_to_all(sent, ALL, split_axis=0, concat_axis=0, tiled=True)  17.6 us
    all_to_all x1, waiting for transfers between devices, shards(): lax.all_to_all(second.reshape((8,) + second.shape[2:]), ('zh', 'y'), 0, 0...  16.5 us
    ppermute x2, waiting for transfers between devices, ring_reduce_scatter(): got_right = lax.ppermute(to_left, axis, bwd)  15.9 us
    ppermute x2, waiting for transfers between devices, ring_all_gather_apply(): from_right = lax.ppermute(blk, axis, bwd)  14.3 us
    dot_general x8, matrix products, partial_out(): jnp.dot(lax.dynamic_index_in_dim(by_row, k, dim, keepdims=False), w_out[:...  10.8 us
    all_to_all x1, waiting for transfers between devices, shards(): lax.all_to_all(first.reshape((8,) + first.shape[2:]), ('zh', 'x'), 0, 0,...  9.78 us
    ppermute x2, waiting for transfers between devices, ring_reduce_scatter(): from_right = lax.ppermute(opposite[..., :half], axis, bwd)  9.28 us
  transfers between devices with their start and end apart: 29, of which 14 were waited for; matrix products, arithmetic and copies ran while one was open for 9% of the time, Pallas kernels for 0%

profile of v3, /device:TPU:0, one launch (start us, length us, event | category | flops | bytes accessed | tf_op | source)
XLA Modules:
  0.0 226.2 jit_solution(4338683126452554792)
XLA Ops:
  0.0 1.5 fusion.4
  1.5 0.8 convert_element_type.94
  2.3 1.5 fusion.6
  3.9 4.2 %collective-permute-start = (bf16[32,4096]{1,0:T(8,128)(2,1)S(1)}, bf16[32,4096]{1,0:T(8,128)(2,1)S(1)}, u32[]{:S(2)}, u32[]{:S(2)}) collective-permute-start(bf16[32,4096]{1,0:T(8,128)(2,1)S(1)} %constant_dynamic-slice_fusion), channel_id=1, source_target_pairs={{0,80},{1,81},{2,82},{3,83},{4,84},{5,85},{6,86},{7,87},{8,88},{9,... | collective-permute-start | bytes 786440 | tf_op jit(solution)/shard_map/ppermute | solution.py:140
  8.2 6.2 %collective-permute-done = bf16[32,4096]{1,0:T(8,128)(2,1)S(1)} collective-permute-done((bf16[32,4096]{1,0:T(8,128)(2,1)S(1)}, bf16[32,4096]{1,0:T(8,128)(2,1)S(1)}, u32[]{:S(2)}, u32[]{:S(2)}) %collective-permute-start) | collective-permute-done | bytes 262176 | tf_op jit(solution)/shard_map/ppermute | solution.py:140
  14.5 1.6 collective-permute-start.9
  16.1 1.7 collective-permute-start.10
  17.8 1.6 collective-permute-start.1
  19.4 1.7 collective-permute-start.2
  21.4 1.9 collective-permute-done.9
  23.6 3.0 %collective-permute-start.12 = (bf16[2,32,1024]{2,1,0:T(8,128)(2,1)S(1)}, bf16[2,32,1024]{2,1,0:T(8,128)(2,1)S(1)}, u32[]{:S(2)}, u32[]{:S(2)}) collective-permute-start(bf16[2,32,1024]{2,1,0:T(8,128)(2,1)S(1)} %slice.169), channel_id=1, source_target_pairs={{0,12},{4,0},{8,4},{12,8},{1,13},{5,1},{9,5},{13,9},{2,14},{6,2},{... | collective-permute-start | bytes 393224 | tf_op jit(solution)/shard_map/ppermute | solution.py:70
  26.7 1.6 collective-permute-start.3
  28.3 1.7 collective-permute-start.4
  30.2 2.4 %collective-permute-start.14 = (bf16[4,2,32,2048]{3,2,1,0:T(8,128)(2,1)S(1)}, bf16[4,2,32,2048]{3,2,1,0:T(8,128)(2,1)S(1)}, u32[]{:S(2)}, u32[]{:S(2)}) collective-permute-start(bf16[4,2,32,2048]{3,2,1,0:T(8,128)(2,1)S(1)} %fusion.63), channel_id=1, source_target_pairs={{0,3},{1,0},{2,1},{3,2},{4,7},{5,4},{6,5},{7,6},{8,11},{9,8},{10,9... | collective-permute-start | bytes 3145736 | tf_op jit(solution)/shard_map/ppermute | solution.py:80
  32.9 1.9 collective-permute-done.4
  34.8 1.3 collective-permute-start.6
  36.1 0.8 collective-permute-start.5
  36.9 0.7 fusion.29
  38.8 0.7 fusion.21
  39.9 14.3 %collective-permute-done.14 = bf16[4,2,32,2048]{3,2,1,0:T(8,128)(2,1)S(1)} collective-permute-done((bf16[4,2,32,2048]{3,2,1,0:T(8,128)(2,1)S(1)}, bf16[4,2,32,2048]{3,2,1,0:T(8,128)(2,1)S(1)}, u32[]{:S(2)}, u32[]{:S(2)}) %collective-permute-start.14) | collective-permute-done | bytes 1048608 | tf_op jit(solution)/shard_map/ppermute | solution.py:80
  54.2 3.5 %collective-permute-start.16 = (bf16[4,2,32,1024]{3,2,1,0:T(8,128)(2,1)S(1)}, bf16[4,2,32,1024]{3,2,1,0:T(8,128)(2,1)S(1)}, u32[]{:S(2)}, u32[]{:S(2)}) collective-permute-start(bf16[4,2,32,1024]{3,2,1,0:T(8,128)(2,1)S(1)} %slice.171), channel_id=1, source_target_pairs={{0,3},{1,0},{2,1},{3,2},{4,7},{5,4},{6,5},{7,6},{8,11},{9,8},{10,9... | collective-permute-start | bytes 1572872 | tf_op jit(solution)/shard_map/ppermute | solution.py:86
  57.9 2.1 collective-permute-start.8
  60.3 0.4 fusion.74
  60.7 0.7 fusion.17
  61.8 0.7 fusion.19
  62.6 0.4 fusion.82
  63.0 0.7 fusion.25
  63.7 0.7 fusion.27
  64.4 0.4 fusion.84
  65.1 5.0 %collective-permute-done.15 = bf16[4,2,32,1024]{3,2,1,0:T(8,128)(2,1)S(1)} collective-permute-done((bf16[4,2,32,1024]{3,2,1,0:T(8,128)(2,1)S(1)}, bf16[4,2,32,1024]{3,2,1,0:T(8,128)(2,1)S(1)}, u32[]{:S(2)}, u32[]{:S(2)}) %collective-permute-start.15) | collective-permute-done | bytes 524320 | tf_op jit(solution)/shard_map/ppermute | solution.py:85
  70.2 1.1 collective-permute-done.7
  71.8 0.7 fusion.15
  73.0 0.7 fusion.23
  73.8 1.5 add_convert_fusion
  75.4 7.0 %all-to-all-start = ((bf16[128,8,576]{2,1,0:T(8,128)(2,1)}), bf16[128,8,576]{2,1,0:T(8,128)(2,1)S(1)}, u32[]{:S(2)}, u32[]{:S(2)}) async-start(bf16[128,8,576]{2,1,0:T(8,128)(2,1)} %bitcast.31), calls=%async_computation | async-start | bytes 2621440 | tf_op jit(solution)/shard_map/all_to_all | solution.py:165
  82.6 20.6 %all-to-all-done = bf16[128,8,576]{2,1,0:T(8,128)(2,1)S(1)} async-done(((bf16[128,8,576]{2,1,0:T(8,128)(2,1)}), bf16[128,8,576]{2,1,0:T(8,128)(2,1)S(1)}, u32[]{:S(2)}, u32[]{:S(2)}) %all-to-all-start) | async-done | bytes 1179680 | tf_op jit(solution)/shard_map/all_to_all | solution.py:165
  104.8 3.7 %fusion.125 = (f32[8,8,16]{2,1,0:T(8,128)S(1)}, f32[8,8,16,256]{3,2,1,0:T(8,128)S(1)}) fusion(bf16[8,256,8,128]{3,2,1,0:T(8,128)(2,1)} %param.12, bf16[8,8,16,64]{3,2,1,0:T(8,128)(2,1)S(1)} %bitcast.197, bf16[8,8,16,64]{3,2,1,0:T(8,128)(2,1)S(1)} %bitcast.195, pred[8,256]{1,0:T(8,128)(4,1)S(1)} %iota_compare_fusion), kind=kOutput, calls=%fused_computation.189 | convolution fusion | flops 68418560 | bytes 5511168 | tf_op jit(solution)/shard_map/rgqd,rtgd->rgqt/dot_general | solution.py:39
  108.9 1.0 fusion.56
  110.3 1.1 broadcast_in_dim.116
  111.3 5.6 %all-to-all-start.1 = ((bf16[128,8,512]{2,1,0:T(8,128)(2,1)}), bf16[128,8,512]{2,1,0:T(8,128)(2,1)S(1)}, u32[]{:S(2)}, u32[]{:S(2)}) async-start(bf16[128,8,512]{2,1,0:T(8,128)(2,1)} %bitcast.43), calls=%async_computation.1 | async-start | bytes 2097152 | tf_op jit(solution)/shard_map/all_to_all | solution.py:174
  116.9 17.6 %all-to-all-done.1 = bf16[128,8,512]{2,1,0:T(8,128)(2,1)S(1)} async-done(((bf16[128,8,512]{2,1,0:T(8,128)(2,1)}), bf16[128,8,512]{2,1,0:T(8,128)(2,1)S(1)}, u32[]{:S(2)}, u32[]{:S(2)}) %all-to-all-start.1) | async-done | bytes 1048608 | tf_op jit(solution)/shard_map/all_to_all | solution.py:174
  134.6 2.5 %convolution_convert_fusion = bf16[2,4,32,2048]{3,2,1,0:T(8,128)(2,1)S(1)} fusion(bf16[512,4096]{1,0:T(8,128)(2,1)} %param.15, bf16[2,4,4,32,512]{4,3,2,1,0:T(8,128)(2,1)S(1)} %bitcast.185, s32[]{:T(128)S(6)} %select_n.145), kind=kOutput, calls=%fused_computation.7 | convolution fusion | flops 537395200 | bytes 3407876 | tf_op jit(solution)/shard_map/dot_general | solution.py:179
  137.0 2.3 %convolution_convert_fusion.1 = bf16[2,4,32,2048]{3,2,1,0:T(8,128)(2,1)S(1)} fusion(bf16[512,4096]{1,0:T(8,128)(2,1)} %param.15, bf16[2,4,4,32,512]{4,3,2,1,0:T(8,128)(2,1)S(1)} %bitcast.186, s32[]{:T(128)S(6)} %select_n.147), kind=kOutput, calls=%fused_computation.8 | convolution fusion | flops 537395200 | bytes 3407876 | tf_op jit(solution)/shard_map/dot_general | solution.py:179
  139.4 0.7 convolution_convert_fusion.2
  140.1 0.7 convolution_convert_fusion.5
  141.0 2.6 %collective-permute-start.21 = (bf16[2,4,32,1024]{3,2,1,0:T(8,128)(2,1)S(1)}, bf16[2,4,32,1024]{3,2,1,0:T(8,128)(2,1)S(1)}, u32[]{:S(2)}, u32[]{:S(2)}) collective-permute-start(bf16[2,4,32,1024]{3,2,1,0:T(8,128)(2,1)S(1)} %get-tuple-element.13), channel_id=1, source_target_pairs={{0,12},{4,0},{8,4},{12,8},{1,13},{5,1},{9,5},{13,9},{2,14},{6,2},{... | collective-permute-start | bytes 1572872 | tf_op jit(solution)/shard_map/ppermute | solution.py:109
  143.7 2.0 collective-permute-start.17
  145.8 0.7 convolution_convert_fusion.4
  146.5 0.7 convolution_convert_fusion.6
  147.3 9.3 %collective-permute-done.17 = bf16[2,4,32,1024]{3,2,1,0:T(8,128)(2,1)S(1)} collective-permute-done((bf16[2,4,32,1024]{3,2,1,0:T(8,128)(2,1)S(1)}, bf16[2,4,32,1024]{3,2,1,0:T(8,128)(2,1)S(1)}, u32[]{:S(2)}, u32[]{:S(2)}) %collective-permute-start.17) | collective-permute-done | bytes 524320 | tf_op jit(solution)/shard_map/ppermute | solution.py:109
  156.7 2.9 %collective-permute-start.18 = (bf16[2,4,32,2048]{3,2,1,0:T(8,128)(2,1)S(1)}, bf16[2,4,32,2048]{3,2,1,0:T(8,128)(2,1)S(1)}, u32[]{:S(2)}, u32[]{:S(2)}) collective-permute-start(bf16[2,4,32,2048]{3,2,1,0:T(8,128)(2,1)S(1)} %pad_maximum_fusion), channel_id=1, source_target_pairs={{0,3},{1,0},{2,1},{3,2},{4,7},{5,4},{6,5},{7,6},{8,11},{9,8},{10,9... | collective-permute-start | bytes 3145736 | tf_op jit(solution)/shard_map/ppermute | solution.py:115
  160.1 2.1 collective-permute-start.22
  162.3 1.1 pad_maximum_fusion.3
  163.4 0.8 convolution_convert_fusion.7
  164.1 15.9 %collective-permute-done.18 = bf16[2,4,32,2048]{3,2,1,0:T(8,128)(2,1)S(1)} collective-permute-done((bf16[2,4,32,2048]{3,2,1,0:T(8,128)(2,1)S(1)}, bf16[2,4,32,2048]{3,2,1,0:T(8,128)(2,1)S(1)}, u32[]{:S(2)}, u32[]{:S(2)}) %collective-permute-start.18) | collective-permute-done | bytes 1048608 | tf_op jit(solution)/shard_map/ppermute | solution.py:115
  180.0 3.7 %collective-permute-done.20 = bf16[2,4,32,2048]{3,2,1,0:T(8,128)(2,1)S(1)} collective-permute-done((bf16[2,4,32,2048]{3,2,1,0:T(8,128)(2,1)S(1)}, bf16[2,4,32,2048]{3,2,1,0:T(8,128)(2,1)S(1)}, u32[]{:S(2)}, u32[]{:S(2)}) %collective-permute-start.20) | collective-permute-done | bytes 1048608 | tf_op jit(solution)/shard_map/ppermute | solution.py:116
  183.7 1.1 add_add_fusion.1
  184.8 5.4 %all-to-all-start.2 = ((bf16[8,32,2048]{2,1,0:T(8,128)(2,1)}), bf16[8,32,2048]{2,1,0:T(8,128)(2,1)S(1)}, u32[]{:S(2)}, u32[]{:S(2)}) async-start(bf16[8,32,2048]{2,1,0:T(8,128)(2,1)} %bitcast.52), calls=%async_computation.2 | async-start | bytes 2097152 | tf_op jit(solution)/shard_map/all_to_all | solution.py:187
  190.2 2.3 %convolution_convert_fusion.3 = bf16[2,4,32,2048]{3,2,1,0:T(8,128)(2,1)S(1)} fusion(bf16[512,4096]{1,0:T(8,128)(2,1)} %param.15, bf16[2,4,4,32,512]{4,3,2,1,0:T(8,128)(2,1)S(1)} %bitcast.192, s32[]{:T(128)S(6)} %select_n.152), kind=kOutput, calls=%fused_computation.10 | convolution fusion | flops 537395200 | bytes 3407876 | tf_op jit(solution)/shard_map/dot_general | solution.py:179
  192.6 2.7 %add_add_fusion = bf16[2,4,32,2048]{3,2,1,0:T(8,128)(2,1)} fusion(bf16[2,4,32,2048]{3,2,1,0:T(8,128)(2,1)} %collective-permute-done.24, bf16[2,4,32,2048]{3,2,1,0:T(8,128)(2,1)S(1)} %convolution_convert_fusion.3, bf16[2,4,32,2048]{3,2,1,0:T(8,128)(2,1)} %collective-permute-done.22), kind=kLoop, calls=%fused_computation.66 | loop fusion | flops 1048576 | bytes 4194304 | tf_op jit(solution)/shard_map/add | solution.py:117
  195.2 9.8 %all-to-all-done.2 = bf16[8,32,2048]{2,1,0:T(8,128)(2,1)S(1)} async-done(((bf16[8,32,2048]{2,1,0:T(8,128)(2,1)}), bf16[8,32,2048]{2,1,0:T(8,128)(2,1)S(1)}, u32[]{:S(2)}, u32[]{:S(2)}) %all-to-all-start.2) | async-done | bytes 1048608 | tf_op jit(solution)/shard_map/all_to_all | solution.py:187
  205.0 3.6 %all-to-all-start.3 = ((bf16[8,32,2048]{2,1,0:T(8,128)(2,1)}), bf16[8,32,2048]{2,1,0:T(8,128)(2,1)S(1)}, u32[]{:S(2)}, u32[]{:S(2)}) async-start(bf16[8,32,2048]{2,1,0:T(8,128)(2,1)} %bitcast.60), calls=%async_computation.3 | async-start | bytes 2097152 | tf_op jit(solution)/shard_map/all_to_all | solution.py:188
  208.8 16.5 %all-to-all-done.3 = bf16[8,32,2048]{2,1,0:T(8,128)(2,1)S(1)} async-done(((bf16[8,32,2048]{2,1,0:T(8,128)(2,1)}), bf16[8,32,2048]{2,1,0:T(8,128)(2,1)S(1)}, u32[]{:S(2)}, u32[]{:S(2)}) %all-to-all-start.3) | async-done | bytes 1048608 | tf_op jit(solution)/shard_map/all_to_all | solution.py:188
  225.4 0.7 pad_maximum_fusion.5
  (109 shorter events, 8.8 us)
Async XLA Ops:
  3.9 10.5 %collective-permute-start = (bf16[32,4096]{1,0:T(8,128)(2,1)S(1)}, bf16[32,4096]{1,0:T(8,128)(2,1)S(1)}, u32[]{:S(2)}, u32[]{:S(2)}) collective-permute-start(bf16[32,4096]{1,0:T(8,128)(2,1)S(1)} %constant_dynamic-slice_fusion), channel_id=1, source_target_pairs={{0,80},{1,81},{2,82},{3,83},{4,84},{5,85},{6,86},{7,87},{8,88},{9,... | collective-permute-start | bytes 786440 | tf_op jit(solution)/shard_map/ppermute | solution.py:140
  14.5 8.8 %collective-permute-start.9 = (bf16[2,32,2048]{2,1,0:T(8,128)(2,1)S(1)}, bf16[2,32,2048]{2,1,0:T(8,128)(2,1)S(1)}, u32[]{:S(2)}, u32[]{:S(2)}) collective-permute-start(bf16[2,32,2048]{2,1,0:T(8,128)(2,1)S(1)} %get-tuple-element.19), channel_id=1, source_target_pairs={{0,4},{4,8},{8,12},{12,0},{1,5},{5,9},{9,13},{13,1},{2,6},{6,10},{... | collective-permute-start | bytes 786440 | tf_op jit(solution)/shard_map/ppermute | solution.py:62
  16.1 7.6 %collective-permute-start.10 = (bf16[2,32,2048]{2,1,0:T(8,128)(2,1)S(1)}, bf16[2,32,2048]{2,1,0:T(8,128)(2,1)S(1)}, u32[]{:S(2)}, u32[]{:S(2)}) collective-permute-start(bf16[2,32,2048]{2,1,0:T(8,128)(2,1)S(1)} %get-tuple-element.19), channel_id=1, source_target_pairs={{0,12},{4,0},{8,4},{12,8},{1,13},{5,1},{9,5},{13,9},{2,14},{6,2},{... | collective-permute-start | bytes 786440 | tf_op jit(solution)/shard_map/ppermute | solution.py:66
  17.8 8.9 %collective-permute-start.1 = (bf16[2,32,2048]{2,1,0:T(8,128)(2,1)S(1)}, bf16[2,32,2048]{2,1,0:T(8,128)(2,1)S(1)}, u32[]{:S(2)}, u32[]{:S(2)}) collective-permute-start(bf16[2,32,2048]{2,1,0:T(8,128)(2,1)S(1)} %get-tuple-element.20), channel_id=1, source_target_pairs={{0,1},{1,2},{2,3},{3,0},{4,5},{5,6},{6,7},{7,4},{8,9},{9,10},{10,1... | collective-permute-start | bytes 786440 | tf_op jit(solution)/shard_map/ppermute | solution.py:62
  19.4 8.9 %collective-permute-start.2 = (bf16[2,32,2048]{2,1,0:T(8,128)(2,1)S(1)}, bf16[2,32,2048]{2,1,0:T(8,128)(2,1)S(1)}, u32[]{:S(2)}, u32[]{:S(2)}) collective-permute-start(bf16[2,32,2048]{2,1,0:T(8,128)(2,1)S(1)} %get-tuple-element.20), channel_id=1, source_target_pairs={{0,3},{1,0},{2,1},{3,2},{4,7},{5,4},{6,5},{7,6},{8,11},{9,8},{10,9... | collective-permute-start | bytes 786440 | tf_op jit(solution)/shard_map/ppermute | solution.py:66
  21.3 15.6 %copy-start.1 = (bf16[4096,512]{1,0:T(8,128)(2,1)S(1)}, bf16[4096,512]{1,0:T(8,128)(2,1)}, u32[]{:S(2)}) copy-start(bf16[4096,512]{1,0:T(8,128)(2,1)} %param.10) | copy-start | bytes 12582916
  23.3 6.9 %collective-permute-start.11 = (bf16[2,32,1024]{2,1,0:T(8,128)(2,1)S(1)}, bf16[2,32,1024]{2,1,0:T(8,128)(2,1)S(1)}, u32[]{:S(2)}, u32[]{:S(2)}) collective-permute-start(bf16[2,32,1024]{2,1,0:T(8,128)(2,1)S(1)} %slice.168), channel_id=1, source_target_pairs={{0,4},{4,8},{8,12},{12,0},{1,5},{5,9},{9,13},{13,1},{2,6},{6,10},{... | collective-permute-start | bytes 393224 | tf_op jit(solution)/shard_map/ppermute | solution.py:69
  23.6 6.6 %collective-permute-start.12 = (bf16[2,32,1024]{2,1,0:T(8,128)(2,1)S(1)}, bf16[2,32,1024]{2,1,0:T(8,128)(2,1)S(1)}, u32[]{:S(2)}, u32[]{:S(2)}) collective-permute-start(bf16[2,32,1024]{2,1,0:T(8,128)(2,1)S(1)} %slice.169), channel_id=1, source_target_pairs={{0,12},{4,0},{8,4},{12,8},{1,13},{5,1},{9,5},{13,9},{2,14},{6,2},{... | collective-permute-start | bytes 393224 | tf_op jit(solution)/shard_map/ppermute | solution.py:70
  26.7 6.2 %collective-permute-start.3 = (bf16[2,32,1024]{2,1,0:T(8,128)(2,1)S(1)}, bf16[2,32,1024]{2,1,0:T(8,128)(2,1)S(1)}, u32[]{:S(2)}, u32[]{:S(2)}) collective-permute-start(bf16[2,32,1024]{2,1,0:T(8,128)(2,1)S(1)} %slice.163), channel_id=1, source_target_pairs={{0,1},{1,2},{2,3},{3,0},{4,5},{5,6},{6,7},{7,4},{8,9},{9,10},{10,1... | collective-permute-start | bytes 393224 | tf_op jit(solution)/shard_map/ppermute | solution.py:69
  28.3 6.4 %collective-permute-start.4 = (bf16[2,32,1024]{2,1,0:T(8,128)(2,1)S(1)}, bf16[2,32,1024]{2,1,0:T(8,128)(2,1)S(1)}, u32[]{:S(2)}, u32[]{:S(2)}) collective-permute-start(bf16[2,32,1024]{2,1,0:T(8,128)(2,1)S(1)} %slice.164), channel_id=1, source_target_pairs={{0,3},{1,0},{2,1},{3,2},{4,7},{5,4},{6,5},{7,6},{8,11},{9,8},{10,9... | collective-permute-start | bytes 393224 | tf_op jit(solution)/shard_map/ppermute | solution.py:70
  30.2 7.4 %copy-start.4 = (bf16[4096,64]{0,1:T(8,128)(2,1)S(1)}, bf16[4096,64]{0,1:T(8,128)(2,1)}, u32[]{:S(2)}) copy-start(bf16[4096,64]{0,1:T(8,128)(2,1)} %param.11) | copy-start | bytes 1572868
  30.2 23.9 %collective-permute-start.14 = (bf16[4,2,32,2048]{3,2,1,0:T(8,128)(2,1)S(1)}, bf16[4,2,32,2048]{3,2,1,0:T(8,128)(2,1)S(1)}, u32[]{:S(2)}, u32[]{:S(2)}) collective-permute-start(bf16[4,2,32,2048]{3,2,1,0:T(8,128)(2,1)S(1)} %fusion.63), channel_id=1, source_target_pairs={{0,3},{1,0},{2,1},{3,2},{4,7},{5,4},{6,5},{7,6},{8,11},{9,8},{10,9... | collective-permute-start | bytes 3145736 | tf_op jit(solution)/shard_map/ppermute | solution.py:80
  32.6 25.1 %collective-permute-start.13 = (bf16[4,2,32,2048]{3,2,1,0:T(8,128)(2,1)S(1)}, bf16[4,2,32,2048]{3,2,1,0:T(8,128)(2,1)S(1)}, u32[]{:S(2)}, u32[]{:S(2)}) collective-permute-start(bf16[4,2,32,2048]{3,2,1,0:T(8,128)(2,1)S(1)} %fusion.63), channel_id=1, source_target_pairs={{0,1},{1,2},{2,3},{3,0},{4,5},{5,6},{6,7},{7,4},{8,9},{9,10},{10,1... | collective-permute-start | bytes 3145736 | tf_op jit(solution)/shard_map/ppermute | solution.py:79
  34.8 23.0 %collective-permute-start.6 = (bf16[4,2,32,2048]{3,2,1,0:T(8,128)(2,1)S(1)}, bf16[4,2,32,2048]{3,2,1,0:T(8,128)(2,1)S(1)}, u32[]{:S(2)}, u32[]{:S(2)}) collective-permute-start(bf16[4,2,32,2048]{3,2,1,0:T(8,128)(2,1)S(1)} %fusion.62), channel_id=1, source_target_pairs={{0,12},{4,0},{8,4},{12,8},{1,13},{5,1},{9,5},{13,9},{2,14},{6,2},{... | collective-permute-start | bytes 3145736 | tf_op jit(solution)/shard_map/ppermute | solution.py:80
  36.1 23.9 %collective-permute-start.5 = (bf16[4,2,32,2048]{3,2,1,0:T(8,128)(2,1)S(1)}, bf16[4,2,32,2048]{3,2,1,0:T(8,128)(2,1)S(1)}, u32[]{:S(2)}, u32[]{:S(2)}) collective-permute-start(bf16[4,2,32,2048]{3,2,1,0:T(8,128)(2,1)S(1)} %fusion.62), channel_id=1, source_target_pairs={{0,4},{4,8},{8,12},{12,0},{1,5},{5,9},{9,13},{13,1},{2,6},{6,10},{... | collective-permute-start | bytes 3145736 | tf_op jit(solution)/shard_map/ppermute | solution.py:79
  54.2 17.1 %collective-permute-start.16 = (bf16[4,2,32,1024]{3,2,1,0:T(8,128)(2,1)S(1)}, bf16[4,2,32,1024]{3,2,1,0:T(8,128)(2,1)S(1)}, u32[]{:S(2)}, u32[]{:S(2)}) collective-permute-start(bf16[4,2,32,1024]{3,2,1,0:T(8,128)(2,1)S(1)} %slice.171), channel_id=1, source_target_pairs={{0,3},{1,0},{2,1},{3,2},{4,7},{5,4},{6,5},{7,6},{8,11},{9,8},{10,9... | collective-permute-start | bytes 1572872 | tf_op jit(solution)/shard_map/ppermute | solution.py:86
  57.7 12.4 %collective-permute-start.15 = (bf16[4,2,32,1024]{3,2,1,0:T(8,128)(2,1)S(1)}, bf16[4,2,32,1024]{3,2,1,0:T(8,128)(2,1)S(1)}, u32[]{:S(2)}, u32[]{:S(2)}) collective-permute-start(bf16[4,2,32,1024]{3,2,1,0:T(8,128)(2,1)S(1)} %slice.170), channel_id=1, source_target_pairs={{0,1},{1,2},{2,3},{3,0},{4,5},{5,6},{6,7},{7,4},{8,9},{9,10},{10,1... | collective-permute-start | bytes 1572872 | tf_op jit(solution)/shard_map/ppermute | solution.py:85
  57.9 14.6 %collective-permute-start.8 = (bf16[4,2,32,1024]{3,2,1,0:T(8,128)(2,1)S(1)}, bf16[4,2,32,1024]{3,2,1,0:T(8,128)(2,1)S(1)}, u32[]{:S(2)}, u32[]{:S(2)}) collective-permute-start(bf16[4,2,32,1024]{3,2,1,0:T(8,128)(2,1)S(1)} %slice.166), channel_id=1, source_target_pairs={{0,12},{4,0},{8,4},{12,8},{1,13},{5,1},{9,5},{13,9},{2,14},{6,2},{... | collective-permute-start | bytes 1572872 | tf_op jit(solution)/shard_map/ppermute | solution.py:86
  60.0 11.2 %collective-permute-start.7 = (bf16[4,2,32,1024]{3,2,1,0:T(8,128)(2,1)S(1)}, bf16[4,2,32,1024]{3,2,1,0:T(8,128)(2,1)S(1)}, u32[]{:S(2)}, u32[]{:S(2)}) collective-permute-start(bf16[4,2,32,1024]{3,2,1,0:T(8,128)(2,1)S(1)} %slice.165), channel_id=1, source_target_pairs={{0,4},{4,8},{8,12},{12,0},{1,5},{5,9},{9,13},{13,1},{2,6},{6,10},{... | collective-permute-start | bytes 1572872 | tf_op jit(solution)/shard_map/ppermute | solution.py:85
  75.4 7.0 %copy-start = (s32[8]{0:T(128)S(1)}, s32[8]{0:T(128)}, u32[]{:S(2)}) copy-start(s32[8]{0:T(128)} %param.14) | copy-start | bytes 100
  75.4 27.8 %all-to-all-start = ((bf16[128,8,576]{2,1,0:T(8,128)(2,1)}), bf16[128,8,576]{2,1,0:T(8,128)(2,1)S(1)}, u32[]{:S(2)}, u32[]{:S(2)}) async-start(bf16[128,8,576]{2,1,0:T(8,128)(2,1)} %bitcast.31), calls=%async_computation | async-start | bytes 2621440 | tf_op jit(solution)/shard_map/all_to_all | solution.py:165
  104.8 4.1 %copy-start.2 = (bf16[8,256,8,128]{3,2,1,0:T(8,128)(2,1)S(1)}, bf16[8,256,8,128]{3,2,1,0:T(8,128)(2,1)}, u32[]{:S(2)}) copy-start(bf16[8,256,8,128]{3,2,1,0:T(8,128)(2,1)} %param.13) | copy-start | bytes 12582916
  111.3 23.2 %all-to-all-start.1 = ((bf16[128,8,512]{2,1,0:T(8,128)(2,1)}), bf16[128,8,512]{2,1,0:T(8,128)(2,1)S(1)}, u32[]{:S(2)}, u32[]{:S(2)}) async-start(bf16[128,8,512]{2,1,0:T(8,128)(2,1)} %bitcast.43), calls=%async_computation.1 | async-start | bytes 2097152 | tf_op jit(solution)/shard_map/all_to_all | solution.py:174
  134.6 4.8 %copy-start.3 = (bf16[512,4096]{1,0:T(8,128)(2,1)S(1)}, bf16[512,4096]{1,0:T(8,128)(2,1)}, u32[]{:S(2)}) copy-start(bf16[512,4096]{1,0:T(8,128)(2,1)} %param.15) | copy-start | bytes 12582916
  141.0 18.9 %collective-permute-start.21 = (bf16[2,4,32,1024]{3,2,1,0:T(8,128)(2,1)S(1)}, bf16[2,4,32,1024]{3,2,1,0:T(8,128)(2,1)S(1)}, u32[]{:S(2)}, u32[]{:S(2)}) collective-permute-start(bf16[2,4,32,1024]{3,2,1,0:T(8,128)(2,1)S(1)} %get-tuple-element.13), channel_id=1, source_target_pairs={{0,12},{4,0},{8,4},{12,8},{1,13},{5,1},{9,5},{13,9},{2,14},{6,2},{... | collective-permute-start | bytes 1572872 | tf_op jit(solution)/shard_map/ppermute | solution.py:109
  143.6 18.6 %collective-permute-start.23 = (bf16[2,4,32,1024]{3,2,1,0:T(8,128)(2,1)S(1)}, bf16[2,4,32,1024]{3,2,1,0:T(8,128)(2,1)S(1)}, u32[]{:S(2)}, u32[]{:S(2)}) collective-permute-start(bf16[2,4,32,1024]{3,2,1,0:T(8,128)(2,1)S(1)} %get-tuple-element.14), channel_id=1, source_target_pairs={{0,4},{4,8},{8,12},{12,0},{1,5},{5,9},{9,13},{13,1},{2,6},{6,10},{... | collective-permute-start | bytes 1572872 | tf_op jit(solution)/shard_map/ppermute | solution.py:110
  143.7 12.9 %collective-permute-start.17 = (bf16[2,4,32,1024]{3,2,1,0:T(8,128)(2,1)S(1)}, bf16[2,4,32,1024]{3,2,1,0:T(8,128)(2,1)S(1)}, u32[]{:S(2)}, u32[]{:S(2)}) collective-permute-start(bf16[2,4,32,1024]{3,2,1,0:T(8,128)(2,1)S(1)} %get-tuple-element.7), channel_id=1, source_target_pairs={{0,3},{1,0},{2,1},{3,2},{4,7},{5,4},{6,5},{7,6},{8,11},{9,8},{10,9... | collective-permute-start | bytes 1572872 | tf_op jit(solution)/shard_map/ppermute | solution.py:109
  145.7 13.9 %collective-permute-start.19 = (bf16[2,4,32,1024]{3,2,1,0:T(8,128)(2,1)S(1)}, bf16[2,4,32,1024]{3,2,1,0:T(8,128)(2,1)S(1)}, u32[]{:S(2)}, u32[]{:S(2)}) collective-permute-start(bf16[2,4,32,1024]{3,2,1,0:T(8,128)(2,1)S(1)} %get-tuple-element.8), channel_id=1, source_target_pairs={{0,1},{1,2},{2,3},{3,0},{4,5},{5,6},{6,7},{7,4},{8,9},{9,10},{10,1... | collective-permute-start | bytes 1572872 | tf_op jit(solution)/shard_map/ppermute | solution.py:110
  156.7 23.3 %collective-permute-start.18 = (bf16[2,4,32,2048]{3,2,1,0:T(8,128)(2,1)S(1)}, bf16[2,4,32,2048]{3,2,1,0:T(8,128)(2,1)S(1)}, u32[]{:S(2)}, u32[]{:S(2)}) collective-permute-start(bf16[2,4,32,2048]{3,2,1,0:T(8,128)(2,1)S(1)} %pad_maximum_fusion), channel_id=1, source_target_pairs={{0,3},{1,0},{2,1},{3,2},{4,7},{5,4},{6,5},{7,6},{8,11},{9,8},{10,9... | collective-permute-start | bytes 3145736 | tf_op jit(solution)/shard_map/ppermute | solution.py:115
  159.8 23.8 %collective-permute-start.20 = (bf16[2,4,32,2048]{3,2,1,0:T(8,128)(2,1)S(1)}, bf16[2,4,32,2048]{3,2,1,0:T(8,128)(2,1)S(1)}, u32[]{:S(2)}, u32[]{:S(2)}) collective-permute-start(bf16[2,4,32,2048]{3,2,1,0:T(8,128)(2,1)S(1)} %pad_maximum_fusion.1), channel_id=1, source_target_pairs={{0,1},{1,2},{2,3},{3,0},{4,5},{5,6},{6,7},{7,4},{8,9},{9,10},{10,1... | collective-permute-start | bytes 3145736 | tf_op jit(solution)/shard_map/ppermute | solution.py:116
  160.1 32.4 %collective-permute-start.22 = (bf16[2,4,32,2048]{3,2,1,0:T(8,128)(2,1)S(1)}, bf16[2,4,32,2048]{3,2,1,0:T(8,128)(2,1)}, u32[]{:S(2)}, u32[]{:S(2)}) collective-permute-start(bf16[2,4,32,2048]{3,2,1,0:T(8,128)(2,1)S(1)} %pad_maximum_fusion.2), channel_id=1, source_target_pairs={{0,12},{4,0},{8,4},{12,8},{1,13},{5,1},{9,5},{13,9},{2,14},{6,2},{... | collective-permute-start | bytes 3145736 | tf_op jit(solution)/shard_map/ppermute | solution.py:115
  163.4 29.2 %collective-permute-start.24 = (bf16[2,4,32,2048]{3,2,1,0:T(8,128)(2,1)}, bf16[2,4,32,2048]{3,2,1,0:T(8,128)(2,1)}, u32[]{:S(2)}, u32[]{:S(2)}) collective-permute-start(bf16[2,4,32,2048]{3,2,1,0:T(8,128)(2,1)} %pad_maximum_fusion.3), channel_id=1, source_target_pairs={{0,4},{4,8},{8,12},{12,0},{1,5},{5,9},{9,13},{13,1},{2,6},{6,10},{... | collective-permute-start | bytes 3145736 | tf_op jit(solution)/shard_map/ppermute | solution.py:116
  184.8 20.2 %all-to-all-start.2 = ((bf16[8,32,2048]{2,1,0:T(8,128)(2,1)}), bf16[8,32,2048]{2,1,0:T(8,128)(2,1)S(1)}, u32[]{:S(2)}, u32[]{:S(2)}) async-start(bf16[8,32,2048]{2,1,0:T(8,128)(2,1)} %bitcast.52), calls=%async_computation.2 | async-start | bytes 2097152 | tf_op jit(solution)/shard_map/all_to_all | solution.py:187
  205.0 20.3 %all-to-all-start.3 = ((bf16[8,32,2048]{2,1,0:T(8,128)(2,1)}), bf16[8,32,2048]{2,1,0:T(8,128)(2,1)S(1)}, u32[]{:S(2)}, u32[]{:S(2)}) async-start(bf16[8,32,2048]{2,1,0:T(8,128)(2,1)} %bitcast.60), calls=%async_computation.3 | async-start | bytes 2097152 | tf_op jit(solution)/shard_map/all_to_all | solution.py:188

commit v4 on v2

--- a/solution.py
+++ b/solution.py
@@ -72,6 +72,25 @@
     return lax.dynamic_update_index_in_dim(out, opposite, (idx + 2) % n, dim)
 
 
+def direct_all_gather(blk, axis, n, dim):
+    idx = lax.axis_index(axis)
+    out = jnp.zeros(blk.shape[:dim] + (n,) + blk.shape[dim:], blk.dtype)
+    out = lax.dynamic_update_index_in_dim(out, blk, idx, dim)
+    for d in range(1, n):
+        got = lax.ppermute(blk, axis, [(i, (i + d) % n) for i in range(n)])
+        out = lax.dynamic_update_index_in_dim(out, got, (idx - d) % n, dim)
+    return out
+
+
+def direct_reduce_scatter(make, axis, n):
+    idx = lax.axis_index(axis)
+    total = make(idx).astype(jnp.float32)
+    for d in range(1, n):
+        got = lax.ppermute(make((idx + d) % n), axis, [(i, (i + d) % n) for i in range(n)])
+        total = total + got.astype(jnp.float32)
+    return total.astype(jnp.bfloat16)
+
+
 def ring_all_gather_apply(blk, axis, n, dim, fn):
     idx = lax.axis_index(axis)
     fwd = [(i, (i + 1) % n) for i in range(n)]
@@ -144,8 +163,8 @@
     pair = lax.dynamic_update_index_in_dim(pair, got, 1 - zh, 0)
     first = pair[..., : width_part // 2]
     second = pair[..., width_part // 2 :]
-    first = ring_all_gather(first, "y", 4, 0)
-    second = ring_all_gather(second, "x", 4, 0)
+    first = direct_all_gather(first, "y", 4, 0)
+    second = direct_all_gather(second, "x", 4, 0)
     half = width_part // 2
 
     def project(lo, hi):
@@ -184,8 +203,8 @@
 
     first = ring_reduce_scatter(partial_out(2, 0, cols // 2), "y", 4)
     second = ring_reduce_scatter(partial_out(1, cols // 2, cols), "x", 4)
-    first = ring_reduce_scatter(blocks_of(first, 1), "x", 4)
-    second = ring_reduce_scatter(blocks_of(second, 1), "y", 4)
+    first = direct_reduce_scatter(blocks_of(first, 1), "x", 4)
+    second = direct_reduce_scatter(blocks_of(second, 1), "y", 4)
     first = ring_reduce_scatter(blocks_of(first, 0), "zh", 2)
     second = ring_reduce_scatter(blocks_of(second, 0), "zh", 2)
     return jnp.concatenate([first, second], axis=-1)

time: 217 us -> 221 us (1.018)
  waiting for transfers between devices: 113 us -> 122 us
  starting transfers between devices: 66.5 us -> 61.7 us
    ppermute x4 -> x2, waiting for transfers between devices: 16.8 us -> 0.01 us  [ring_reduce_scatter(): got_right = lax.ppermute(to_left, axis, bwd)]
    ppermute x8 -> x12, waiting for transfers between devices: 4.04 us -> 18.5 us  [the longest x6 9.96 us: direct_reduce_scatter(): lax.ppermute(make((idx + d) % n), axis, [(i, (i + d) % n) for i in range(...]
    ppermute x4 -> x2, waiting for transfers between devices: 7.82 us -> 17.4 us  [ring_reduce_scatter(): got_left = lax.ppermute(to_right, axis, fwd)]
    ppermute x4 -> x2, waiting for transfers between devices: 9.35 us -> 0.01 us  [ring_reduce_scatter(): from_right = lax.ppermute(opposite[..., :half], axis, bwd)]
    ppermute x4 -> x2, waiting for transfers between devices: 4.09 us -> 11.9 us  [ring_reduce_scatter(): from_left = lax.ppermute(opposite[..., half:], axis, fwd)]
    ppermute x8 -> x12, starting transfers between devices: 13.3 us -> 20.3 us  [the longest x6 13.2 us: direct_all_gather(): got = lax.ppermute(blk, axis, [(i, (i + d) % n) for i in range(n)])]
    ppermute x4 -> x2, starting transfers between devices: 11.6 us -> 5.86 us  [ring_reduce_scatter(): got_right = lax.ppermute(to_left, axis, bwd)]
    ppermute x4 -> x2, starting transfers between devices: 9.87 us -> 4.66 us  [ring_reduce_scatter(): from_right = lax.ppermute(opposite[..., :half], axis, bwd)]
  transfers between devices with their start and end apart: 37 -> 33, of which waited for: 17 -> 15; matrix products, arithmetic and copies ran while one was open for 6% -> 6% of each run, Pallas kernels for 0% -> 0%
where the time goes in v4:
time: 221 us; the launch traced here: 220 us
  waiting for transfers between devices  122 us (55%)
  starting transfers between devices  61.7 us (28%)
  matrix products  23 us (10%)
  other arithmetic  9.31 us (4%)
  local copies, waits for them, and re-layouts  3.66 us (2%)
    all_to_all x1, waiting for transfers between devices, shards(): lax.all_to_all(projected.astype(jnp.bfloat16), ALL, split_axis=0, concat_...  20.6 us
    all_to_all x1, waiting for transfers between devices, shards(): lax.all_to_all(sent, ALL, split_axis=0, concat_axis=0, tiled=True)  17.6 us
    ppermute x2, waiting for transfers between devices, ring_reduce_scatter(): got_left = lax.ppermute(to_right, axis, fwd)  17.4 us
    ppermute x2, waiting for transfers between devices, ring_all_gather_apply(): from_right = lax.ppermute(blk, axis, bwd)  16.2 us
    ppermute x6, starting transfers between devices, direct_all_gather(): got = lax.ppermute(blk, axis, [(i, (i + d) % n) for i in range(n)])  13.2 us
    ppermute x2, waiting for transfers between devices, ring_reduce_scatter(): from_left = lax.ppermute(opposite[..., half:], axis, fwd)  11.9 us
    ppermute x6, waiting for transfers between devices, direct_reduce_scatter(): lax.ppermute(make((idx + d) % n), axis, [(i, (i + d) % n) for i in range(...  9.96 us
    dot_general x8, matrix products, partial_out(): jnp.dot(lax.dynamic_index_in_dim(by_row, k, dim, keepdims=False), w_out[:...  9.03 us
  transfers between devices with their start and end apart: 33, of which 15 were waited for; matrix products, arithmetic and copies ran while one was open for 6% of the time, Pallas kernels for 0%

profile of v4, /device:TPU:0, one launch (start us, length us, event | category | flops | bytes accessed | tf_op | source)
XLA Modules:
  0.0 220.4 jit_solution(11526456750816063355)
XLA Ops:
  0.0 1.5 fusion.4
  1.5 0.8 convert_element_type.123
  2.3 1.5 fusion.6
  3.9 4.2 %collective-permute-start = (bf16[32,4096]{1,0:T(8,128)(2,1)S(1)}, bf16[32,4096]{1,0:T(8,128)(2,1)S(1)}, u32[]{:S(2)}, u32[]{:S(2)}) collective-permute-start(bf16[32,4096]{1,0:T(8,128)(2,1)S(1)} %constant_dynamic-slice_fusion), channel_id=1, source_target_pairs={{0,80},{1,81},{2,82},{3,83},{4,84},{5,85},{6,86},{7,87},{8,88},{9,... | collective-permute-start | bytes 786440 | tf_op jit(solution)/shard_map/ppermute | solution.py:159
  8.2 6.2 %collective-permute-done = bf16[32,4096]{1,0:T(8,128)(2,1)S(1)} collective-permute-done((bf16[32,4096]{1,0:T(8,128)(2,1)S(1)}, bf16[32,4096]{1,0:T(8,128)(2,1)S(1)}, u32[]{:S(2)}, u32[]{:S(2)}) %collective-permute-start) | collective-permute-done | bytes 262176 | tf_op jit(solution)/shard_map/ppermute | solution.py:159
  14.5 3.1 %collective-permute-start.9 = (bf16[2,32,2048]{2,1,0:T(8,128)(2,1)S(1)}, bf16[2,32,2048]{2,1,0:T(8,128)(2,1)S(1)}, u32[]{:S(2)}, u32[]{:S(2)}) collective-permute-start(bf16[2,32,2048]{2,1,0:T(8,128)(2,1)S(1)} %get-tuple-element.25), channel_id=1, source_target_pairs={{0,8},{4,12},{8,0},{12,4},{1,9},{5,13},{9,1},{13,5},{2,10},{6,14},... | collective-permute-start | bytes 786440 | tf_op jit(solution)/shard_map/ppermute | solution.py:80
  17.6 0.6 collective-permute-start.8
  18.2 2.6 %collective-permute-start.10 = (bf16[2,32,2048]{2,1,0:T(8,128)(2,1)S(1)}, bf16[2,32,2048]{2,1,0:T(8,128)(2,1)S(1)}, u32[]{:S(2)}, u32[]{:S(2)}) collective-permute-start(bf16[2,32,2048]{2,1,0:T(8,128)(2,1)S(1)} %get-tuple-element.25), channel_id=1, source_target_pairs={{0,12},{4,0},{8,4},{12,8},{1,13},{5,1},{9,5},{13,9},{2,14},{6,2},{... | collective-permute-start | bytes 786440 | tf_op jit(solution)/shard_map/ppermute | solution.py:80
  20.8 3.2 %collective-permute-start.2 = (bf16[2,32,2048]{2,1,0:T(8,128)(2,1)S(1)}, bf16[2,32,2048]{2,1,0:T(8,128)(2,1)S(1)}, u32[]{:S(2)}, u32[]{:S(2)}) collective-permute-start(bf16[2,32,2048]{2,1,0:T(8,128)(2,1)S(1)} %get-tuple-element.26), channel_id=1, source_target_pairs={{0,2},{1,3},{2,0},{3,1},{4,6},{5,7},{6,4},{7,5},{8,10},{9,11},{10,... | collective-permute-start | bytes 786440 | tf_op jit(solution)/shard_map/ppermute | solution.py:80
  24.0 0.7 collective-permute-start.1
  25.0 4.1 %collective-permute-done.8 = bf16[2,32,2048]{2,1,0:T(8,128)(2,1)S(1)} collective-permute-done((bf16[2,32,2048]{2,1,0:T(8,128)(2,1)S(1)}, bf16[2,32,2048]{2,1,0:T(8,128)(2,1)S(1)}, u32[]{:S(2)}, u32[]{:S(2)}) %collective-permute-start.8) | collective-permute-done | bytes 262176 | tf_op jit(solution)/shard_map/ppermute | solution.py:80
  29.2 3.0 %collective-permute-start.3 = (bf16[2,32,2048]{2,1,0:T(8,128)(2,1)S(1)}, bf16[2,32,2048]{2,1,0:T(8,128)(2,1)S(1)}, u32[]{:S(2)}, u32[]{:S(2)}) collective-permute-start(bf16[2,32,2048]{2,1,0:T(8,128)(2,1)S(1)} %get-tuple-element.26), channel_id=1, source_target_pairs={{0,3},{1,0},{2,1},{3,2},{4,7},{5,4},{6,5},{7,6},{8,11},{9,8},{10,9... | collective-permute-start | bytes 786440 | tf_op jit(solution)/shard_map/ppermute | solution.py:80
  32.3 0.8 collective-permute-start.12
  33.1 1.3 collective-permute-start.11
  34.7 4.2 %collective-permute-done.3 = bf16[2,32,2048]{2,1,0:T(8,128)(2,1)S(1)} collective-permute-done((bf16[2,32,2048]{2,1,0:T(8,128)(2,1)S(1)}, bf16[2,32,2048]{2,1,0:T(8,128)(2,1)S(1)}, u32[]{:S(2)}, u32[]{:S(2)}) %collective-permute-start.3) | collective-permute-done | bytes 262176 | tf_op jit(solution)/shard_map/ppermute | solution.py:80
  38.9 0.6 collective-permute-start.5
  39.5 1.5 collective-permute-start.4
  41.0 0.7 fusion.29
  41.7 0.4 fusion.90
  42.9 0.7 fusion.21
  44.0 16.2 %collective-permute-done.12 = bf16[4,2,32,2048]{3,2,1,0:T(8,128)(2,1)S(1)} collective-permute-done((bf16[4,2,32,2048]{3,2,1,0:T(8,128)(2,1)S(1)}, bf16[4,2,32,2048]{3,2,1,0:T(8,128)(2,1)S(1)}, u32[]{:S(2)}, u32[]{:S(2)}) %collective-permute-start.12) | collective-permute-done | bytes 1048608 | tf_op jit(solution)/shard_map/ppermute | solution.py:99
  60.3 3.8 %collective-permute-start.14 = (bf16[4,2,32,1024]{3,2,1,0:T(8,128)(2,1)S(1)}, bf16[4,2,32,1024]{3,2,1,0:T(8,128)(2,1)S(1)}, u32[]{:S(2)}, u32[]{:S(2)}) collective-permute-start(bf16[4,2,32,1024]{3,2,1,0:T(8,128)(2,1)S(1)} %slice.151), channel_id=1, source_target_pairs={{0,3},{1,0},{2,1},{3,2},{4,7},{5,4},{6,5},{7,6},{8,11},{9,8},{10,9... | collective-permute-start | bytes 1572872 | tf_op jit(solution)/shard_map/ppermute | solution.py:105
  64.4 2.3 %collective-permute-start.6 = (bf16[4,2,32,1024]{3,2,1,0:T(8,128)(2,1)S(1)}, bf16[4,2,32,1024]{3,2,1,0:T(8,128)(2,1)S(1)}, u32[]{:S(2)}, u32[]{:S(2)}) collective-permute-start(bf16[4,2,32,1024]{3,2,1,0:T(8,128)(2,1)S(1)} %slice.147), channel_id=1, source_target_pairs={{0,4},{4,8},{8,12},{12,0},{1,5},{5,9},{9,13},{13,1},{2,6},{6,10},{... | collective-permute-start | bytes 1572872 | tf_op jit(solution)/shard_map/ppermute | solution.py:104
  66.6 0.4 fusion.78
  67.1 0.7 fusion.17
  68.2 0.7 fusion.19
  69.3 0.7 fusion.25
  70.1 0.7 fusion.27
  71.4 6.5 %collective-permute-done.13 = bf16[4,2,32,1024]{3,2,1,0:T(8,128)(2,1)S(1)} collective-permute-done((bf16[4,2,32,1024]{3,2,1,0:T(8,128)(2,1)S(1)}, bf16[4,2,32,1024]{3,2,1,0:T(8,128)(2,1)S(1)}, u32[]{:S(2)}, u32[]{:S(2)}) %collective-permute-start.13) | collective-permute-done | bytes 524320 | tf_op jit(solution)/shard_map/ppermute | solution.py:104
  78.9 0.7 fusion.15
  80.1 0.7 fusion.23
  81.0 1.6 add_convert_fusion
  82.5 6.7 %all-to-all-start = ((bf16[128,8,576]{2,1,0:T(8,128)(2,1)}), bf16[128,8,576]{2,1,0:T(8,128)(2,1)S(1)}, u32[]{:S(2)}, u32[]{:S(2)}) async-start(bf16[128,8,576]{2,1,0:T(8,128)(2,1)} %bitcast.31), calls=%async_computation | async-start | bytes 2621440 | tf_op jit(solution)/shard_map/all_to_all | solution.py:184
  89.4 20.6 %all-to-all-done = bf16[128,8,576]{2,1,0:T(8,128)(2,1)S(1)} async-done(((bf16[128,8,576]{2,1,0:T(8,128)(2,1)}), bf16[128,8,576]{2,1,0:T(8,128)(2,1)S(1)}, u32[]{:S(2)}, u32[]{:S(2)}) %all-to-all-start) | async-done | bytes 1179680 | tf_op jit(solution)/shard_map/all_to_all | solution.py:184
  111.7 3.7 %fusion.129 = (f32[8,8,16]{2,1,0:T(8,128)S(1)}, f32[8,8,16,256]{3,2,1,0:T(8,128)S(1)}) fusion(bf16[8,256,8,128]{3,2,1,0:T(8,128)(2,1)} %param.12, bf16[8,8,16,64]{3,2,1,0:T(8,128)(2,1)S(1)} %bitcast.217, bf16[8,8,16,64]{3,2,1,0:T(8,128)(2,1)S(1)} %bitcast.215, pred[8,256]{1,0:T(8,128)(4,1)S(1)} %iota_compare_fusion), kind=kOutput, calls=%fused_computation.205 | convolution fusion | flops 68418560 | bytes 5511168 | tf_op jit(solution)/shard_map/rgqd,rtgd->rgqt/dot_general | solution.py:39
  115.8 1.0 fusion.56
  117.1 1.1 broadcast_in_dim.116
  118.2 5.6 %all-to-all-start.1 = ((bf16[128,8,512]{2,1,0:T(8,128)(2,1)}), bf16[128,8,512]{2,1,0:T(8,128)(2,1)S(1)}, u32[]{:S(2)}, u32[]{:S(2)}) async-start(bf16[128,8,512]{2,1,0:T(8,128)(2,1)} %bitcast.43), calls=%async_computation.1 | async-start | bytes 2097152 | tf_op jit(solution)/shard_map/all_to_all | solution.py:193
  123.9 17.6 %all-to-all-done.1 = bf16[128,8,512]{2,1,0:T(8,128)(2,1)S(1)} async-done(((bf16[128,8,512]{2,1,0:T(8,128)(2,1)}), bf16[128,8,512]{2,1,0:T(8,128)(2,1)S(1)}, u32[]{:S(2)}, u32[]{:S(2)}) %all-to-all-start.1) | async-done | bytes 1048608 | tf_op jit(solution)/shard_map/all_to_all | solution.py:193
  141.5 2.5 %convolution_convert_fusion.2 = bf16[2,4,32,2048]{3,2,1,0:T(8,128)(2,1)S(1)} fusion(bf16[512,4096]{1,0:T(8,128)(2,1)} %param.15, bf16[2,4,4,32,512]{4,3,2,1,0:T(8,128)(2,1)S(1)} %bitcast.205, s32[]{:T(128)S(6)} %select_n.209), kind=kOutput, calls=%fused_computation.9 | convolution fusion | flops 537395200 | bytes 3407876 | tf_op jit(solution)/shard_map/dot_general | solution.py:198
  143.9 2.3 %convolution_convert_fusion.6 = bf16[2,4,32,2048]{3,2,1,0:T(8,128)(2,1)S(1)} fusion(bf16[512,4096]{1,0:T(8,128)(2,1)} %param.15, bf16[2,4,4,32,512]{4,3,2,1,0:T(8,128)(2,1)S(1)} %bitcast.206, s32[]{:T(128)S(6)} %select_n.202), kind=kOutput, calls=%fused_computation.13 | convolution fusion | flops 537395200 | bytes 3407876 | tf_op jit(solution)/shard_map/dot_general | solution.py:198
  146.2 0.7 convolution_convert_fusion
  147.0 0.7 convolution_convert_fusion.1
  147.7 0.7 convolution_convert_fusion.5
  148.5 2.6 %collective-permute-start.23 = (bf16[2,4,32,1024]{3,2,1,0:T(8,128)(2,1)S(1)}, bf16[2,4,32,1024]{3,2,1,0:T(8,128)(2,1)S(1)}, u32[]{:S(2)}, u32[]{:S(2)}) collective-permute-start(bf16[2,4,32,1024]{3,2,1,0:T(8,128)(2,1)S(1)} %get-tuple-element.19), channel_id=1, source_target_pairs={{0,12},{4,0},{8,4},{12,8},{1,13},{5,1},{9,5},{13,9},{2,14},{6,2},{... | collective-permute-start | bytes 1572872 | tf_op jit(solution)/shard_map/ppermute | solution.py:128
  151.2 2.0 collective-permute-start.15
  153.3 0.7 convolution_convert_fusion.4
  154.0 0.7 convolution_convert_fusion.3
  154.8 11.9 %collective-permute-done.17 = bf16[2,4,32,1024]{3,2,1,0:T(8,128)(2,1)S(1)} collective-permute-done((bf16[2,4,32,1024]{3,2,1,0:T(8,128)(2,1)S(1)}, bf16[2,4,32,1024]{3,2,1,0:T(8,128)(2,1)S(1)}, u32[]{:S(2)}, u32[]{:S(2)}) %collective-permute-start.17) | collective-permute-done | bytes 524320 | tf_op jit(solution)/shard_map/ppermute | solution.py:129
  167.1 3.3 %collective-permute-start.16 = (bf16[2,4,32,2048]{3,2,1,0:T(8,128)(2,1)S(1)}, bf16[2,4,32,2048]{3,2,1,0:T(8,128)(2,1)S(1)}, u32[]{:S(2)}, u32[]{:S(2)}) collective-permute-start(bf16[2,4,32,2048]{3,2,1,0:T(8,128)(2,1)S(1)} %pad_maximum_fusion), channel_id=1, source_target_pairs={{0,3},{1,0},{2,1},{3,2},{4,7},{5,4},{6,5},{7,6},{8,11},{9,8},{10,9... | collective-permute-start | bytes 3145736 | tf_op jit(solution)/shard_map/ppermute | solution.py:134
  170.6 0.8 collective-permute-start.26
  171.5 2.6 %collective-permute-start.24 = (bf16[2,4,32,2048]{3,2,1,0:T(8,128)(2,1)S(1)}, bf16[2,4,32,2048]{3,2,1,0:T(8,128)(2,1)S(1)}, u32[]{:S(2)}, u32[]{:S(2)}) collective-permute-start(bf16[2,4,32,2048]{3,2,1,0:T(8,128)(2,1)S(1)} %pad_maximum_fusion.2), channel_id=1, source_target_pairs={{0,12},{4,0},{8,4},{12,8},{1,13},{5,1},{9,5},{13,9},{2,14},{6,2},{... | collective-permute-start | bytes 3145736 | tf_op jit(solution)/shard_map/ppermute | solution.py:134
  174.1 0.7 convolution_convert_fusion.7
  174.8 15.8 %collective-permute-done.18 = bf16[2,4,32,2048]{3,2,1,0:T(8,128)(2,1)S(1)} collective-permute-done((bf16[2,4,32,2048]{3,2,1,0:T(8,128)(2,1)S(1)}, bf16[2,4,32,2048]{3,2,1,0:T(8,128)(2,1)S(1)}, u32[]{:S(2)}, u32[]{:S(2)}) %collective-permute-start.18) | collective-permute-done | bytes 1048608 | tf_op jit(solution)/shard_map/ppermute | solution.py:135
  190.9 0.8 collective-permute-start.19
  191.7 2.5 %collective-permute-start.21 = (bf16[2,32,2048]{2,1,0:T(8,128)(2,1)S(1)}, bf16[2,32,2048]{2,1,0:T(8,128)(2,1)S(1)}, u32[]{:S(2)}, u32[]{:S(2)}) collective-permute-start(bf16[2,32,2048]{2,1,0:T(8,128)(2,1)S(1)} %get-tuple-element.6), channel_id=1, source_target_pairs={{0,12},{4,0},{8,4},{12,8},{1,13},{5,1},{9,5},{13,9},{2,14},{6,2},{... | collective-permute-start | bytes 786440 | tf_op jit(solution)/shard_map/ppermute | solution.py:89
  194.2 0.4 collective-permute-start.20
  194.6 1.6 collective-permute-done.26
  196.6 3.2 %collective-permute-start.29 = (bf16[2,32,2048]{2,1,0:T(8,128)(2,1)S(1)}, bf16[2,32,2048]{2,1,0:T(8,128)(2,1)S(1)}, u32[]{:S(2)}, u32[]{:S(2)}) collective-permute-start(bf16[2,32,2048]{2,1,0:T(8,128)(2,1)S(1)} %get-tuple-element.15), channel_id=1, source_target_pairs={{0,3},{1,0},{2,1},{3,2},{4,7},{5,4},{6,5},{7,6},{8,11},{9,8},{10,9... | collective-permute-start | bytes 786440 | tf_op jit(solution)/shard_map/ppermute | solution.py:89
  199.8 5.3 %collective-permute-done.19 = bf16[2,32,2048]{2,1,0:T(8,128)(2,1)S(1)} collective-permute-done((bf16[2,32,2048]{2,1,0:T(8,128)(2,1)S(1)}, bf16[2,32,2048]{2,1,0:T(8,128)(2,1)S(1)}, u32[]{:S(2)}, u32[]{:S(2)}) %collective-permute-start.19) | collective-permute-done | bytes 262176 | tf_op jit(solution)/shard_map/ppermute | solution.py:89
  205.3 3.0 %collective-permute-start.22 = (bf16[32,2048]{1,0:T(8,128)(2,1)S(1)}, bf16[32,2048]{1,0:T(8,128)(2,1)S(1)}, u32[]{:S(2)}, u32[]{:S(2)}) collective-permute-start(bf16[32,2048]{1,0:T(8,128)(2,1)S(1)} %dynamic-slice_bitcast_fusion.7), channel_id=1, source_target_pairs={{0,16},{16,0},{1,17},{17,1},{2,18},{18,2},{3,19},{19,3},{4,20},{20... | collective-permute-start | bytes 393224 | tf_op jit(solution)/shard_map/ppermute | solution.py:125
  208.3 4.7 %collective-permute-done.28 = bf16[2,32,2048]{2,1,0:T(8,128)(2,1)S(1)} collective-permute-done((bf16[2,32,2048]{2,1,0:T(8,128)(2,1)S(1)}, bf16[2,32,2048]{2,1,0:T(8,128)(2,1)S(1)}, u32[]{:S(2)}, u32[]{:S(2)}) %collective-permute-start.28) | collective-permute-done | bytes 262176 | tf_op jit(solution)/shard_map/ppermute | solution.py:89
  213.3 6.4 %collective-permute-done.30 = bf16[32,2048]{1,0:T(8,128)(2,1)S(1)} collective-permute-done((bf16[32,2048]{1,0:T(8,128)(2,1)S(1)}, bf16[32,2048]{1,0:T(8,128)(2,1)S(1)}, u32[]{:S(2)}, u32[]{:S(2)}) %collective-permute-start.30) | collective-permute-done | bytes 131104 | tf_op jit(solution)/shard_map/ppermute | solution.py:125
  219.7 0.7 pad_maximum_fusion.5
  (119 shorter events, 9.7 us)
Async XLA Ops:
  3.9 10.5 %collective-permute-start = (bf16[32,4096]{1,0:T(8,128)(2,1)S(1)}, bf16[32,4096]{1,0:T(8,128)(2,1)S(1)}, u32[]{:S(2)}, u32[]{:S(2)}) collective-permute-start(bf16[32,4096]{1,0:T(8,128)(2,1)S(1)} %constant_dynamic-slice_fusion), channel_id=1, source_target_pairs={{0,80},{1,81},{2,82},{3,83},{4,84},{5,85},{6,86},{7,87},{8,88},{9,... | collective-permute-start | bytes 786440 | tf_op jit(solution)/shard_map/ppermute | solution.py:159
  14.5 17.7 %collective-permute-start.9 = (bf16[2,32,2048]{2,1,0:T(8,128)(2,1)S(1)}, bf16[2,32,2048]{2,1,0:T(8,128)(2,1)S(1)}, u32[]{:S(2)}, u32[]{:S(2)}) collective-permute-start(bf16[2,32,2048]{2,1,0:T(8,128)(2,1)S(1)} %get-tuple-element.25), channel_id=1, source_target_pairs={{0,8},{4,12},{8,0},{12,4},{1,9},{5,13},{9,1},{13,5},{2,10},{6,14},... | collective-permute-start | bytes 786440 | tf_op jit(solution)/shard_map/ppermute | solution.py:80
  17.6 11.6 %collective-permute-start.8 = (bf16[2,32,2048]{2,1,0:T(8,128)(2,1)S(1)}, bf16[2,32,2048]{2,1,0:T(8,128)(2,1)S(1)}, u32[]{:S(2)}, u32[]{:S(2)}) collective-permute-start(bf16[2,32,2048]{2,1,0:T(8,128)(2,1)S(1)} %get-tuple-element.25), channel_id=1, source_target_pairs={{0,4},{4,8},{8,12},{12,0},{1,5},{5,9},{9,13},{13,1},{2,6},{6,10},{... | collective-permute-start | bytes 786440 | tf_op jit(solution)/shard_map/ppermute | solution.py:80
  18.2 14.1 %collective-permute-start.10 = (bf16[2,32,2048]{2,1,0:T(8,128)(2,1)S(1)}, bf16[2,32,2048]{2,1,0:T(8,128)(2,1)S(1)}, u32[]{:S(2)}, u32[]{:S(2)}) collective-permute-start(bf16[2,32,2048]{2,1,0:T(8,128)(2,1)S(1)} %get-tuple-element.25), channel_id=1, source_target_pairs={{0,12},{4,0},{8,4},{12,8},{1,13},{5,1},{9,5},{13,9},{2,14},{6,2},{... | collective-permute-start | bytes 786440 | tf_op jit(solution)/shard_map/ppermute | solution.py:80
  20.8 13.8 %collective-permute-start.2 = (bf16[2,32,2048]{2,1,0:T(8,128)(2,1)S(1)}, bf16[2,32,2048]{2,1,0:T(8,128)(2,1)S(1)}, u32[]{:S(2)}, u32[]{:S(2)}) collective-permute-start(bf16[2,32,2048]{2,1,0:T(8,128)(2,1)S(1)} %get-tuple-element.26), channel_id=1, source_target_pairs={{0,2},{1,3},{2,0},{3,1},{4,6},{5,7},{6,4},{7,5},{8,10},{9,11},{10,... | collective-permute-start | bytes 786440 | tf_op jit(solution)/shard_map/ppermute | solution.py:80
  24.0 10.6 %collective-permute-start.1 = (bf16[2,32,2048]{2,1,0:T(8,128)(2,1)S(1)}, bf16[2,32,2048]{2,1,0:T(8,128)(2,1)S(1)}, u32[]{:S(2)}, u32[]{:S(2)}) collective-permute-start(bf16[2,32,2048]{2,1,0:T(8,128)(2,1)S(1)} %get-tuple-element.26), channel_id=1, source_target_pairs={{0,1},{1,2},{2,3},{3,0},{4,5},{5,6},{6,7},{7,4},{8,9},{9,10},{10,1... | collective-permute-start | bytes 786440 | tf_op jit(solution)/shard_map/ppermute | solution.py:80
  24.8 16.2 %copy-start.1 = (bf16[4096,512]{1,0:T(8,128)(2,1)S(1)}, bf16[4096,512]{1,0:T(8,128)(2,1)}, u32[]{:S(2)}) copy-start(bf16[4096,512]{1,0:T(8,128)(2,1)} %param.10) | copy-start | bytes 12582916
  29.2 9.7 %collective-permute-start.3 = (bf16[2,32,2048]{2,1,0:T(8,128)(2,1)S(1)}, bf16[2,32,2048]{2,1,0:T(8,128)(2,1)S(1)}, u32[]{:S(2)}, u32[]{:S(2)}) collective-permute-start(bf16[2,32,2048]{2,1,0:T(8,128)(2,1)S(1)} %get-tuple-element.26), channel_id=1, source_target_pairs={{0,3},{1,0},{2,1},{3,2},{4,7},{5,4},{6,5},{7,6},{8,11},{9,8},{10,9... | collective-permute-start | bytes 786440 | tf_op jit(solution)/shard_map/ppermute | solution.py:80
  32.3 27.9 %collective-permute-start.12 = (bf16[4,2,32,2048]{3,2,1,0:T(8,128)(2,1)S(1)}, bf16[4,2,32,2048]{3,2,1,0:T(8,128)(2,1)S(1)}, u32[]{:S(2)}, u32[]{:S(2)}) collective-permute-start(bf16[4,2,32,2048]{3,2,1,0:T(8,128)(2,1)S(1)} %bitcast_dynamic-update-slice_fusion), channel_id=1, source_target_pairs={{0,3},{1,0},{2,1},{3,2},{4,7},{5,4},{6,5},{7,6},{8,11},{9,8},{10,9... | collective-permute-start | bytes 3145736 | tf_op jit(solution)/shard_map/ppermute | solution.py:99
  33.1 30.9 %collective-permute-start.11 = (bf16[4,2,32,2048]{3,2,1,0:T(8,128)(2,1)S(1)}, bf16[4,2,32,2048]{3,2,1,0:T(8,128)(2,1)S(1)}, u32[]{:S(2)}, u32[]{:S(2)}) collective-permute-start(bf16[4,2,32,2048]{3,2,1,0:T(8,128)(2,1)S(1)} %bitcast_dynamic-update-slice_fusion), channel_id=1, source_target_pairs={{0,1},{1,2},{2,3},{3,0},{4,5},{5,6},{6,7},{7,4},{8,9},{9,10},{10,1... | collective-permute-start | bytes 3145736 | tf_op jit(solution)/shard_map/ppermute | solution.py:98
  34.7 7.1 %copy-start.4 = (bf16[4096,64]{0,1:T(8,128)(2,1)S(1)}, bf16[4096,64]{0,1:T(8,128)(2,1)}, u32[]{:S(2)}) copy-start(bf16[4096,64]{0,1:T(8,128)(2,1)} %param.11) | copy-start | bytes 1572868
  38.9 25.3 %collective-permute-start.5 = (bf16[4,2,32,2048]{3,2,1,0:T(8,128)(2,1)S(1)}, bf16[4,2,32,2048]{3,2,1,0:T(8,128)(2,1)S(1)}, u32[]{:S(2)}, u32[]{:S(2)}) collective-permute-start(bf16[4,2,32,2048]{3,2,1,0:T(8,128)(2,1)S(1)} %bitcast_dynamic-update-slice_fusion.4), channel_id=1, source_target_pairs={{0,12},{4,0},{8,4},{12,8},{1,13},{5,1},{9,5},{13,9},{2,14},{6,2},{... | collective-permute-start | bytes 3145736 | tf_op jit(solution)/shard_map/ppermute | solution.py:99
  39.5 24.8 %collective-permute-start.4 = (bf16[4,2,32,2048]{3,2,1,0:T(8,128)(2,1)S(1)}, bf16[4,2,32,2048]{3,2,1,0:T(8,128)(2,1)S(1)}, u32[]{:S(2)}, u32[]{:S(2)}) collective-permute-start(bf16[4,2,32,2048]{3,2,1,0:T(8,128)(2,1)S(1)} %bitcast_dynamic-update-slice_fusion.4), channel_id=1, source_target_pairs={{0,4},{4,8},{8,12},{12,0},{1,5},{5,9},{9,13},{13,1},{2,6},{6,10},{... | collective-permute-start | bytes 3145736 | tf_op jit(solution)/shard_map/ppermute | solution.py:98
  60.3 18.1 %collective-permute-start.14 = (bf16[4,2,32,1024]{3,2,1,0:T(8,128)(2,1)S(1)}, bf16[4,2,32,1024]{3,2,1,0:T(8,128)(2,1)S(1)}, u32[]{:S(2)}, u32[]{:S(2)}) collective-permute-start(bf16[4,2,32,1024]{3,2,1,0:T(8,128)(2,1)S(1)} %slice.151), channel_id=1, source_target_pairs={{0,3},{1,0},{2,1},{3,2},{4,7},{5,4},{6,5},{7,6},{8,11},{9,8},{10,9... | collective-permute-start | bytes 1572872 | tf_op jit(solution)/shard_map/ppermute | solution.py:105
  64.1 13.8 %collective-permute-start.13 = (bf16[4,2,32,1024]{3,2,1,0:T(8,128)(2,1)S(1)}, bf16[4,2,32,1024]{3,2,1,0:T(8,128)(2,1)S(1)}, u32[]{:S(2)}, u32[]{:S(2)}) collective-permute-start(bf16[4,2,32,1024]{3,2,1,0:T(8,128)(2,1)S(1)} %slice.150), channel_id=1, source_target_pairs={{0,1},{1,2},{2,3},{3,0},{4,5},{5,6},{6,7},{7,4},{8,9},{9,10},{10,1... | collective-permute-start | bytes 1572872 | tf_op jit(solution)/shard_map/ppermute | solution.py:104
  64.2 15.4 %collective-permute-start.7 = (bf16[4,2,32,1024]{3,2,1,0:T(8,128)(2,1)S(1)}, bf16[4,2,32,1024]{3,2,1,0:T(8,128)(2,1)S(1)}, u32[]{:S(2)}, u32[]{:S(2)}) collective-permute-start(bf16[4,2,32,1024]{3,2,1,0:T(8,128)(2,1)S(1)} %slice.148), channel_id=1, source_target_pairs={{0,12},{4,0},{8,4},{12,8},{1,13},{5,1},{9,5},{13,9},{2,14},{6,2},{... | collective-permute-start | bytes 1572872 | tf_op jit(solution)/shard_map/ppermute | solution.py:105
  64.4 14.0 %collective-permute-start.6 = (bf16[4,2,32,1024]{3,2,1,0:T(8,128)(2,1)S(1)}, bf16[4,2,32,1024]{3,2,1,0:T(8,128)(2,1)S(1)}, u32[]{:S(2)}, u32[]{:S(2)}) collective-permute-start(bf16[4,2,32,1024]{3,2,1,0:T(8,128)(2,1)S(1)} %slice.147), channel_id=1, source_target_pairs={{0,4},{4,8},{8,12},{12,0},{1,5},{5,9},{9,13},{13,1},{2,6},{6,10},{... | collective-permute-start | bytes 1572872 | tf_op jit(solution)/shard_map/ppermute | solution.py:104
  82.5 6.7 %copy-start = (s32[8]{0:T(128)S(1)}, s32[8]{0:T(128)}, u32[]{:S(2)}) copy-start(s32[8]{0:T(128)} %param.14) | copy-start | bytes 100
  82.5 27.5 %all-to-all-start = ((bf16[128,8,576]{2,1,0:T(8,128)(2,1)}), bf16[128,8,576]{2,1,0:T(8,128)(2,1)S(1)}, u32[]{:S(2)}, u32[]{:S(2)}) async-start(bf16[128,8,576]{2,1,0:T(8,128)(2,1)} %bitcast.31), calls=%async_computation | async-start | bytes 2621440 | tf_op jit(solution)/shard_map/all_to_all | solution.py:184
  111.7 4.1 %copy-start.2 = (bf16[8,256,8,128]{3,2,1,0:T(8,128)(2,1)S(1)}, bf16[8,256,8,128]{3,2,1,0:T(8,128)(2,1)}, u32[]{:S(2)}) copy-start(bf16[8,256,8,128]{3,2,1,0:T(8,128)(2,1)} %param.13) | copy-start | bytes 12582916
  118.2 23.2 %all-to-all-start.1 = ((bf16[128,8,512]{2,1,0:T(8,128)(2,1)}), bf16[128,8,512]{2,1,0:T(8,128)(2,1)S(1)}, u32[]{:S(2)}, u32[]{:S(2)}) async-start(bf16[128,8,512]{2,1,0:T(8,128)(2,1)} %bitcast.43), calls=%async_computation.1 | async-start | bytes 2097152 | tf_op jit(solution)/shard_map/all_to_all | solution.py:193
  141.5 4.8 %copy-start.3 = (bf16[512,4096]{1,0:T(8,128)(2,1)S(1)}, bf16[512,4096]{1,0:T(8,128)(2,1)}, u32[]{:S(2)}) copy-start(bf16[512,4096]{1,0:T(8,128)(2,1)} %param.15) | copy-start | bytes 12582916
  148.5 22.9 %collective-permute-start.23 = (bf16[2,4,32,1024]{3,2,1,0:T(8,128)(2,1)S(1)}, bf16[2,4,32,1024]{3,2,1,0:T(8,128)(2,1)S(1)}, u32[]{:S(2)}, u32[]{:S(2)}) collective-permute-start(bf16[2,4,32,1024]{3,2,1,0:T(8,128)(2,1)S(1)} %get-tuple-element.19), channel_id=1, source_target_pairs={{0,12},{4,0},{8,4},{12,8},{1,13},{5,1},{9,5},{13,9},{2,14},{6,2},{... | collective-permute-start | bytes 1572872 | tf_op jit(solution)/shard_map/ppermute | solution.py:128
  151.1 19.2 %collective-permute-start.25 = (bf16[2,4,32,1024]{3,2,1,0:T(8,128)(2,1)S(1)}, bf16[2,4,32,1024]{3,2,1,0:T(8,128)(2,1)S(1)}, u32[]{:S(2)}, u32[]{:S(2)}) collective-permute-start(bf16[2,4,32,1024]{3,2,1,0:T(8,128)(2,1)S(1)} %get-tuple-element.20), channel_id=1, source_target_pairs={{0,4},{4,8},{8,12},{12,0},{1,5},{5,9},{9,13},{13,1},{2,6},{6,10},{... | collective-permute-start | bytes 1572872 | tf_op jit(solution)/shard_map/ppermute | solution.py:129
  151.2 15.7 %collective-permute-start.15 = (bf16[2,4,32,1024]{3,2,1,0:T(8,128)(2,1)S(1)}, bf16[2,4,32,1024]{3,2,1,0:T(8,128)(2,1)S(1)}, u32[]{:S(2)}, u32[]{:S(2)}) collective-permute-start(bf16[2,4,32,1024]{3,2,1,0:T(8,128)(2,1)S(1)} %get-tuple-element.10), channel_id=1, source_target_pairs={{0,3},{1,0},{2,1},{3,2},{4,7},{5,4},{6,5},{7,6},{8,11},{9,8},{10,9... | collective-permute-start | bytes 1572872 | tf_op jit(solution)/shard_map/ppermute | solution.py:128
  153.2 13.4 %collective-permute-start.17 = (bf16[2,4,32,1024]{3,2,1,0:T(8,128)(2,1)S(1)}, bf16[2,4,32,1024]{3,2,1,0:T(8,128)(2,1)S(1)}, u32[]{:S(2)}, u32[]{:S(2)}) collective-permute-start(bf16[2,4,32,1024]{3,2,1,0:T(8,128)(2,1)S(1)} %get-tuple-element.11), channel_id=1, source_target_pairs={{0,1},{1,2},{2,3},{3,0},{4,5},{5,6},{6,7},{7,4},{8,9},{9,10},{10,1... | collective-permute-start | bytes 1572872 | tf_op jit(solution)/shard_map/ppermute | solution.py:129
  166.8 23.8 %collective-permute-start.18 = (bf16[2,4,32,2048]{3,2,1,0:T(8,128)(2,1)S(1)}, bf16[2,4,32,2048]{3,2,1,0:T(8,128)(2,1)S(1)}, u32[]{:S(2)}, u32[]{:S(2)}) collective-permute-start(bf16[2,4,32,2048]{3,2,1,0:T(8,128)(2,1)S(1)} %pad_maximum_fusion.1), channel_id=1, source_target_pairs={{0,1},{1,2},{2,3},{3,0},{4,5},{5,6},{6,7},{7,4},{8,9},{9,10},{10,1... | collective-permute-start | bytes 3145736 | tf_op jit(solution)/shard_map/ppermute | solution.py:135
  167.1 23.6 %collective-permute-start.16 = (bf16[2,4,32,2048]{3,2,1,0:T(8,128)(2,1)S(1)}, bf16[2,4,32,2048]{3,2,1,0:T(8,128)(2,1)S(1)}, u32[]{:S(2)}, u32[]{:S(2)}) collective-permute-start(bf16[2,4,32,2048]{3,2,1,0:T(8,128)(2,1)S(1)} %pad_maximum_fusion), channel_id=1, source_target_pairs={{0,3},{1,0},{2,1},{3,2},{4,7},{5,4},{6,5},{7,6},{8,11},{9,8},{10,9... | collective-permute-start | bytes 3145736 | tf_op jit(solution)/shard_map/ppermute | solution.py:134
  170.6 25.7 %collective-permute-start.26 = (bf16[2,4,32,2048]{3,2,1,0:T(8,128)(2,1)S(1)}, bf16[2,4,32,2048]{3,2,1,0:T(8,128)(2,1)S(1)}, u32[]{:S(2)}, u32[]{:S(2)}) collective-permute-start(bf16[2,4,32,2048]{3,2,1,0:T(8,128)(2,1)S(1)} %pad_maximum_fusion.3), channel_id=1, source_target_pairs={{0,4},{4,8},{8,12},{12,0},{1,5},{5,9},{9,13},{13,1},{2,6},{6,10},{... | collective-permute-start | bytes 3145736 | tf_op jit(solution)/shard_map/ppermute | solution.py:135
  171.5 24.7 %collective-permute-start.24 = (bf16[2,4,32,2048]{3,2,1,0:T(8,128)(2,1)S(1)}, bf16[2,4,32,2048]{3,2,1,0:T(8,128)(2,1)S(1)}, u32[]{:S(2)}, u32[]{:S(2)}) collective-permute-start(bf16[2,4,32,2048]{3,2,1,0:T(8,128)(2,1)S(1)} %pad_maximum_fusion.2), channel_id=1, source_target_pairs={{0,12},{4,0},{8,4},{12,8},{1,13},{5,1},{9,5},{13,9},{2,14},{6,2},{... | collective-permute-start | bytes 3145736 | tf_op jit(solution)/shard_map/ppermute | solution.py:134
  190.9 14.2 %collective-permute-start.19 = (bf16[2,32,2048]{2,1,0:T(8,128)(2,1)S(1)}, bf16[2,32,2048]{2,1,0:T(8,128)(2,1)S(1)}, u32[]{:S(2)}, u32[]{:S(2)}) collective-permute-start(bf16[2,32,2048]{2,1,0:T(8,128)(2,1)S(1)} %get-tuple-element.5), channel_id=1, source_target_pairs={{0,4},{4,8},{8,12},{12,0},{1,5},{5,9},{9,13},{13,1},{2,6},{6,10},{... | collective-permute-start | bytes 786440 | tf_op jit(solution)/shard_map/ppermute | solution.py:89
  191.7 13.3 %collective-permute-start.21 = (bf16[2,32,2048]{2,1,0:T(8,128)(2,1)S(1)}, bf16[2,32,2048]{2,1,0:T(8,128)(2,1)S(1)}, u32[]{:S(2)}, u32[]{:S(2)}) collective-permute-start(bf16[2,32,2048]{2,1,0:T(8,128)(2,1)S(1)} %get-tuple-element.6), channel_id=1, source_target_pairs={{0,12},{4,0},{8,4},{12,8},{1,13},{5,1},{9,5},{13,9},{2,14},{6,2},{... | collective-permute-start | bytes 786440 | tf_op jit(solution)/shard_map/ppermute | solution.py:89
  194.2 10.9 %collective-permute-start.20 = (bf16[2,32,2048]{2,1,0:T(8,128)(2,1)S(1)}, bf16[2,32,2048]{2,1,0:T(8,128)(2,1)S(1)}, u32[]{:S(2)}, u32[]{:S(2)}) collective-permute-start(bf16[2,32,2048]{2,1,0:T(8,128)(2,1)S(1)} %get-tuple-element.7), channel_id=1, source_target_pairs={{0,8},{4,12},{8,0},{12,4},{1,9},{5,13},{9,1},{13,5},{2,10},{6,14},... | collective-permute-start | bytes 786440 | tf_op jit(solution)/shard_map/ppermute | solution.py:89
  196.5 11.8 %collective-permute-start.27 = (bf16[2,32,2048]{2,1,0:T(8,128)(2,1)S(1)}, bf16[2,32,2048]{2,1,0:T(8,128)(2,1)S(1)}, u32[]{:S(2)}, u32[]{:S(2)}) collective-permute-start(bf16[2,32,2048]{2,1,0:T(8,128)(2,1)S(1)} %get-tuple-element.14), channel_id=1, source_target_pairs={{0,1},{1,2},{2,3},{3,0},{4,5},{5,6},{6,7},{7,4},{8,9},{9,10},{10,1... | collective-permute-start | bytes 786440 | tf_op jit(solution)/shard_map/ppermute | solution.py:89
  196.6 11.7 %collective-permute-start.29 = (bf16[2,32,2048]{2,1,0:T(8,128)(2,1)S(1)}, bf16[2,32,2048]{2,1,0:T(8,128)(2,1)S(1)}, u32[]{:S(2)}, u32[]{:S(2)}) collective-permute-start(bf16[2,32,2048]{2,1,0:T(8,128)(2,1)S(1)} %get-tuple-element.15), channel_id=1, source_target_pairs={{0,3},{1,0},{2,1},{3,2},{4,7},{5,4},{6,5},{7,6},{8,11},{9,8},{10,9... | collective-permute-start | bytes 786440 | tf_op jit(solution)/shard_map/ppermute | solution.py:89
  205.1 7.9 %collective-permute-start.28 = (bf16[2,32,2048]{2,1,0:T(8,128)(2,1)S(1)}, bf16[2,32,2048]{2,1,0:T(8,128)(2,1)S(1)}, u32[]{:S(2)}, u32[]{:S(2)}) collective-permute-start(bf16[2,32,2048]{2,1,0:T(8,128)(2,1)S(1)} %get-tuple-element.16), channel_id=1, source_target_pairs={{0,2},{1,3},{2,0},{3,1},{4,6},{5,7},{6,4},{7,5},{8,10},{9,11},{10,... | collective-permute-start | bytes 786440 | tf_op jit(solution)/shard_map/ppermute | solution.py:89
  205.3 8.0 %collective-permute-start.22 = (bf16[32,2048]{1,0:T(8,128)(2,1)S(1)}, bf16[32,2048]{1,0:T(8,128)(2,1)S(1)}, u32[]{:S(2)}, u32[]{:S(2)}) collective-permute-start(bf16[32,2048]{1,0:T(8,128)(2,1)S(1)} %dynamic-slice_bitcast_fusion.7), channel_id=1, source_target_pairs={{0,16},{16,0},{1,17},{17,1},{2,18},{18,2},{3,19},{19,3},{4,20},{20... | collective-permute-start | bytes 393224 | tf_op jit(solution)/shard_map/ppermute | solution.py:125
  213.1 6.6 %collective-permute-start.30 = (bf16[32,2048]{1,0:T(8,128)(2,1)S(1)}, bf16[32,2048]{1,0:T(8,128)(2,1)S(1)}, u32[]{:S(2)}, u32[]{:S(2)}) collective-permute-start(bf16[32,2048]{1,0:T(8,128)(2,1)S(1)} %dynamic-slice_bitcast_fusion.6), channel_id=1, source_target_pairs={{0,16},{16,0},{1,17},{17,1},{2,18},{18,2},{3,19},{19,3},{4,20},{20... | collective-permute-start | bytes 393224 | tf_op jit(solution)/shard_map/ppermute | solution.py:125

commit v5 on v2

--- a/solution.py
+++ b/solution.py
@@ -169,9 +169,8 @@
     query = split_cols[:, :, :query_cols].reshape(rows_dev, peers * query_cols)
     keyval = split_cols[:, :, query_cols:].reshape(rows_dev, peers * pair_cols)
     attended = attend_rows(query, keyval, key_cache, value_cache, lengths)
-    heads_first = attended.reshape(rows_dev, peers, query_cols).transpose(1, 0, 2)
-    sent = jnp.broadcast_to(heads_first[None], (4,) + heads_first.shape).reshape(-1, query_cols)
-    full_rows = lax.all_to_all(sent, ALL, split_axis=0, concat_axis=0, tiled=True)
+    by_heads = lax.all_to_all(attended, GY, split_axis=1, concat_axis=0, tiled=True)
+    full_rows = ring_all_gather(by_heads, "gx", 4, 0).reshape(-1, query_cols)
     cols = w_out.shape[1]
     by_row = full_rows.reshape(2, 4, 4, rows_dev * 4, query_cols)
 

time: 217 us -> 215 us (level)
  blocking collectives: 0 us -> 15.5 us
  waiting for transfers between devices: 113 us -> 100 us
  starting transfers between devices: 66.5 us -> 63.8 us
    all_to_all x1 -> x0, waiting for transfers between devices: 17.6 us -> none  [shards(): lax.all_to_all(sent, ALL, split_axis=0, concat_axis=0, tiled=True)]
    all_to_all x0 -> x1, blocking collectives: none -> 15.5 us  [shards(): lax.all_to_all(attended, GY, split_axis=1, concat_axis=0, tiled=True)]
    ppermute x2, waiting for transfers between devices: 14.3 us -> 0.01 us  [ring_all_gather_apply(): from_right = lax.ppermute(blk, axis, bwd)]
    ppermute x2, waiting for transfers between devices: 0.01 us -> 14.2 us  [ring_all_gather_apply(): from_left = lax.ppermute(blk, axis, fwd)]
    ppermute x2 -> x3, waiting for transfers between devices: 1.9 us -> 7.83 us  [ring_all_gather(): from_left = lax.ppermute(blk, axis, fwd)]
    all_to_all x1 -> x0, starting transfers between devices: 5.58 us -> none  [shards(): lax.all_to_all(sent, ALL, split_axis=0, concat_axis=0, tiled=True)]
    ppermute x4, waiting for transfers between devices: 4.09 us -> 0.01 us  [ring_reduce_scatter(): from_left = lax.ppermute(opposite[..., half:], axis, fwd)]
    ppermute x2 -> x3, waiting for transfers between devices: 0.28 us -> 3.4 us  [ring_all_gather(): first = lax.ppermute(from_left[..., :half], axis, fwd)]
  transfers between devices with their start and end apart: 37 -> 40, of which waited for: 17 -> 18; matrix products, arithmetic and copies ran while one was open for 6% -> 6% of each run, Pallas kernels for 0% -> 0%
where the time goes in v5:
time: 215 us; the launch traced here: 214 us
  waiting for transfers between devices  100 us (47%)
  starting transfers between devices  63.8 us (30%)
  matrix products  21.4 us (10%)
  blocking collectives  15.5 us (7%)
  other arithmetic  9.41 us (4%)
  local copies, waits for them, and re-layouts  2.78 us (1%)
    all_to_all x1, waiting for transfers between devices, shards(): lax.all_to_all(projected.astype(jnp.bfloat16), ALL, split_axis=0, concat_...  20.6 us
    ppermute x4, waiting for transfers between devices, ring_reduce_scatter(): got_right = lax.ppermute(to_left, axis, bwd)  19.4 us
    all_to_all x1, blocking collectives, shards(): lax.all_to_all(attended, GY, split_axis=1, concat_axis=0, tiled=True)  15.5 us
    ppermute x2, waiting for transfers between devices, ring_all_gather_apply(): from_left = lax.ppermute(blk, axis, fwd)  14.2 us
    ppermute x4, waiting for transfers between devices, ring_reduce_scatter(): got_left = lax.ppermute(to_right, axis, fwd)  10.8 us
    ppermute x4, starting transfers between devices, ring_reduce_scatter(): got_right = lax.ppermute(to_left, axis, bwd)  10.2 us
    ppermute x4, waiting for transfers between devices, ring_reduce_scatter(): from_right = lax.ppermute(opposite[..., :half], axis, bwd)  9.06 us
    ppermute x3, waiting for transfers between devices, ring_all_gather(): from_left = lax.ppermute(blk, axis, fwd)  7.83 us
  transfers between devices with their start and end apart: 40, of which 18 were waited for; matrix products, arithmetic and copies ran while one was open for 6% of the time, Pallas kernels for 0%

profile of v5, /device:TPU:0, one launch (start us, length us, event | category | flops | bytes accessed | tf_op | source)
XLA Modules:
  0.0 214.2 jit_solution(2501281783068919253)
XLA Ops:
  0.0 0.8 convert_element_type.87
  0.8 1.5 fusion.4
  2.3 1.5 fusion.6
  3.9 4.2 %collective-permute-start = (bf16[32,4096]{1,0:T(8,128)(2,1)S(1)}, bf16[32,4096]{1,0:T(8,128)(2,1)S(1)}, u32[]{:S(2)}, u32[]{:S(2)}) collective-permute-start(bf16[32,4096]{1,0:T(8,128)(2,1)S(1)} %constant_dynamic-slice_fusion), channel_id=1, source_target_pairs={{0,80},{1,81},{2,82},{3,83},{4,84},{5,85},{6,86},{7,87},{8,88},{9,... | collective-permute-start | bytes 786440 | tf_op jit(solution)/shard_map/ppermute | solution.py:140
  8.2 6.2 %collective-permute-done = bf16[32,4096]{1,0:T(8,128)(2,1)S(1)} collective-permute-done((bf16[32,4096]{1,0:T(8,128)(2,1)S(1)}, bf16[32,4096]{1,0:T(8,128)(2,1)S(1)}, u32[]{:S(2)}, u32[]{:S(2)}) %collective-permute-start) | collective-permute-done | bytes 262176 | tf_op jit(solution)/shard_map/ppermute | solution.py:140
  14.5 1.6 collective-permute-start.9
  16.0 1.7 collective-permute-start.10
  17.8 1.6 collective-permute-start.1
  19.4 1.7 collective-permute-start.2
  21.3 1.9 collective-permute-done.9
  23.6 3.0 %collective-permute-start.12 = (bf16[2,32,1024]{2,1,0:T(8,128)(2,1)S(1)}, bf16[2,32,1024]{2,1,0:T(8,128)(2,1)S(1)}, u32[]{:S(2)}, u32[]{:S(2)}) collective-permute-start(bf16[2,32,1024]{2,1,0:T(8,128)(2,1)S(1)} %slice.225), channel_id=1, source_target_pairs={{0,12},{4,0},{8,4},{12,8},{1,13},{5,1},{9,5},{13,9},{2,14},{6,2},{... | collective-permute-start | bytes 393224 | tf_op jit(solution)/shard_map/ppermute | solution.py:70
  26.7 1.6 collective-permute-start.3
  28.3 1.7 collective-permute-start.4
  30.2 0.9 collective-permute-start.13
  31.2 2.4 %collective-permute-start.14 = (bf16[4,2,32,2048]{3,2,1,0:T(8,128)(2,1)S(1)}, bf16[4,2,32,2048]{3,2,1,0:T(8,128)(2,1)S(1)}, u32[]{:S(2)}, u32[]{:S(2)}) collective-permute-start(bf16[4,2,32,2048]{3,2,1,0:T(8,128)(2,1)S(1)} %fusion.63), channel_id=1, source_target_pairs={{0,3},{1,0},{2,1},{3,2},{4,7},{5,4},{6,5},{7,6},{8,11},{9,8},{10,9... | collective-permute-start | bytes 3145736 | tf_op jit(solution)/shard_map/ppermute | solution.py:80
  33.5 0.8 collective-permute-done.3
  34.9 3.2 %collective-permute-start.6 = (bf16[4,2,32,2048]{3,2,1,0:T(8,128)(2,1)S(1)}, bf16[4,2,32,2048]{3,2,1,0:T(8,128)(2,1)S(1)}, u32[]{:S(2)}, u32[]{:S(2)}) collective-permute-start(bf16[4,2,32,2048]{3,2,1,0:T(8,128)(2,1)S(1)} %fusion.62), channel_id=1, source_target_pairs={{0,12},{4,0},{8,4},{12,8},{1,13},{5,1},{9,5},{13,9},{2,14},{6,2},{... | collective-permute-start | bytes 3145736 | tf_op jit(solution)/shard_map/ppermute | solution.py:80
  38.1 0.7 fusion.21
  40.1 0.7 fusion.29
  41.2 14.2 %collective-permute-done.13 = bf16[4,2,32,2048]{3,2,1,0:T(8,128)(2,1)S(1)} collective-permute-done((bf16[4,2,32,2048]{3,2,1,0:T(8,128)(2,1)S(1)}, bf16[4,2,32,2048]{3,2,1,0:T(8,128)(2,1)S(1)}, u32[]{:S(2)}, u32[]{:S(2)}) %collective-permute-start.13) | collective-permute-done | bytes 1048608 | tf_op jit(solution)/shard_map/ppermute | solution.py:79
  55.5 3.3 %collective-permute-start.16 = (bf16[4,2,32,1024]{3,2,1,0:T(8,128)(2,1)S(1)}, bf16[4,2,32,1024]{3,2,1,0:T(8,128)(2,1)S(1)}, u32[]{:S(2)}, u32[]{:S(2)}) collective-permute-start(bf16[4,2,32,1024]{3,2,1,0:T(8,128)(2,1)S(1)} %slice.227), channel_id=1, source_target_pairs={{0,3},{1,0},{2,1},{3,2},{4,7},{5,4},{6,5},{7,6},{8,11},{9,8},{10,9... | collective-permute-start | bytes 1572872 | tf_op jit(solution)/shard_map/ppermute | solution.py:86
  59.0 3.5 %collective-permute-start.8 = (bf16[4,2,32,1024]{3,2,1,0:T(8,128)(2,1)S(1)}, bf16[4,2,32,1024]{3,2,1,0:T(8,128)(2,1)S(1)}, u32[]{:S(2)}, u32[]{:S(2)}) collective-permute-start(bf16[4,2,32,1024]{3,2,1,0:T(8,128)(2,1)S(1)} %slice.222), channel_id=1, source_target_pairs={{0,12},{4,0},{8,4},{12,8},{1,13},{5,1},{9,5},{13,9},{2,14},{6,2},{... | collective-permute-start | bytes 1572872 | tf_op jit(solution)/shard_map/ppermute | solution.py:86
  62.5 0.7 fusion.19
  63.6 0.7 fusion.17
  64.8 0.7 fusion.27
  67.4 1.1 collective-permute-done.15
  68.5 2.9 %collective-permute-done.7 = bf16[4,2,32,1024]{3,2,1,0:T(8,128)(2,1)S(1)} collective-permute-done((bf16[4,2,32,1024]{3,2,1,0:T(8,128)(2,1)S(1)}, bf16[4,2,32,1024]{3,2,1,0:T(8,128)(2,1)S(1)}, u32[]{:S(2)}, u32[]{:S(2)}) %collective-permute-start.7) | collective-permute-done | bytes 524320 | tf_op jit(solution)/shard_map/ppermute | solution.py:85
  71.9 0.7 fusion.15
  72.7 0.7 fusion.23
  74.0 1.6 add_convert_fusion
  75.5 5.4 %all-to-all-start = ((bf16[128,8,576]{2,1,0:T(8,128)(2,1)}), bf16[128,8,576]{2,1,0:T(8,128)(2,1)S(1)}, u32[]{:S(2)}, u32[]{:S(2)}) async-start(bf16[128,8,576]{2,1,0:T(8,128)(2,1)} %bitcast.31), calls=%async_computation | async-start | bytes 2621440 | tf_op jit(solution)/shard_map/all_to_all | solution.py:165
  81.2 20.6 %all-to-all-done = bf16[128,8,576]{2,1,0:T(8,128)(2,1)S(1)} async-done(((bf16[128,8,576]{2,1,0:T(8,128)(2,1)}), bf16[128,8,576]{2,1,0:T(8,128)(2,1)S(1)}, u32[]{:S(2)}, u32[]{:S(2)}) %all-to-all-start) | async-done | bytes 1179680 | tf_op jit(solution)/shard_map/all_to_all | solution.py:165
  103.4 3.7 %fusion.132 = (f32[8,8,16]{2,1,0:T(8,128)S(1)}, f32[8,8,16,256]{3,2,1,0:T(8,128)S(1)}) fusion(bf16[8,256,8,128]{3,2,1,0:T(8,128)(2,1)} %param.12, bf16[8,8,16,64]{3,2,1,0:T(8,128)(2,1)S(1)} %bitcast.236, bf16[8,8,16,64]{3,2,1,0:T(8,128)(2,1)S(1)} %bitcast.234, pred[8,256]{1,0:T(8,128)(4,1)S(1)} %iota_compare_fusion), kind=kOutput, calls=%fused_computation.220 | convolution fusion | flops 68418560 | bytes 5511168 | tf_op jit(solution)/shard_map/rgqd,rtgd->rgqt/dot_general | solution.py:39
  107.6 1.0 fusion.56
  108.9 15.5 %all_to_all.25 = bf16[8,32,512]{2,0,1:T(8,128)(2,1)S(1)} all-to-all(bf16[8,32,512]{2,0,1:T(8,128)(2,1)S(1)} %copy.54), channel_id=1, replica_groups=mesh['gx'=4,'zh'=2,'x'=4,'y'=4] {'zh','x','y'}, dimensions={1} | all-to-all | bytes 524288 | tf_op jit(solution)/shard_map/all_to_all | solution.py:172
  124.4 1.7 collective-permute-start.18
  126.3 5.9 %collective-permute-done.17 = bf16[256,512]{1,0:T(8,128)(2,1)S(1)} collective-permute-done((bf16[256,512]{1,0:T(8,128)(2,1)S(1)}, bf16[256,512]{1,0:T(8,128)(2,1)S(1)}, u32[]{:S(2)}, u32[]{:S(2)}) %collective-permute-start.17) | collective-permute-done | bytes 262176 | tf_op jit(solution)/shard_map/ppermute | solution.py:62
  132.3 2.0 collective-permute-start.20
  134.4 2.6 %collective-permute-done.19 = bf16[256,256]{1,0:T(8,128)(2,1)S(1)} collective-permute-done((bf16[256,256]{1,0:T(8,128)(2,1)S(1)}, bf16[256,256]{1,0:T(8,128)(2,1)S(1)}, u32[]{:S(2)}, u32[]{:S(2)}) %collective-permute-start.19) | collective-permute-done | bytes 131104 | tf_op jit(solution)/shard_map/ppermute | solution.py:69
  137.1 2.3 %convolution_convert_fusion.5 = bf16[2,4,32,2048]{3,2,1,0:T(8,128)(2,1)S(1)} fusion(bf16[512,4096]{1,0:T(8,128)(2,1)} %param.15, bf16[2,4,4,32,512]{4,3,2,1,0:T(8,128)(2,1)S(1)} %bitcast.225, s32[]{:T(128)S(6)} %select_n.209), kind=kOutput, calls=%fused_computation.12 | convolution fusion | flops 537395200 | bytes 3407876 | tf_op jit(solution)/shard_map/dot_general | solution.py:178
  139.4 0.7 convolution_convert_fusion.6
  140.1 0.7 convolution_convert_fusion.4
  140.8 0.7 convolution_convert_fusion.1
  141.6 0.7 convolution_convert_fusion.2
  142.4 1.4 collective-permute-start.21
  143.8 0.7 collective-permute-start.23
  144.6 1.6 collective-permute-start.30
  147.4 0.7 convolution_convert_fusion.7
  148.1 9.0 %collective-permute-done.21 = bf16[2,4,32,1024]{3,2,1,0:T(8,128)(2,1)S(1)} collective-permute-done((bf16[2,4,32,1024]{3,2,1,0:T(8,128)(2,1)S(1)}, bf16[2,4,32,1024]{3,2,1,0:T(8,128)(2,1)S(1)}, u32[]{:S(2)}, u32[]{:S(2)}) %collective-permute-start.21) | collective-permute-done | bytes 524320 | tf_op jit(solution)/shard_map/ppermute | solution.py:109
  157.3 2.6 %collective-permute-start.22 = (bf16[2,4,32,2048]{3,2,1,0:T(8,128)(2,1)S(1)}, bf16[2,4,32,2048]{3,2,1,0:T(8,128)(2,1)S(1)}, u32[]{:S(2)}, u32[]{:S(2)}) collective-permute-start(bf16[2,4,32,2048]{3,2,1,0:T(8,128)(2,1)S(1)} %pad_maximum_fusion), channel_id=1, source_target_pairs={{0,3},{1,0},{2,1},{3,2},{4,7},{5,4},{6,5},{7,6},{8,11},{9,8},{10,9... | collective-permute-start | bytes 3145736 | tf_op jit(solution)/shard_map/ppermute | solution.py:115
  160.4 1.6 collective-permute-start.31
  162.7 0.7 convolution_convert_fusion.3
  163.4 19.0 %collective-permute-done.22 = bf16[2,4,32,2048]{3,2,1,0:T(8,128)(2,1)S(1)} collective-permute-done((bf16[2,4,32,2048]{3,2,1,0:T(8,128)(2,1)S(1)}, bf16[2,4,32,2048]{3,2,1,0:T(8,128)(2,1)S(1)}, u32[]{:S(2)}, u32[]{:S(2)}) %collective-permute-start.22) | collective-permute-done | bytes 1048608 | tf_op jit(solution)/shard_map/ppermute | solution.py:115
  182.5 3.6 %collective-permute-done.24 = bf16[2,4,32,2048]{3,2,1,0:T(8,128)(2,1)S(1)} collective-permute-done((bf16[2,4,32,2048]{3,2,1,0:T(8,128)(2,1)S(1)}, bf16[2,4,32,2048]{3,2,1,0:T(8,128)(2,1)S(1)}, u32[]{:S(2)}, u32[]{:S(2)}) %collective-permute-start.24) | collective-permute-done | bytes 1048608 | tf_op jit(solution)/shard_map/ppermute | solution.py:116
  186.4 1.6 collective-permute-start.25
  188.7 2.7 %collective-permute-start.34 = (bf16[2,32,1024]{2,1,0:T(8,128)(2,1)S(1)}, bf16[2,32,1024]{2,1,0:T(8,128)(2,1)S(1)}, u32[]{:S(2)}, u32[]{:S(2)}) collective-permute-start(bf16[2,32,1024]{2,1,0:T(8,128)(2,1)S(1)} %get-tuple-element.35), channel_id=1, source_target_pairs={{0,3},{1,0},{2,1},{3,2},{4,7},{5,4},{6,5},{7,6},{8,11},{9,8},{10,9... | collective-permute-start | bytes 393224 | tf_op jit(solution)/shard_map/ppermute | solution.py:109
  191.5 2.9 %collective-permute-start.26 = (bf16[2,32,2048]{2,1,0:T(8,128)(2,1)S(1)}, bf16[2,32,2048]{2,1,0:T(8,128)(2,1)S(1)}, u32[]{:S(2)}, u32[]{:S(2)}) collective-permute-start(bf16[2,32,2048]{2,1,0:T(8,128)(2,1)S(1)} %pad_maximum_fusion.5), channel_id=1, source_target_pairs={{0,12},{4,0},{8,4},{12,8},{1,13},{5,1},{9,5},{13,9},{2,14},{6,2},{... | collective-permute-start | bytes 786440 | tf_op jit(solution)/shard_map/ppermute | solution.py:115
  194.5 3.2 %collective-permute-start.35 = (bf16[2,32,2048]{2,1,0:T(8,128)(2,1)S(1)}, bf16[2,32,2048]{2,1,0:T(8,128)(2,1)S(1)}, u32[]{:S(2)}, u32[]{:S(2)}) collective-permute-start(bf16[2,32,2048]{2,1,0:T(8,128)(2,1)S(1)} %pad_maximum_fusion.7), channel_id=1, source_target_pairs={{0,3},{1,0},{2,1},{3,2},{4,7},{5,4},{6,5},{7,6},{8,11},{9,8},{10,9... | collective-permute-start | bytes 786440 | tf_op jit(solution)/shard_map/ppermute | solution.py:115
  198.2 3.8 %collective-permute-done.28 = bf16[2,32,2048]{2,1,0:T(8,128)(2,1)S(1)} collective-permute-done((bf16[2,32,2048]{2,1,0:T(8,128)(2,1)S(1)}, bf16[2,32,2048]{2,1,0:T(8,128)(2,1)S(1)}, u32[]{:S(2)}, u32[]{:S(2)}) %collective-permute-start.28) | collective-permute-done | bytes 262176 | tf_op jit(solution)/shard_map/ppermute | solution.py:116
  202.1 3.3 %collective-permute-done.37 = bf16[2,32,2048]{2,1,0:T(8,128)(2,1)S(1)} collective-permute-done((bf16[2,32,2048]{2,1,0:T(8,128)(2,1)S(1)}, bf16[2,32,2048]{2,1,0:T(8,128)(2,1)S(1)}, u32[]{:S(2)}, u32[]{:S(2)}) %collective-permute-start.37) | collective-permute-done | bytes 262176 | tf_op jit(solution)/shard_map/ppermute | solution.py:116
  205.6 3.5 %collective-permute-start.38 = (bf16[32,2048]{1,0:T(8,128)(2,1)S(1)}, bf16[32,2048]{1,0:T(8,128)(2,1)S(1)}, u32[]{:S(2)}, u32[]{:S(2)}) collective-permute-start(bf16[32,2048]{1,0:T(8,128)(2,1)S(1)} %get-tuple-element.49), channel_id=1, source_target_pairs={{0,16},{16,0},{1,17},{17,1},{2,18},{18,2},{3,19},{19,3},{4,20},{20... | collective-permute-start | bytes 393224 | tf_op jit(solution)/shard_map/ppermute | solution.py:106
  209.1 2.9 %collective-permute-done.29 = bf16[32,2048]{1,0:T(8,128)(2,1)S(1)} collective-permute-done((bf16[32,2048]{1,0:T(8,128)(2,1)S(1)}, bf16[32,2048]{1,0:T(8,128)(2,1)S(1)}, u32[]{:S(2)}, u32[]{:S(2)}) %collective-permute-start.29) | collective-permute-done | bytes 131104 | tf_op jit(solution)/shard_map/ppermute | solution.py:106
  212.1 1.4 collective-permute-done.38
  213.5 0.7 pad_maximum_fusion.9
  (153 shorter events, 14.5 us)
Async XLA Ops:
  3.9 10.5 %collective-permute-start = (bf16[32,4096]{1,0:T(8,128)(2,1)S(1)}, bf16[32,4096]{1,0:T(8,128)(2,1)S(1)}, u32[]{:S(2)}, u32[]{:S(2)}) collective-permute-start(bf16[32,4096]{1,0:T(8,128)(2,1)S(1)} %constant_dynamic-slice_fusion), channel_id=1, source_target_pairs={{0,80},{1,81},{2,82},{3,83},{4,84},{5,85},{6,86},{7,87},{8,88},{9,... | collective-permute-start | bytes 786440 | tf_op jit(solution)/shard_map/ppermute | solution.py:140
  14.5 8.8 %collective-permute-start.9 = (bf16[2,32,2048]{2,1,0:T(8,128)(2,1)S(1)}, bf16[2,32,2048]{2,1,0:T(8,128)(2,1)S(1)}, u32[]{:S(2)}, u32[]{:S(2)}) collective-permute-start(bf16[2,32,2048]{2,1,0:T(8,128)(2,1)S(1)} %get-tuple-element.25), channel_id=1, source_target_pairs={{0,4},{4,8},{8,12},{12,0},{1,5},{5,9},{9,13},{13,1},{2,6},{6,10},{... | collective-permute-start | bytes 786440 | tf_op jit(solution)/shard_map/ppermute | solution.py:62
  16.0 7.6 %collective-permute-start.10 = (bf16[2,32,2048]{2,1,0:T(8,128)(2,1)S(1)}, bf16[2,32,2048]{2,1,0:T(8,128)(2,1)S(1)}, u32[]{:S(2)}, u32[]{:S(2)}) collective-permute-start(bf16[2,32,2048]{2,1,0:T(8,128)(2,1)S(1)} %get-tuple-element.25), channel_id=1, source_target_pairs={{0,12},{4,0},{8,4},{12,8},{1,13},{5,1},{9,5},{13,9},{2,14},{6,2},{... | collective-permute-start | bytes 786440 | tf_op jit(solution)/shard_map/ppermute | solution.py:66
  17.8 8.9 %collective-permute-start.1 = (bf16[2,32,2048]{2,1,0:T(8,128)(2,1)S(1)}, bf16[2,32,2048]{2,1,0:T(8,128)(2,1)S(1)}, u32[]{:S(2)}, u32[]{:S(2)}) collective-permute-start(bf16[2,32,2048]{2,1,0:T(8,128)(2,1)S(1)} %get-tuple-element.26), channel_id=1, source_target_pairs={{0,1},{1,2},{2,3},{3,0},{4,5},{5,6},{6,7},{7,4},{8,9},{9,10},{10,1... | collective-permute-start | bytes 786440 | tf_op jit(solution)/shard_map/ppermute | solution.py:62
  19.4 8.9 %collective-permute-start.2 = (bf16[2,32,2048]{2,1,0:T(8,128)(2,1)S(1)}, bf16[2,32,2048]{2,1,0:T(8,128)(2,1)S(1)}, u32[]{:S(2)}, u32[]{:S(2)}) collective-permute-start(bf16[2,32,2048]{2,1,0:T(8,128)(2,1)S(1)} %get-tuple-element.26), channel_id=1, source_target_pairs={{0,3},{1,0},{2,1},{3,2},{4,7},{5,4},{6,5},{7,6},{8,11},{9,8},{10,9... | collective-permute-start | bytes 786440 | tf_op jit(solution)/shard_map/ppermute | solution.py:66
  21.3 16.8 %copy-start.1 = (bf16[4096,512]{1,0:T(8,128)(2,1)S(1)}, bf16[4096,512]{1,0:T(8,128)(2,1)}, u32[]{:S(2)}) copy-start(bf16[4096,512]{1,0:T(8,128)(2,1)} %param.10) | copy-start | bytes 12582916
  23.3 6.9 %collective-permute-start.11 = (bf16[2,32,1024]{2,1,0:T(8,128)(2,1)S(1)}, bf16[2,32,1024]{2,1,0:T(8,128)(2,1)S(1)}, u32[]{:S(2)}, u32[]{:S(2)}) collective-permute-start(bf16[2,32,1024]{2,1,0:T(8,128)(2,1)S(1)} %slice.224), channel_id=1, source_target_pairs={{0,4},{4,8},{8,12},{12,0},{1,5},{5,9},{9,13},{13,1},{2,6},{6,10},{... | collective-permute-start | bytes 393224 | tf_op jit(solution)/shard_map/ppermute | solution.py:69
  23.6 6.6 %collective-permute-start.12 = (bf16[2,32,1024]{2,1,0:T(8,128)(2,1)S(1)}, bf16[2,32,1024]{2,1,0:T(8,128)(2,1)S(1)}, u32[]{:S(2)}, u32[]{:S(2)}) collective-permute-start(bf16[2,32,1024]{2,1,0:T(8,128)(2,1)S(1)} %slice.225), channel_id=1, source_target_pairs={{0,12},{4,0},{8,4},{12,8},{1,13},{5,1},{9,5},{13,9},{2,14},{6,2},{... | collective-permute-start | bytes 393224 | tf_op jit(solution)/shard_map/ppermute | solution.py:70
  26.7 7.6 %collective-permute-start.3 = (bf16[2,32,1024]{2,1,0:T(8,128)(2,1)S(1)}, bf16[2,32,1024]{2,1,0:T(8,128)(2,1)S(1)}, u32[]{:S(2)}, u32[]{:S(2)}) collective-permute-start(bf16[2,32,1024]{2,1,0:T(8,128)(2,1)S(1)} %slice.219), channel_id=1, source_target_pairs={{0,1},{1,2},{2,3},{3,0},{4,5},{5,6},{6,7},{7,4},{8,9},{9,10},{10,1... | collective-permute-start | bytes 393224 | tf_op jit(solution)/shard_map/ppermute | solution.py:69
  28.3 6.4 %collective-permute-start.4 = (bf16[2,32,1024]{2,1,0:T(8,128)(2,1)S(1)}, bf16[2,32,1024]{2,1,0:T(8,128)(2,1)S(1)}, u32[]{:S(2)}, u32[]{:S(2)}) collective-permute-start(bf16[2,32,1024]{2,1,0:T(8,128)(2,1)S(1)} %slice.220), channel_id=1, source_target_pairs={{0,3},{1,0},{2,1},{3,2},{4,7},{5,4},{6,5},{7,6},{8,11},{9,8},{10,9... | collective-permute-start | bytes 393224 | tf_op jit(solution)/shard_map/ppermute | solution.py:70
  30.2 8.6 %copy-start.4 = (bf16[4096,64]{0,1:T(8,128)(2,1)S(1)}, bf16[4096,64]{0,1:T(8,128)(2,1)}, u32[]{:S(2)}) copy-start(bf16[4096,64]{0,1:T(8,128)(2,1)} %param.11) | copy-start | bytes 1572868
  30.2 25.1 %collective-permute-start.13 = (bf16[4,2,32,2048]{3,2,1,0:T(8,128)(2,1)S(1)}, bf16[4,2,32,2048]{3,2,1,0:T(8,128)(2,1)S(1)}, u32[]{:S(2)}, u32[]{:S(2)}) collective-permute-start(bf16[4,2,32,2048]{3,2,1,0:T(8,128)(2,1)S(1)} %fusion.63), channel_id=1, source_target_pairs={{0,1},{1,2},{2,3},{3,0},{4,5},{5,6},{6,7},{7,4},{8,9},{9,10},{10,1... | collective-permute-start | bytes 3145736 | tf_op jit(solution)/shard_map/ppermute | solution.py:79
  31.2 24.3 %collective-permute-start.14 = (bf16[4,2,32,2048]{3,2,1,0:T(8,128)(2,1)S(1)}, bf16[4,2,32,2048]{3,2,1,0:T(8,128)(2,1)S(1)}, u32[]{:S(2)}, u32[]{:S(2)}) collective-permute-start(bf16[4,2,32,2048]{3,2,1,0:T(8,128)(2,1)S(1)} %fusion.63), channel_id=1, source_target_pairs={{0,3},{1,0},{2,1},{3,2},{4,7},{5,4},{6,5},{7,6},{8,11},{9,8},{10,9... | collective-permute-start | bytes 3145736 | tf_op jit(solution)/shard_map/ppermute | solution.py:80
  34.8 24.0 %collective-permute-start.5 = (bf16[4,2,32,2048]{3,2,1,0:T(8,128)(2,1)S(1)}, bf16[4,2,32,2048]{3,2,1,0:T(8,128)(2,1)S(1)}, u32[]{:S(2)}, u32[]{:S(2)}) collective-permute-start(bf16[4,2,32,2048]{3,2,1,0:T(8,128)(2,1)S(1)} %fusion.62), channel_id=1, source_target_pairs={{0,4},{4,8},{8,12},{12,0},{1,5},{5,9},{9,13},{13,1},{2,6},{6,10},{... | collective-permute-start | bytes 3145736 | tf_op jit(solution)/shard_map/ppermute | solution.py:79
  34.9 24.1 %collective-permute-start.6 = (bf16[4,2,32,2048]{3,2,1,0:T(8,128)(2,1)S(1)}, bf16[4,2,32,2048]{3,2,1,0:T(8,128)(2,1)S(1)}, u32[]{:S(2)}, u32[]{:S(2)}) collective-permute-start(bf16[4,2,32,2048]{3,2,1,0:T(8,128)(2,1)S(1)} %fusion.62), channel_id=1, source_target_pairs={{0,12},{4,0},{8,4},{12,8},{1,13},{5,1},{9,5},{13,9},{2,14},{6,2},{... | collective-permute-start | bytes 3145736 | tf_op jit(solution)/shard_map/ppermute | solution.py:80
  55.4 13.0 %collective-permute-start.15 = (bf16[4,2,32,1024]{3,2,1,0:T(8,128)(2,1)S(1)}, bf16[4,2,32,1024]{3,2,1,0:T(8,128)(2,1)S(1)}, u32[]{:S(2)}, u32[]{:S(2)}) collective-permute-start(bf16[4,2,32,1024]{3,2,1,0:T(8,128)(2,1)S(1)} %slice.226), channel_id=1, source_target_pairs={{0,1},{1,2},{2,3},{3,0},{4,5},{5,6},{6,7},{7,4},{8,9},{9,10},{10,1... | collective-permute-start | bytes 1572872 | tf_op jit(solution)/shard_map/ppermute | solution.py:85
  55.5 15.8 %collective-permute-start.16 = (bf16[4,2,32,1024]{3,2,1,0:T(8,128)(2,1)S(1)}, bf16[4,2,32,1024]{3,2,1,0:T(8,128)(2,1)S(1)}, u32[]{:S(2)}, u32[]{:S(2)}) collective-permute-start(bf16[4,2,32,1024]{3,2,1,0:T(8,128)(2,1)S(1)} %slice.227), channel_id=1, source_target_pairs={{0,3},{1,0},{2,1},{3,2},{4,7},{5,4},{6,5},{7,6},{8,11},{9,8},{10,9... | collective-permute-start | bytes 1572872 | tf_op jit(solution)/shard_map/ppermute | solution.py:86
  58.9 12.5 %collective-permute-start.7 = (bf16[4,2,32,1024]{3,2,1,0:T(8,128)(2,1)S(1)}, bf16[4,2,32,1024]{3,2,1,0:T(8,128)(2,1)S(1)}, u32[]{:S(2)}, u32[]{:S(2)}) collective-permute-start(bf16[4,2,32,1024]{3,2,1,0:T(8,128)(2,1)S(1)} %slice.221), channel_id=1, source_target_pairs={{0,4},{4,8},{8,12},{12,0},{1,5},{5,9},{9,13},{13,1},{2,6},{6,10},{... | collective-permute-start | bytes 1572872 | tf_op jit(solution)/shard_map/ppermute | solution.py:85
  59.0 13.6 %collective-permute-start.8 = (bf16[4,2,32,1024]{3,2,1,0:T(8,128)(2,1)S(1)}, bf16[4,2,32,1024]{3,2,1,0:T(8,128)(2,1)S(1)}, u32[]{:S(2)}, u32[]{:S(2)}) collective-permute-start(bf16[4,2,32,1024]{3,2,1,0:T(8,128)(2,1)S(1)} %slice.222), channel_id=1, source_target_pairs={{0,12},{4,0},{8,4},{12,8},{1,13},{5,1},{9,5},{13,9},{2,14},{6,2},{... | collective-permute-start | bytes 1572872 | tf_op jit(solution)/shard_map/ppermute | solution.py:86
  75.5 5.5 %copy-start = (s32[8]{0:T(128)S(1)}, s32[8]{0:T(128)}, u32[]{:S(2)}) copy-start(s32[8]{0:T(128)} %param.14) | copy-start | bytes 100
  75.5 26.2 %all-to-all-start = ((bf16[128,8,576]{2,1,0:T(8,128)(2,1)}), bf16[128,8,576]{2,1,0:T(8,128)(2,1)S(1)}, u32[]{:S(2)}, u32[]{:S(2)}) async-start(bf16[128,8,576]{2,1,0:T(8,128)(2,1)} %bitcast.31), calls=%async_computation | async-start | bytes 2621440 | tf_op jit(solution)/shard_map/all_to_all | solution.py:165
  103.4 4.1 %copy-start.2 = (bf16[8,256,8,128]{3,2,1,0:T(8,128)(2,1)S(1)}, bf16[8,256,8,128]{3,2,1,0:T(8,128)(2,1)}, u32[]{:S(2)}) copy-start(bf16[8,256,8,128]{3,2,1,0:T(8,128)(2,1)} %param.13) | copy-start | bytes 12582916
  124.4 7.8 %collective-permute-start.17 = (bf16[256,512]{1,0:T(8,128)(2,1)S(1)}, bf16[256,512]{1,0:T(8,128)(2,1)S(1)}, u32[]{:S(2)}, u32[]{:S(2)}) collective-permute-start(bf16[256,512]{1,0:T(8,128)(2,1)S(1)} %bitcast.223), channel_id=1, source_target_pairs={{0,32},{32,64},{64,96},{96,0},{1,33},{33,65},{65,97},{97,1},{2,34}... | collective-permute-start | bytes 786440 | tf_op jit(solution)/shard_map/ppermute | solution.py:62
  124.4 7.9 %collective-permute-start.18 = (bf16[256,512]{1,0:T(8,128)(2,1)S(1)}, bf16[256,512]{1,0:T(8,128)(2,1)S(1)}, u32[]{:S(2)}, u32[]{:S(2)}) collective-permute-start(bf16[256,512]{1,0:T(8,128)(2,1)S(1)} %bitcast.224), channel_id=1, source_target_pairs={{0,96},{32,0},{64,32},{96,64},{1,97},{33,1},{65,33},{97,65},{2,98}... | collective-permute-start | bytes 786440 | tf_op jit(solution)/shard_map/ppermute | solution.py:66
  132.2 4.8 %collective-permute-start.19 = (bf16[256,256]{1,0:T(8,128)(2,1)S(1)}, bf16[256,256]{1,0:T(8,128)(2,1)S(1)}, u32[]{:S(2)}, u32[]{:S(2)}) collective-permute-start(bf16[256,256]{1,0:T(8,128)(2,1)S(1)} %slice.236), channel_id=1, source_target_pairs={{0,32},{32,64},{64,96},{96,0},{1,33},{33,65},{65,97},{97,1},{2,34}... | collective-permute-start | bytes 393224 | tf_op jit(solution)/shard_map/ppermute | solution.py:69
  132.3 7.1 %copy-start.3 = (bf16[512,4096]{1,0:T(8,128)(2,1)S(1)}, bf16[512,4096]{1,0:T(8,128)(2,1)}, u32[]{:S(2)}) copy-start(bf16[512,4096]{1,0:T(8,128)(2,1)} %param.15) | copy-start | bytes 12582916
  132.3 4.7 %collective-permute-start.20 = (bf16[256,256]{1,0:T(8,128)(2,1)S(1)}, bf16[256,256]{1,0:T(8,128)(2,1)S(1)}, u32[]{:S(2)}, u32[]{:S(2)}) collective-permute-start(bf16[256,256]{1,0:T(8,128)(2,1)S(1)} %slice.237), channel_id=1, source_target_pairs={{0,96},{32,0},{64,32},{96,64},{1,97},{33,1},{65,33},{97,65},{2,98}... | collective-permute-start | bytes 393224 | tf_op jit(solution)/shard_map/ppermute | solution.py:70
  142.4 14.8 %collective-permute-start.21 = (bf16[2,4,32,1024]{3,2,1,0:T(8,128)(2,1)S(1)}, bf16[2,4,32,1024]{3,2,1,0:T(8,128)(2,1)S(1)}, u32[]{:S(2)}, u32[]{:S(2)}) collective-permute-start(bf16[2,4,32,1024]{3,2,1,0:T(8,128)(2,1)S(1)} %get-tuple-element.10), channel_id=1, source_target_pairs={{0,3},{1,0},{2,1},{3,2},{4,7},{5,4},{6,5},{7,6},{8,11},{9,8},{10,9... | collective-permute-start | bytes 1572872 | tf_op jit(solution)/shard_map/ppermute | solution.py:109
  143.8 16.1 %collective-permute-start.23 = (bf16[2,4,32,1024]{3,2,1,0:T(8,128)(2,1)S(1)}, bf16[2,4,32,1024]{3,2,1,0:T(8,128)(2,1)S(1)}, u32[]{:S(2)}, u32[]{:S(2)}) collective-permute-start(bf16[2,4,32,1024]{3,2,1,0:T(8,128)(2,1)S(1)} %get-tuple-element.11), channel_id=1, source_target_pairs={{0,1},{1,2},{2,3},{3,0},{4,5},{5,6},{6,7},{7,4},{8,9},{9,10},{10,1... | collective-permute-start | bytes 1572872 | tf_op jit(solution)/shard_map/ppermute | solution.py:110
  144.6 15.6 %collective-permute-start.30 = (bf16[2,4,32,1024]{3,2,1,0:T(8,128)(2,1)S(1)}, bf16[2,4,32,1024]{3,2,1,0:T(8,128)(2,1)S(1)}, u32[]{:S(2)}, u32[]{:S(2)}) collective-permute-start(bf16[2,4,32,1024]{3,2,1,0:T(8,128)(2,1)S(1)} %get-tuple-element.19), channel_id=1, source_target_pairs={{0,12},{4,0},{8,4},{12,8},{1,13},{5,1},{9,5},{13,9},{2,14},{6,2},{... | collective-permute-start | bytes 1572872 | tf_op jit(solution)/shard_map/ppermute | solution.py:109
  146.2 15.8 %collective-permute-start.32 = (bf16[2,4,32,1024]{3,2,1,0:T(8,128)(2,1)S(1)}, bf16[2,4,32,1024]{3,2,1,0:T(8,128)(2,1)S(1)}, u32[]{:S(2)}, u32[]{:S(2)}) collective-permute-start(bf16[2,4,32,1024]{3,2,1,0:T(8,128)(2,1)S(1)} %get-tuple-element.20), channel_id=1, source_target_pairs={{0,4},{4,8},{8,12},{12,0},{1,5},{5,9},{9,13},{13,1},{2,6},{6,10},{... | collective-permute-start | bytes 1572872 | tf_op jit(solution)/shard_map/ppermute | solution.py:110
  157.3 25.1 %collective-permute-start.22 = (bf16[2,4,32,2048]{3,2,1,0:T(8,128)(2,1)S(1)}, bf16[2,4,32,2048]{3,2,1,0:T(8,128)(2,1)S(1)}, u32[]{:S(2)}, u32[]{:S(2)}) collective-permute-start(bf16[2,4,32,2048]{3,2,1,0:T(8,128)(2,1)S(1)} %pad_maximum_fusion), channel_id=1, source_target_pairs={{0,3},{1,0},{2,1},{3,2},{4,7},{5,4},{6,5},{7,6},{8,11},{9,8},{10,9... | collective-permute-start | bytes 3145736 | tf_op jit(solution)/shard_map/ppermute | solution.py:115
  160.1 26.0 %collective-permute-start.24 = (bf16[2,4,32,2048]{3,2,1,0:T(8,128)(2,1)S(1)}, bf16[2,4,32,2048]{3,2,1,0:T(8,128)(2,1)S(1)}, u32[]{:S(2)}, u32[]{:S(2)}) collective-permute-start(bf16[2,4,32,2048]{3,2,1,0:T(8,128)(2,1)S(1)} %pad_maximum_fusion.1), channel_id=1, source_target_pairs={{0,1},{1,2},{2,3},{3,0},{4,5},{5,6},{6,7},{7,4},{8,9},{9,10},{10,1... | collective-permute-start | bytes 3145736 | tf_op jit(solution)/shard_map/ppermute | solution.py:116
  160.4 28.1 %collective-permute-start.31 = (bf16[2,4,32,2048]{3,2,1,0:T(8,128)(2,1)S(1)}, bf16[2,4,32,2048]{3,2,1,0:T(8,128)(2,1)S(1)}, u32[]{:S(2)}, u32[]{:S(2)}) collective-permute-start(bf16[2,4,32,2048]{3,2,1,0:T(8,128)(2,1)S(1)} %pad_maximum_fusion.2), channel_id=1, source_target_pairs={{0,12},{4,0},{8,4},{12,8},{1,13},{5,1},{9,5},{13,9},{2,14},{6,2},{... | collective-permute-start | bytes 3145736 | tf_op jit(solution)/shard_map/ppermute | solution.py:115
  162.2 26.3 %collective-permute-start.33 = (bf16[2,4,32,2048]{3,2,1,0:T(8,128)(2,1)S(1)}, bf16[2,4,32,2048]{3,2,1,0:T(8,128)(2,1)S(1)}, u32[]{:S(2)}, u32[]{:S(2)}) collective-permute-start(bf16[2,4,32,2048]{3,2,1,0:T(8,128)(2,1)S(1)} %pad_maximum_fusion.3), channel_id=1, source_target_pairs={{0,4},{4,8},{8,12},{12,0},{1,5},{5,9},{9,13},{13,1},{2,6},{6,10},{... | collective-permute-start | bytes 3145736 | tf_op jit(solution)/shard_map/ppermute | solution.py:116
  186.4 5.0 %collective-permute-start.25 = (bf16[2,32,1024]{2,1,0:T(8,128)(2,1)S(1)}, bf16[2,32,1024]{2,1,0:T(8,128)(2,1)S(1)}, u32[]{:S(2)}, u32[]{:S(2)}) collective-permute-start(bf16[2,32,1024]{2,1,0:T(8,128)(2,1)S(1)} %get-tuple-element.29), channel_id=1, source_target_pairs={{0,12},{4,0},{8,4},{12,8},{1,13},{5,1},{9,5},{13,9},{2,14},{6,2},{... | collective-permute-start | bytes 393224 | tf_op jit(solution)/shard_map/ppermute | solution.py:109
  188.0 6.3 %collective-permute-start.27 = (bf16[2,32,1024]{2,1,0:T(8,128)(2,1)S(1)}, bf16[2,32,1024]{2,1,0:T(8,128)(2,1)S(1)}, u32[]{:S(2)}, u32[]{:S(2)}) collective-permute-start(bf16[2,32,1024]{2,1,0:T(8,128)(2,1)S(1)} %get-tuple-element.30), channel_id=1, source_target_pairs={{0,4},{4,8},{8,12},{12,0},{1,5},{5,9},{9,13},{13,1},{2,6},{6,10},{... | collective-permute-start | bytes 393224 | tf_op jit(solution)/shard_map/ppermute | solution.py:110
  188.7 5.7 %collective-permute-start.34 = (bf16[2,32,1024]{2,1,0:T(8,128)(2,1)S(1)}, bf16[2,32,1024]{2,1,0:T(8,128)(2,1)S(1)}, u32[]{:S(2)}, u32[]{:S(2)}) collective-permute-start(bf16[2,32,1024]{2,1,0:T(8,128)(2,1)S(1)} %get-tuple-element.35), channel_id=1, source_target_pairs={{0,3},{1,0},{2,1},{3,2},{4,7},{5,4},{6,5},{7,6},{8,11},{9,8},{10,9... | collective-permute-start | bytes 393224 | tf_op jit(solution)/shard_map/ppermute | solution.py:109
  191.4 6.3 %collective-permute-start.36 = (bf16[2,32,1024]{2,1,0:T(8,128)(2,1)S(1)}, bf16[2,32,1024]{2,1,0:T(8,128)(2,1)S(1)}, u32[]{:S(2)}, u32[]{:S(2)}) collective-permute-start(bf16[2,32,1024]{2,1,0:T(8,128)(2,1)S(1)} %get-tuple-element.36), channel_id=1, source_target_pairs={{0,1},{1,2},{2,3},{3,0},{4,5},{5,6},{6,7},{7,4},{8,9},{9,10},{10,1... | collective-permute-start | bytes 393224 | tf_op jit(solution)/shard_map/ppermute | solution.py:110
  191.5 6.7 %collective-permute-start.26 = (bf16[2,32,2048]{2,1,0:T(8,128)(2,1)S(1)}, bf16[2,32,2048]{2,1,0:T(8,128)(2,1)S(1)}, u32[]{:S(2)}, u32[]{:S(2)}) collective-permute-start(bf16[2,32,2048]{2,1,0:T(8,128)(2,1)S(1)} %pad_maximum_fusion.5), channel_id=1, source_target_pairs={{0,12},{4,0},{8,4},{12,8},{1,13},{5,1},{9,5},{13,9},{2,14},{6,2},{... | collective-permute-start | bytes 786440 | tf_op jit(solution)/shard_map/ppermute | solution.py:115
  194.4 7.7 %collective-permute-start.28 = (bf16[2,32,2048]{2,1,0:T(8,128)(2,1)S(1)}, bf16[2,32,2048]{2,1,0:T(8,128)(2,1)S(1)}, u32[]{:S(2)}, u32[]{:S(2)}) collective-permute-start(bf16[2,32,2048]{2,1,0:T(8,128)(2,1)S(1)} %pad_maximum_fusion.6), channel_id=1, source_target_pairs={{0,4},{4,8},{8,12},{12,0},{1,5},{5,9},{9,13},{13,1},{2,6},{6,10},{... | collective-permute-start | bytes 786440 | tf_op jit(solution)/shard_map/ppermute | solution.py:116
  194.5 7.5 %collective-permute-start.35 = (bf16[2,32,2048]{2,1,0:T(8,128)(2,1)S(1)}, bf16[2,32,2048]{2,1,0:T(8,128)(2,1)S(1)}, u32[]{:S(2)}, u32[]{:S(2)}) collective-permute-start(bf16[2,32,2048]{2,1,0:T(8,128)(2,1)S(1)} %pad_maximum_fusion.7), channel_id=1, source_target_pairs={{0,3},{1,0},{2,1},{3,2},{4,7},{5,4},{6,5},{7,6},{8,11},{9,8},{10,9... | collective-permute-start | bytes 786440 | tf_op jit(solution)/shard_map/ppermute | solution.py:115
  197.7 7.7 %collective-permute-start.37 = (bf16[2,32,2048]{2,1,0:T(8,128)(2,1)S(1)}, bf16[2,32,2048]{2,1,0:T(8,128)(2,1)S(1)}, u32[]{:S(2)}, u32[]{:S(2)}) collective-permute-start(bf16[2,32,2048]{2,1,0:T(8,128)(2,1)S(1)} %pad_maximum_fusion.8), channel_id=1, source_target_pairs={{0,1},{1,2},{2,3},{3,0},{4,5},{5,6},{6,7},{7,4},{8,9},{9,10},{10,1... | collective-permute-start | bytes 786440 | tf_op jit(solution)/shard_map/ppermute | solution.py:116
  205.5 6.6 %collective-permute-start.29 = (bf16[32,2048]{1,0:T(8,128)(2,1)S(1)}, bf16[32,2048]{1,0:T(8,128)(2,1)S(1)}, u32[]{:S(2)}, u32[]{:S(2)}) collective-permute-start(bf16[32,2048]{1,0:T(8,128)(2,1)S(1)} %get-tuple-element.50), channel_id=1, source_target_pairs={{0,16},{16,0},{1,17},{17,1},{2,18},{18,2},{3,19},{19,3},{4,20},{20... | collective-permute-start | bytes 393224 | tf_op jit(solution)/shard_map/ppermute | solution.py:106
  205.6 7.8 %collective-permute-start.38 = (bf16[32,2048]{1,0:T(8,128)(2,1)S(1)}, bf16[32,2048]{1,0:T(8,128)(2,1)S(1)}, u32[]{:S(2)}, u32[]{:S(2)}) collective-permute-start(bf16[32,2048]{1,0:T(8,128)(2,1)S(1)} %get-tuple-element.49), channel_id=1, source_target_pairs={{0,16},{16,0},{1,17},{17,1},{2,18},{18,2},{3,19},{19,3},{4,20},{20... | collective-permute-start | bytes 393224 | tf_op jit(solution)/shard_map/ppermute | solution.py:106

commit v6 on v5

--- a/solution.py
+++ b/solution.py
@@ -72,6 +72,16 @@
     return lax.dynamic_update_index_in_dim(out, opposite, (idx + 2) % n, dim)
 
 
+def direct_all_gather(blk, axis, n, dim):
+    idx = lax.axis_index(axis)
+    out = jnp.zeros(blk.shape[:dim] + (n,) + blk.shape[dim:], blk.dtype)
+    out = lax.dynamic_update_index_in_dim(out, blk, idx, dim)
+    for d in range(1, n):
+        got = lax.ppermute(blk, axis, [(i, (i + d) % n) for i in range(n)])
+        out = lax.dynamic_update_index_in_dim(out, got, (idx - d) % n, dim)
+    return out
+
+
 def ring_all_gather_apply(blk, axis, n, dim, fn):
     idx = lax.axis_index(axis)
     fwd = [(i, (i + 1) % n) for i in range(n)]
@@ -170,7 +180,7 @@
     keyval = split_cols[:, :, query_cols:].reshape(rows_dev, peers * pair_cols)
     attended = attend_rows(query, keyval, key_cache, value_cache, lengths)
     by_heads = lax.all_to_all(attended, GY, split_axis=1, concat_axis=0, tiled=True)
-    full_rows = ring_all_gather(by_heads, "gx", 4, 0).reshape(-1, query_cols)
+    full_rows = direct_all_gather(by_heads, "gx", 4, 0).reshape(-1, query_cols)
     cols = w_out.shape[1]
     by_row = full_rows.reshape(2, 4, 4, rows_dev * 4, query_cols)
 

time: 215 us -> 214 us (level)
    ppermute x0 -> x3, waiting for transfers between devices: none -> 10.1 us  [direct_all_gather(): got = lax.ppermute(blk, axis, [(i, (i + d) % n) for i in range(n)])]
    ppermute x3 -> x2, waiting for transfers between devices: 7.83 us -> 1.9 us  [ring_all_gather(): from_left = lax.ppermute(blk, axis, fwd)]
    ppermute x3 -> x2, waiting for transfers between devices: 3.4 us -> 0.77 us  [ring_all_gather(): first = lax.ppermute(from_left[..., :half], axis, fwd)]
    ppermute x3 -> x2, starting transfers between devices: 6.76 us -> 4.75 us  [ring_all_gather(): second = lax.ppermute(from_right[..., half:], axis, bwd)]
    ppermute x3 -> x2, starting transfers between devices: 5.15 us -> 3.41 us  [ring_all_gather(): from_right = lax.ppermute(blk, axis, bwd)]
  transfers between devices with their start and end apart: 40 -> 39, of which waited for: 18 -> 20; matrix products, arithmetic and copies ran while one was open for 6% -> 6% of each run, Pallas kernels for 0% -> 0%
where the time goes in v6:
time: 214 us
  waiting for transfers between devices  102 us (48%)
  starting transfers between devices  62 us (29%)
  matrix products  21.4 us (10%)
  blocking collectives  15.5 us (7%)
  other arithmetic  9.39 us (4%)
  local copies, waits for them, and re-layouts  2.78 us (1%)
    ppermute x4, waiting for transfers between devices, ring_reduce_scatter(): got_right = lax.ppermute(to_left, axis, bwd)  21.1 us
    all_to_all x1, waiting for transfers between devices, shards(): lax.all_to_all(projected.astype(jnp.bfloat16), ALL, split_axis=0, concat_...  20.6 us
    all_to_all x1, blocking collectives, shards(): lax.all_to_all(attended, GY, split_axis=1, concat_axis=0, tiled=True)  15.5 us
    ppermute x2, waiting for transfers between devices, ring_all_gather_apply(): from_left = lax.ppermute(blk, axis, fwd)  14.2 us
    ppermute x4, starting transfers between devices, ring_reduce_scatter(): got_right = lax.ppermute(to_left, axis, bwd)  10.7 us
    ppermute x3, waiting for transfers between devices, direct_all_gather(): got = lax.ppermute(blk, axis, [(i, (i + d) % n) for i in range(n)])  10.1 us
    ppermute x4, waiting for transfers between devices, ring_reduce_scatter(): got_left = lax.ppermute(to_right, axis, fwd)  9.69 us
    ppermute x4, waiting for transfers between devices, ring_reduce_scatter(): from_right = lax.ppermute(opposite[..., :half], axis, bwd)  8.6 us
  transfers between devices with their start and end apart: 39, of which 20 were waited for; matrix products, arithmetic and copies ran while one was open for 6% of the time, Pallas kernels for 0%

profile of v6, /device:TPU:0, one launch (start us, length us, event | category | flops | bytes accessed | tf_op | source)
XLA Modules:
  0.0 214.0 jit_solution(2304659158645518319)
XLA Ops:
  0.0 0.8 convert_element_type.87
  0.8 1.5 fusion.4
  2.3 1.5 fusion.6
  3.9 4.2 %collective-permute-start = (bf16[32,4096]{1,0:T(8,128)(2,1)S(1)}, bf16[32,4096]{1,0:T(8,128)(2,1)S(1)}, u32[]{:S(2)}, u32[]{:S(2)}) collective-permute-start(bf16[32,4096]{1,0:T(8,128)(2,1)S(1)} %constant_dynamic-slice_fusion), channel_id=1, source_target_pairs={{0,80},{1,81},{2,82},{3,83},{4,84},{5,85},{6,86},{7,87},{8,88},{9,... | collective-permute-start | bytes 786440 | tf_op jit(solution)/shard_map/ppermute | solution.py:150
  8.2 6.2 %collective-permute-done = bf16[32,4096]{1,0:T(8,128)(2,1)S(1)} collective-permute-done((bf16[32,4096]{1,0:T(8,128)(2,1)S(1)}, bf16[32,4096]{1,0:T(8,128)(2,1)S(1)}, u32[]{:S(2)}, u32[]{:S(2)}) %collective-permute-start) | collective-permute-done | bytes 262176 | tf_op jit(solution)/shard_map/ppermute | solution.py:150
  14.5 1.6 collective-permute-start.9
  16.0 1.7 collective-permute-start.10
  17.8 1.6 collective-permute-start.1
  19.4 1.7 collective-permute-start.2
  21.3 1.9 collective-permute-done.9
  23.6 3.0 %collective-permute-start.12 = (bf16[2,32,1024]{2,1,0:T(8,128)(2,1)S(1)}, bf16[2,32,1024]{2,1,0:T(8,128)(2,1)S(1)}, u32[]{:S(2)}, u32[]{:S(2)}) collective-permute-start(bf16[2,32,1024]{2,1,0:T(8,128)(2,1)S(1)} %slice.217), channel_id=1, source_target_pairs={{0,12},{4,0},{8,4},{12,8},{1,13},{5,1},{9,5},{13,9},{2,14},{6,2},{... | collective-permute-start | bytes 393224 | tf_op jit(solution)/shard_map/ppermute | solution.py:70
  26.7 1.6 collective-permute-start.3
  28.3 1.7 collective-permute-start.4
  30.2 0.9 collective-permute-start.13
  31.2 2.4 %collective-permute-start.14 = (bf16[4,2,32,2048]{3,2,1,0:T(8,128)(2,1)S(1)}, bf16[4,2,32,2048]{3,2,1,0:T(8,128)(2,1)S(1)}, u32[]{:S(2)}, u32[]{:S(2)}) collective-permute-start(bf16[4,2,32,2048]{3,2,1,0:T(8,128)(2,1)S(1)} %fusion.63), channel_id=1, source_target_pairs={{0,3},{1,0},{2,1},{3,2},{4,7},{5,4},{6,5},{7,6},{8,11},{9,8},{10,9... | collective-permute-start | bytes 3145736 | tf_op jit(solution)/shard_map/ppermute | solution.py:90
  33.5 0.8 collective-permute-done.3
  34.9 3.2 %collective-permute-start.6 = (bf16[4,2,32,2048]{3,2,1,0:T(8,128)(2,1)S(1)}, bf16[4,2,32,2048]{3,2,1,0:T(8,128)(2,1)S(1)}, u32[]{:S(2)}, u32[]{:S(2)}) collective-permute-start(bf16[4,2,32,2048]{3,2,1,0:T(8,128)(2,1)S(1)} %fusion.62), channel_id=1, source_target_pairs={{0,12},{4,0},{8,4},{12,8},{1,13},{5,1},{9,5},{13,9},{2,14},{6,2},{... | collective-permute-start | bytes 3145736 | tf_op jit(solution)/shard_map/ppermute | solution.py:90
  38.1 0.7 fusion.21
  40.1 0.7 fusion.29
  41.2 14.2 %collective-permute-done.13 = bf16[4,2,32,2048]{3,2,1,0:T(8,128)(2,1)S(1)} collective-permute-done((bf16[4,2,32,2048]{3,2,1,0:T(8,128)(2,1)S(1)}, bf16[4,2,32,2048]{3,2,1,0:T(8,128)(2,1)S(1)}, u32[]{:S(2)}, u32[]{:S(2)}) %collective-permute-start.13) | collective-permute-done | bytes 1048608 | tf_op jit(solution)/shard_map/ppermute | solution.py:89
  55.5 3.3 %collective-permute-start.16 = (bf16[4,2,32,1024]{3,2,1,0:T(8,128)(2,1)S(1)}, bf16[4,2,32,1024]{3,2,1,0:T(8,128)(2,1)S(1)}, u32[]{:S(2)}, u32[]{:S(2)}) collective-permute-start(bf16[4,2,32,1024]{3,2,1,0:T(8,128)(2,1)S(1)} %slice.219), channel_id=1, source_target_pairs={{0,3},{1,0},{2,1},{3,2},{4,7},{5,4},{6,5},{7,6},{8,11},{9,8},{10,9... | collective-permute-start | bytes 1572872 | tf_op jit(solution)/shard_map/ppermute | solution.py:96
  59.0 3.5 %collective-permute-start.8 = (bf16[4,2,32,1024]{3,2,1,0:T(8,128)(2,1)S(1)}, bf16[4,2,32,1024]{3,2,1,0:T(8,128)(2,1)S(1)}, u32[]{:S(2)}, u32[]{:S(2)}) collective-permute-start(bf16[4,2,32,1024]{3,2,1,0:T(8,128)(2,1)S(1)} %slice.214), channel_id=1, source_target_pairs={{0,12},{4,0},{8,4},{12,8},{1,13},{5,1},{9,5},{13,9},{2,14},{6,2},{... | collective-permute-start | bytes 1572872 | tf_op jit(solution)/shard_map/ppermute | solution.py:96
  62.5 0.7 fusion.19
  63.6 0.7 fusion.17
  64.8 0.7 fusion.27
  67.4 1.1 collective-permute-done.15
  68.5 2.9 %collective-permute-done.7 = bf16[4,2,32,1024]{3,2,1,0:T(8,128)(2,1)S(1)} collective-permute-done((bf16[4,2,32,1024]{3,2,1,0:T(8,128)(2,1)S(1)}, bf16[4,2,32,1024]{3,2,1,0:T(8,128)(2,1)S(1)}, u32[]{:S(2)}, u32[]{:S(2)}) %collective-permute-start.7) | collective-permute-done | bytes 524320 | tf_op jit(solution)/shard_map/ppermute | solution.py:95
  71.9 0.7 fusion.15
  72.7 0.7 fusion.23
  74.0 1.6 add_convert_fusion
  75.5 5.4 %all-to-all-start = ((bf16[128,8,576]{2,1,0:T(8,128)(2,1)}), bf16[128,8,576]{2,1,0:T(8,128)(2,1)S(1)}, u32[]{:S(2)}, u32[]{:S(2)}) async-start(bf16[128,8,576]{2,1,0:T(8,128)(2,1)} %bitcast.31), calls=%async_computation | async-start | bytes 2621440 | tf_op jit(solution)/shard_map/all_to_all | solution.py:175
  81.2 20.6 %all-to-all-done = bf16[128,8,576]{2,1,0:T(8,128)(2,1)S(1)} async-done(((bf16[128,8,576]{2,1,0:T(8,128)(2,1)}), bf16[128,8,576]{2,1,0:T(8,128)(2,1)S(1)}, u32[]{:S(2)}, u32[]{:S(2)}) %all-to-all-start) | async-done | bytes 1179680 | tf_op jit(solution)/shard_map/all_to_all | solution.py:175
  103.4 3.7 %fusion.131 = (f32[8,8,16]{2,1,0:T(8,128)S(1)}, f32[8,8,16,256]{3,2,1,0:T(8,128)S(1)}) fusion(bf16[8,256,8,128]{3,2,1,0:T(8,128)(2,1)} %param.12, bf16[8,8,16,64]{3,2,1,0:T(8,128)(2,1)S(1)} %bitcast.235, bf16[8,8,16,64]{3,2,1,0:T(8,128)(2,1)S(1)} %bitcast.233, pred[8,256]{1,0:T(8,128)(4,1)S(1)} %iota_compare_fusion), kind=kOutput, calls=%fused_computation.219 | convolution fusion | flops 68418560 | bytes 5511168 | tf_op jit(solution)/shard_map/rgqd,rtgd->rgqt/dot_general | solution.py:39
  107.6 1.0 fusion.56
  108.9 15.5 %all_to_all.25 = bf16[8,32,512]{2,0,1:T(8,128)(2,1)S(1)} all-to-all(bf16[8,32,512]{2,0,1:T(8,128)(2,1)S(1)} %copy.54), channel_id=1, replica_groups=mesh['gx'=4,'zh'=2,'x'=4,'y'=4] {'zh','x','y'}, dimensions={1} | all-to-all | bytes 524288 | tf_op jit(solution)/shard_map/all_to_all | solution.py:182
  124.9 1.5 collective-permute-start.19
  126.5 5.9 %collective-permute-done.17 = bf16[256,512]{1,0:T(8,128)(2,1)S(1)} collective-permute-done((bf16[256,512]{1,0:T(8,128)(2,1)S(1)}, bf16[256,512]{1,0:T(8,128)(2,1)S(1)}, u32[]{:S(2)}, u32[]{:S(2)}) %collective-permute-start.17) | collective-permute-done | bytes 262176 | tf_op jit(solution)/shard_map/ppermute | solution.py:80
  132.5 1.1 collective-permute-done.18
  133.6 3.0 %collective-permute-done.19 = bf16[256,512]{1,0:T(8,128)(2,1)S(1)} collective-permute-done((bf16[256,512]{1,0:T(8,128)(2,1)S(1)}, bf16[256,512]{1,0:T(8,128)(2,1)S(1)}, u32[]{:S(2)}, u32[]{:S(2)}) %collective-permute-start.19) | collective-permute-done | bytes 262176 | tf_op jit(solution)/shard_map/ppermute | solution.py:80
  136.7 2.3 %convolution_convert_fusion.5 = bf16[2,4,32,2048]{3,2,1,0:T(8,128)(2,1)S(1)} fusion(bf16[512,4096]{1,0:T(8,128)(2,1)} %param.15, bf16[2,4,4,32,512]{4,3,2,1,0:T(8,128)(2,1)S(1)} %bitcast.224, s32[]{:T(128)S(6)} %select_n.211), kind=kOutput, calls=%fused_computation.12 | convolution fusion | flops 537395200 | bytes 3407876 | tf_op jit(solution)/shard_map/dot_general | solution.py:188
  139.7 0.7 convolution_convert_fusion.4
  140.4 0.7 convolution_convert_fusion.1
  141.2 0.7 convolution_convert_fusion.2
  142.0 1.3 collective-permute-start.20
  143.3 0.8 collective-permute-start.22
  144.2 1.5 collective-permute-start.29
  147.7 8.3 %collective-permute-done.20 = bf16[2,4,32,1024]{3,2,1,0:T(8,128)(2,1)S(1)} collective-permute-done((bf16[2,4,32,1024]{3,2,1,0:T(8,128)(2,1)S(1)}, bf16[2,4,32,1024]{3,2,1,0:T(8,128)(2,1)S(1)}, u32[]{:S(2)}, u32[]{:S(2)}) %collective-permute-start.20) | collective-permute-done | bytes 524320 | tf_op jit(solution)/shard_map/ppermute | solution.py:119
  156.2 2.5 %collective-permute-start.21 = (bf16[2,4,32,2048]{3,2,1,0:T(8,128)(2,1)S(1)}, bf16[2,4,32,2048]{3,2,1,0:T(8,128)(2,1)S(1)}, u32[]{:S(2)}, u32[]{:S(2)}) collective-permute-start(bf16[2,4,32,2048]{3,2,1,0:T(8,128)(2,1)S(1)} %pad_maximum_fusion), channel_id=1, source_target_pairs={{0,3},{1,0},{2,1},{3,2},{4,7},{5,4},{6,5},{7,6},{8,11},{9,8},{10,9... | collective-permute-start | bytes 3145736 | tf_op jit(solution)/shard_map/ppermute | solution.py:125
  159.2 2.5 %collective-permute-start.30 = (bf16[2,4,32,2048]{3,2,1,0:T(8,128)(2,1)S(1)}, bf16[2,4,32,2048]{3,2,1,0:T(8,128)(2,1)S(1)}, u32[]{:S(2)}, u32[]{:S(2)}) collective-permute-start(bf16[2,4,32,2048]{3,2,1,0:T(8,128)(2,1)S(1)} %pad_maximum_fusion.2), channel_id=1, source_target_pairs={{0,12},{4,0},{8,4},{12,8},{1,13},{5,1},{9,5},{13,9},{2,14},{6,2},{... | collective-permute-start | bytes 3145736 | tf_op jit(solution)/shard_map/ppermute | solution.py:125
  161.9 0.7 convolution_convert_fusion.3
  162.6 19.6 %collective-permute-done.21 = bf16[2,4,32,2048]{3,2,1,0:T(8,128)(2,1)S(1)} collective-permute-done((bf16[2,4,32,2048]{3,2,1,0:T(8,128)(2,1)S(1)}, bf16[2,4,32,2048]{3,2,1,0:T(8,128)(2,1)S(1)}, u32[]{:S(2)}, u32[]{:S(2)}) %collective-permute-start.21) | collective-permute-done | bytes 1048608 | tf_op jit(solution)/shard_map/ppermute | solution.py:125
  182.3 3.6 %collective-permute-done.23 = bf16[2,4,32,2048]{3,2,1,0:T(8,128)(2,1)S(1)} collective-permute-done((bf16[2,4,32,2048]{3,2,1,0:T(8,128)(2,1)S(1)}, bf16[2,4,32,2048]{3,2,1,0:T(8,128)(2,1)S(1)}, u32[]{:S(2)}, u32[]{:S(2)}) %collective-permute-start.23) | collective-permute-done | bytes 1048608 | tf_op jit(solution)/shard_map/ppermute | solution.py:126
  186.2 1.6 collective-permute-start.24
  188.6 2.7 %collective-permute-start.33 = (bf16[2,32,1024]{2,1,0:T(8,128)(2,1)S(1)}, bf16[2,32,1024]{2,1,0:T(8,128)(2,1)S(1)}, u32[]{:S(2)}, u32[]{:S(2)}) collective-permute-start(bf16[2,32,1024]{2,1,0:T(8,128)(2,1)S(1)} %get-tuple-element.35), channel_id=1, source_target_pairs={{0,3},{1,0},{2,1},{3,2},{4,7},{5,4},{6,5},{7,6},{8,11},{9,8},{10,9... | collective-permute-start | bytes 393224 | tf_op jit(solution)/shard_map/ppermute | solution.py:119
  191.5 2.9 %collective-permute-start.25 = (bf16[2,32,2048]{2,1,0:T(8,128)(2,1)S(1)}, bf16[2,32,2048]{2,1,0:T(8,128)(2,1)S(1)}, u32[]{:S(2)}, u32[]{:S(2)}) collective-permute-start(bf16[2,32,2048]{2,1,0:T(8,128)(2,1)S(1)} %pad_maximum_fusion.5), channel_id=1, source_target_pairs={{0,12},{4,0},{8,4},{12,8},{1,13},{5,1},{9,5},{13,9},{2,14},{6,2},{... | collective-permute-start | bytes 786440 | tf_op jit(solution)/shard_map/ppermute | solution.py:125
  194.6 2.9 %collective-permute-start.34 = (bf16[2,32,2048]{2,1,0:T(8,128)(2,1)S(1)}, bf16[2,32,2048]{2,1,0:T(8,128)(2,1)S(1)}, u32[]{:S(2)}, u32[]{:S(2)}) collective-permute-start(bf16[2,32,2048]{2,1,0:T(8,128)(2,1)S(1)} %pad_maximum_fusion.7), channel_id=1, source_target_pairs={{0,3},{1,0},{2,1},{3,2},{4,7},{5,4},{6,5},{7,6},{8,11},{9,8},{10,9... | collective-permute-start | bytes 786440 | tf_op jit(solution)/shard_map/ppermute | solution.py:125
  197.7 1.5 collective-permute-done.25
  199.1 3.5 %collective-permute-done.27 = bf16[2,32,2048]{2,1,0:T(8,128)(2,1)S(1)} collective-permute-done((bf16[2,32,2048]{2,1,0:T(8,128)(2,1)S(1)}, bf16[2,32,2048]{2,1,0:T(8,128)(2,1)S(1)}, u32[]{:S(2)}, u32[]{:S(2)}) %collective-permute-start.27) | collective-permute-done | bytes 262176 | tf_op jit(solution)/shard_map/ppermute | solution.py:126
  202.7 2.5 %collective-permute-done.36 = bf16[2,32,2048]{2,1,0:T(8,128)(2,1)S(1)} collective-permute-done((bf16[2,32,2048]{2,1,0:T(8,128)(2,1)S(1)}, bf16[2,32,2048]{2,1,0:T(8,128)(2,1)S(1)}, u32[]{:S(2)}, u32[]{:S(2)}) %collective-permute-start.36) | collective-permute-done | bytes 262176 | tf_op jit(solution)/shard_map/ppermute | solution.py:126
  205.3 1.0 collective-permute-start.28
  206.3 2.6 %collective-permute-start.37 = (bf16[32,2048]{1,0:T(8,128)(2,1)S(1)}, bf16[32,2048]{1,0:T(8,128)(2,1)S(1)}, u32[]{:S(2)}, u32[]{:S(2)}) collective-permute-start(bf16[32,2048]{1,0:T(8,128)(2,1)S(1)} %get-tuple-element.49), channel_id=1, source_target_pairs={{0,16},{16,0},{1,17},{17,1},{2,18},{18,2},{3,19},{19,3},{4,20},{20... | collective-permute-start | bytes 393224 | tf_op jit(solution)/shard_map/ppermute | solution.py:116
  208.9 2.9 %collective-permute-done.28 = bf16[32,2048]{1,0:T(8,128)(2,1)S(1)} collective-permute-done((bf16[32,2048]{1,0:T(8,128)(2,1)S(1)}, bf16[32,2048]{1,0:T(8,128)(2,1)S(1)}, u32[]{:S(2)}, u32[]{:S(2)}) %collective-permute-start.28) | collective-permute-done | bytes 131104 | tf_op jit(solution)/shard_map/ppermute | solution.py:116
  211.9 1.4 collective-permute-done.37
  213.3 0.7 pad_maximum_fusion.9
  (149 shorter events, 15.8 us)
Async XLA Ops:
  3.9 10.5 %collective-permute-start = (bf16[32,4096]{1,0:T(8,128)(2,1)S(1)}, bf16[32,4096]{1,0:T(8,128)(2,1)S(1)}, u32[]{:S(2)}, u32[]{:S(2)}) collective-permute-start(bf16[32,4096]{1,0:T(8,128)(2,1)S(1)} %constant_dynamic-slice_fusion), channel_id=1, source_target_pairs={{0,80},{1,81},{2,82},{3,83},{4,84},{5,85},{6,86},{7,87},{8,88},{9,... | collective-permute-start | bytes 786440 | tf_op jit(solution)/shard_map/ppermute | solution.py:150
  14.5 8.8 %collective-permute-start.9 = (bf16[2,32,2048]{2,1,0:T(8,128)(2,1)S(1)}, bf16[2,32,2048]{2,1,0:T(8,128)(2,1)S(1)}, u32[]{:S(2)}, u32[]{:S(2)}) collective-permute-start(bf16[2,32,2048]{2,1,0:T(8,128)(2,1)S(1)} %get-tuple-element.25), channel_id=1, source_target_pairs={{0,4},{4,8},{8,12},{12,0},{1,5},{5,9},{9,13},{13,1},{2,6},{6,10},{... | collective-permute-start | bytes 786440 | tf_op jit(solution)/shard_map/ppermute | solution.py:62
  16.0 7.6 %collective-permute-start.10 = (bf16[2,32,2048]{2,1,0:T(8,128)(2,1)S(1)}, bf16[2,32,2048]{2,1,0:T(8,128)(2,1)S(1)}, u32[]{:S(2)}, u32[]{:S(2)}) collective-permute-start(bf16[2,32,2048]{2,1,0:T(8,128)(2,1)S(1)} %get-tuple-element.25), channel_id=1, source_target_pairs={{0,12},{4,0},{8,4},{12,8},{1,13},{5,1},{9,5},{13,9},{2,14},{6,2},{... | collective-permute-start | bytes 786440 | tf_op jit(solution)/shard_map/ppermute | solution.py:66
  17.8 8.9 %collective-permute-start.1 = (bf16[2,32,2048]{2,1,0:T(8,128)(2,1)S(1)}, bf16[2,32,2048]{2,1,0:T(8,128)(2,1)S(1)}, u32[]{:S(2)}, u32[]{:S(2)}) collective-permute-start(bf16[2,32,2048]{2,1,0:T(8,128)(2,1)S(1)} %get-tuple-element.26), channel_id=1, source_target_pairs={{0,1},{1,2},{2,3},{3,0},{4,5},{5,6},{6,7},{7,4},{8,9},{9,10},{10,1... | collective-permute-start | bytes 786440 | tf_op jit(solution)/shard_map/ppermute | solution.py:62
  19.4 8.9 %collective-permute-start.2 = (bf16[2,32,2048]{2,1,0:T(8,128)(2,1)S(1)}, bf16[2,32,2048]{2,1,0:T(8,128)(2,1)S(1)}, u32[]{:S(2)}, u32[]{:S(2)}) collective-permute-start(bf16[2,32,2048]{2,1,0:T(8,128)(2,1)S(1)} %get-tuple-element.26), channel_id=1, source_target_pairs={{0,3},{1,0},{2,1},{3,2},{4,7},{5,4},{6,5},{7,6},{8,11},{9,8},{10,9... | collective-permute-start | bytes 786440 | tf_op jit(solution)/shard_map/ppermute | solution.py:66
  21.3 16.8 %copy-start.1 = (bf16[4096,512]{1,0:T(8,128)(2,1)S(1)}, bf16[4096,512]{1,0:T(8,128)(2,1)}, u32[]{:S(2)}) copy-start(bf16[4096,512]{1,0:T(8,128)(2,1)} %param.10) | copy-start | bytes 12582916
  23.3 6.9 %collective-permute-start.11 = (bf16[2,32,1024]{2,1,0:T(8,128)(2,1)S(1)}, bf16[2,32,1024]{2,1,0:T(8,128)(2,1)S(1)}, u32[]{:S(2)}, u32[]{:S(2)}) collective-permute-start(bf16[2,32,1024]{2,1,0:T(8,128)(2,1)S(1)} %slice.216), channel_id=1, source_target_pairs={{0,4},{4,8},{8,12},{12,0},{1,5},{5,9},{9,13},{13,1},{2,6},{6,10},{... | collective-permute-start | bytes 393224 | tf_op jit(solution)/shard_map/ppermute | solution.py:69
  23.6 6.6 %collective-permute-start.12 = (bf16[2,32,1024]{2,1,0:T(8,128)(2,1)S(1)}, bf16[2,32,1024]{2,1,0:T(8,128)(2,1)S(1)}, u32[]{:S(2)}, u32[]{:S(2)}) collective-permute-start(bf16[2,32,1024]{2,1,0:T(8,128)(2,1)S(1)} %slice.217), channel_id=1, source_target_pairs={{0,12},{4,0},{8,4},{12,8},{1,13},{5,1},{9,5},{13,9},{2,14},{6,2},{... | collective-permute-start | bytes 393224 | tf_op jit(solution)/shard_map/ppermute | solution.py:70
  26.7 7.6 %collective-permute-start.3 = (bf16[2,32,1024]{2,1,0:T(8,128)(2,1)S(1)}, bf16[2,32,1024]{2,1,0:T(8,128)(2,1)S(1)}, u32[]{:S(2)}, u32[]{:S(2)}) collective-permute-start(bf16[2,32,1024]{2,1,0:T(8,128)(2,1)S(1)} %slice.211), channel_id=1, source_target_pairs={{0,1},{1,2},{2,3},{3,0},{4,5},{5,6},{6,7},{7,4},{8,9},{9,10},{10,1... | collective-permute-start | bytes 393224 | tf_op jit(solution)/shard_map/ppermute | solution.py:69
  28.3 6.4 %collective-permute-start.4 = (bf16[2,32,1024]{2,1,0:T(8,128)(2,1)S(1)}, bf16[2,32,1024]{2,1,0:T(8,128)(2,1)S(1)}, u32[]{:S(2)}, u32[]{:S(2)}) collective-permute-start(bf16[2,32,1024]{2,1,0:T(8,128)(2,1)S(1)} %slice.212), channel_id=1, source_target_pairs={{0,3},{1,0},{2,1},{3,2},{4,7},{5,4},{6,5},{7,6},{8,11},{9,8},{10,9... | collective-permute-start | bytes 393224 | tf_op jit(solution)/shard_map/ppermute | solution.py:70
  30.2 8.6 %copy-start.4 = (bf16[4096,64]{0,1:T(8,128)(2,1)S(1)}, bf16[4096,64]{0,1:T(8,128)(2,1)}, u32[]{:S(2)}) copy-start(bf16[4096,64]{0,1:T(8,128)(2,1)} %param.11) | copy-start | bytes 1572868
  30.2 25.1 %collective-permute-start.13 = (bf16[4,2,32,2048]{3,2,1,0:T(8,128)(2,1)S(1)}, bf16[4,2,32,2048]{3,2,1,0:T(8,128)(2,1)S(1)}, u32[]{:S(2)}, u32[]{:S(2)}) collective-permute-start(bf16[4,2,32,2048]{3,2,1,0:T(8,128)(2,1)S(1)} %fusion.63), channel_id=1, source_target_pairs={{0,1},{1,2},{2,3},{3,0},{4,5},{5,6},{6,7},{7,4},{8,9},{9,10},{10,1... | collective-permute-start | bytes 3145736 | tf_op jit(solution)/shard_map/ppermute | solution.py:89
  31.2 24.3 %collective-permute-start.14 = (bf16[4,2,32,2048]{3,2,1,0:T(8,128)(2,1)S(1)}, bf16[4,2,32,2048]{3,2,1,0:T(8,128)(2,1)S(1)}, u32[]{:S(2)}, u32[]{:S(2)}) collective-permute-start(bf16[4,2,32,2048]{3,2,1,0:T(8,128)(2,1)S(1)} %fusion.63), channel_id=1, source_target_pairs={{0,3},{1,0},{2,1},{3,2},{4,7},{5,4},{6,5},{7,6},{8,11},{9,8},{10,9... | collective-permute-start | bytes 3145736 | tf_op jit(solution)/shard_map/ppermute | solution.py:90
  34.8 24.0 %collective-permute-start.5 = (bf16[4,2,32,2048]{3,2,1,0:T(8,128)(2,1)S(1)}, bf16[4,2,32,2048]{3,2,1,0:T(8,128)(2,1)S(1)}, u32[]{:S(2)}, u32[]{:S(2)}) collective-permute-start(bf16[4,2,32,2048]{3,2,1,0:T(8,128)(2,1)S(1)} %fusion.62), channel_id=1, source_target_pairs={{0,4},{4,8},{8,12},{12,0},{1,5},{5,9},{9,13},{13,1},{2,6},{6,10},{... | collective-permute-start | bytes 3145736 | tf_op jit(solution)/shard_map/ppermute | solution.py:89
  34.9 24.1 %collective-permute-start.6 = (bf16[4,2,32,2048]{3,2,1,0:T(8,128)(2,1)S(1)}, bf16[4,2,32,2048]{3,2,1,0:T(8,128)(2,1)S(1)}, u32[]{:S(2)}, u32[]{:S(2)}) collective-permute-start(bf16[4,2,32,2048]{3,2,1,0:T(8,128)(2,1)S(1)} %fusion.62), channel_id=1, source_target_pairs={{0,12},{4,0},{8,4},{12,8},{1,13},{5,1},{9,5},{13,9},{2,14},{6,2},{... | collective-permute-start | bytes 3145736 | tf_op jit(solution)/shard_map/ppermute | solution.py:90
  55.4 13.0 %collective-permute-start.15 = (bf16[4,2,32,1024]{3,2,1,0:T(8,128)(2,1)S(1)}, bf16[4,2,32,1024]{3,2,1,0:T(8,128)(2,1)S(1)}, u32[]{:S(2)}, u32[]{:S(2)}) collective-permute-start(bf16[4,2,32,1024]{3,2,1,0:T(8,128)(2,1)S(1)} %slice.218), channel_id=1, source_target_pairs={{0,1},{1,2},{2,3},{3,0},{4,5},{5,6},{6,7},{7,4},{8,9},{9,10},{10,1... | collective-permute-start | bytes 1572872 | tf_op jit(solution)/shard_map/ppermute | solution.py:95
  55.5 15.8 %collective-permute-start.16 = (bf16[4,2,32,1024]{3,2,1,0:T(8,128)(2,1)S(1)}, bf16[4,2,32,1024]{3,2,1,0:T(8,128)(2,1)S(1)}, u32[]{:S(2)}, u32[]{:S(2)}) collective-permute-start(bf16[4,2,32,1024]{3,2,1,0:T(8,128)(2,1)S(1)} %slice.219), channel_id=1, source_target_pairs={{0,3},{1,0},{2,1},{3,2},{4,7},{5,4},{6,5},{7,6},{8,11},{9,8},{10,9... | collective-permute-start | bytes 1572872 | tf_op jit(solution)/shard_map/ppermute | solution.py:96
  58.9 12.5 %collective-permute-start.7 = (bf16[4,2,32,1024]{3,2,1,0:T(8,128)(2,1)S(1)}, bf16[4,2,32,1024]{3,2,1,0:T(8,128)(2,1)S(1)}, u32[]{:S(2)}, u32[]{:S(2)}) collective-permute-start(bf16[4,2,32,1024]{3,2,1,0:T(8,128)(2,1)S(1)} %slice.213), channel_id=1, source_target_pairs={{0,4},{4,8},{8,12},{12,0},{1,5},{5,9},{9,13},{13,1},{2,6},{6,10},{... | collective-permute-start | bytes 1572872 | tf_op jit(solution)/shard_map/ppermute | solution.py:95
  59.0 13.6 %collective-permute-start.8 = (bf16[4,2,32,1024]{3,2,1,0:T(8,128)(2,1)S(1)}, bf16[4,2,32,1024]{3,2,1,0:T(8,128)(2,1)S(1)}, u32[]{:S(2)}, u32[]{:S(2)}) collective-permute-start(bf16[4,2,32,1024]{3,2,1,0:T(8,128)(2,1)S(1)} %slice.214), channel_id=1, source_target_pairs={{0,12},{4,0},{8,4},{12,8},{1,13},{5,1},{9,5},{13,9},{2,14},{6,2},{... | collective-permute-start | bytes 1572872 | tf_op jit(solution)/shard_map/ppermute | solution.py:96
  75.5 5.5 %copy-start = (s32[8]{0:T(128)S(1)}, s32[8]{0:T(128)}, u32[]{:S(2)}) copy-start(s32[8]{0:T(128)} %param.14) | copy-start | bytes 100
  75.5 26.2 %all-to-all-start = ((bf16[128,8,576]{2,1,0:T(8,128)(2,1)}), bf16[128,8,576]{2,1,0:T(8,128)(2,1)S(1)}, u32[]{:S(2)}, u32[]{:S(2)}) async-start(bf16[128,8,576]{2,1,0:T(8,128)(2,1)} %bitcast.31), calls=%async_computation | async-start | bytes 2621440 | tf_op jit(solution)/shard_map/all_to_all | solution.py:175
  103.4 4.1 %copy-start.2 = (bf16[8,256,8,128]{3,2,1,0:T(8,128)(2,1)S(1)}, bf16[8,256,8,128]{3,2,1,0:T(8,128)(2,1)}, u32[]{:S(2)}) copy-start(bf16[8,256,8,128]{3,2,1,0:T(8,128)(2,1)} %param.13) | copy-start | bytes 12582916
  124.4 8.0 %collective-permute-start.17 = (bf16[256,512]{1,0:T(8,128)(2,1)S(1)}, bf16[256,512]{1,0:T(8,128)(2,1)S(1)}, u32[]{:S(2)}, u32[]{:S(2)}) collective-permute-start(bf16[256,512]{1,0:T(8,128)(2,1)S(1)} %bitcast.221), channel_id=1, source_target_pairs={{0,32},{32,64},{64,96},{96,0},{1,33},{33,65},{65,97},{97,1},{2,34}... | collective-permute-start | bytes 786440 | tf_op jit(solution)/shard_map/ppermute | solution.py:80
  124.4 9.2 %collective-permute-start.18 = (bf16[256,512]{1,0:T(8,128)(2,1)S(1)}, bf16[256,512]{1,0:T(8,128)(2,1)S(1)}, u32[]{:S(2)}, u32[]{:S(2)}) collective-permute-start(bf16[256,512]{1,0:T(8,128)(2,1)S(1)} %bitcast.222), channel_id=1, source_target_pairs={{0,64},{32,96},{64,0},{96,32},{1,65},{33,97},{65,1},{97,33},{2,66}... | collective-permute-start | bytes 786440 | tf_op jit(solution)/shard_map/ppermute | solution.py:80
  124.9 11.7 %collective-permute-start.19 = (bf16[256,512]{1,0:T(8,128)(2,1)S(1)}, bf16[256,512]{1,0:T(8,128)(2,1)S(1)}, u32[]{:S(2)}, u32[]{:S(2)}) collective-permute-start(bf16[256,512]{1,0:T(8,128)(2,1)S(1)} %bitcast.223), channel_id=1, source_target_pairs={{0,96},{32,0},{64,32},{96,64},{1,97},{33,1},{65,33},{97,65},{2,98}... | collective-permute-start | bytes 786440 | tf_op jit(solution)/shard_map/ppermute | solution.py:80
  126.5 12.5 %copy-start.3 = (bf16[512,4096]{1,0:T(8,128)(2,1)S(1)}, bf16[512,4096]{1,0:T(8,128)(2,1)}, u32[]{:S(2)}) copy-start(bf16[512,4096]{1,0:T(8,128)(2,1)} %param.15) | copy-start | bytes 12582916
  142.0 14.0 %collective-permute-start.20 = (bf16[2,4,32,1024]{3,2,1,0:T(8,128)(2,1)S(1)}, bf16[2,4,32,1024]{3,2,1,0:T(8,128)(2,1)S(1)}, u32[]{:S(2)}, u32[]{:S(2)}) collective-permute-start(bf16[2,4,32,1024]{3,2,1,0:T(8,128)(2,1)S(1)} %get-tuple-element.10), channel_id=1, source_target_pairs={{0,3},{1,0},{2,1},{3,2},{4,7},{5,4},{6,5},{7,6},{8,11},{9,8},{10,9... | collective-permute-start | bytes 1572872 | tf_op jit(solution)/shard_map/ppermute | solution.py:119
  143.3 15.4 %collective-permute-start.22 = (bf16[2,4,32,1024]{3,2,1,0:T(8,128)(2,1)S(1)}, bf16[2,4,32,1024]{3,2,1,0:T(8,128)(2,1)S(1)}, u32[]{:S(2)}, u32[]{:S(2)}) collective-permute-start(bf16[2,4,32,1024]{3,2,1,0:T(8,128)(2,1)S(1)} %get-tuple-element.11), channel_id=1, source_target_pairs={{0,1},{1,2},{2,3},{3,0},{4,5},{5,6},{6,7},{7,4},{8,9},{9,10},{10,1... | collective-permute-start | bytes 1572872 | tf_op jit(solution)/shard_map/ppermute | solution.py:120
  144.2 14.8 %collective-permute-start.29 = (bf16[2,4,32,1024]{3,2,1,0:T(8,128)(2,1)S(1)}, bf16[2,4,32,1024]{3,2,1,0:T(8,128)(2,1)S(1)}, u32[]{:S(2)}, u32[]{:S(2)}) collective-permute-start(bf16[2,4,32,1024]{3,2,1,0:T(8,128)(2,1)S(1)} %get-tuple-element.19), channel_id=1, source_target_pairs={{0,12},{4,0},{8,4},{12,8},{1,13},{5,1},{9,5},{13,9},{2,14},{6,2},{... | collective-permute-start | bytes 1572872 | tf_op jit(solution)/shard_map/ppermute | solution.py:119
  145.7 16.0 %collective-permute-start.31 = (bf16[2,4,32,1024]{3,2,1,0:T(8,128)(2,1)S(1)}, bf16[2,4,32,1024]{3,2,1,0:T(8,128)(2,1)S(1)}, u32[]{:S(2)}, u32[]{:S(2)}) collective-permute-start(bf16[2,4,32,1024]{3,2,1,0:T(8,128)(2,1)S(1)} %get-tuple-element.20), channel_id=1, source_target_pairs={{0,4},{4,8},{8,12},{12,0},{1,5},{5,9},{9,13},{13,1},{2,6},{6,10},{... | collective-permute-start | bytes 1572872 | tf_op jit(solution)/shard_map/ppermute | solution.py:120
  156.2 26.1 %collective-permute-start.21 = (bf16[2,4,32,2048]{3,2,1,0:T(8,128)(2,1)S(1)}, bf16[2,4,32,2048]{3,2,1,0:T(8,128)(2,1)S(1)}, u32[]{:S(2)}, u32[]{:S(2)}) collective-permute-start(bf16[2,4,32,2048]{3,2,1,0:T(8,128)(2,1)S(1)} %pad_maximum_fusion), channel_id=1, source_target_pairs={{0,3},{1,0},{2,1},{3,2},{4,7},{5,4},{6,5},{7,6},{8,11},{9,8},{10,9... | collective-permute-start | bytes 3145736 | tf_op jit(solution)/shard_map/ppermute | solution.py:125
  158.9 27.0 %collective-permute-start.23 = (bf16[2,4,32,2048]{3,2,1,0:T(8,128)(2,1)S(1)}, bf16[2,4,32,2048]{3,2,1,0:T(8,128)(2,1)S(1)}, u32[]{:S(2)}, u32[]{:S(2)}) collective-permute-start(bf16[2,4,32,2048]{3,2,1,0:T(8,128)(2,1)S(1)} %pad_maximum_fusion.1), channel_id=1, source_target_pairs={{0,1},{1,2},{2,3},{3,0},{4,5},{5,6},{6,7},{7,4},{8,9},{9,10},{10,1... | collective-permute-start | bytes 3145736 | tf_op jit(solution)/shard_map/ppermute | solution.py:126
  159.2 29.1 %collective-permute-start.30 = (bf16[2,4,32,2048]{3,2,1,0:T(8,128)(2,1)S(1)}, bf16[2,4,32,2048]{3,2,1,0:T(8,128)(2,1)S(1)}, u32[]{:S(2)}, u32[]{:S(2)}) collective-permute-start(bf16[2,4,32,2048]{3,2,1,0:T(8,128)(2,1)S(1)} %pad_maximum_fusion.2), channel_id=1, source_target_pairs={{0,12},{4,0},{8,4},{12,8},{1,13},{5,1},{9,5},{13,9},{2,14},{6,2},{... | collective-permute-start | bytes 3145736 | tf_op jit(solution)/shard_map/ppermute | solution.py:125
  161.8 26.5 %collective-permute-start.32 = (bf16[2,4,32,2048]{3,2,1,0:T(8,128)(2,1)S(1)}, bf16[2,4,32,2048]{3,2,1,0:T(8,128)(2,1)S(1)}, u32[]{:S(2)}, u32[]{:S(2)}) collective-permute-start(bf16[2,4,32,2048]{3,2,1,0:T(8,128)(2,1)S(1)} %pad_maximum_fusion.3), channel_id=1, source_target_pairs={{0,4},{4,8},{8,12},{12,0},{1,5},{5,9},{9,13},{13,1},{2,6},{6,10},{... | collective-permute-start | bytes 3145736 | tf_op jit(solution)/shard_map/ppermute | solution.py:126
  186.2 5.3 %collective-permute-start.24 = (bf16[2,32,1024]{2,1,0:T(8,128)(2,1)S(1)}, bf16[2,32,1024]{2,1,0:T(8,128)(2,1)S(1)}, u32[]{:S(2)}, u32[]{:S(2)}) collective-permute-start(bf16[2,32,1024]{2,1,0:T(8,128)(2,1)S(1)} %get-tuple-element.29), channel_id=1, source_target_pairs={{0,12},{4,0},{8,4},{12,8},{1,13},{5,1},{9,5},{13,9},{2,14},{6,2},{... | collective-permute-start | bytes 393224 | tf_op jit(solution)/shard_map/ppermute | solution.py:119
  187.8 6.6 %collective-permute-start.26 = (bf16[2,32,1024]{2,1,0:T(8,128)(2,1)S(1)}, bf16[2,32,1024]{2,1,0:T(8,128)(2,1)S(1)}, u32[]{:S(2)}, u32[]{:S(2)}) collective-permute-start(bf16[2,32,1024]{2,1,0:T(8,128)(2,1)S(1)} %get-tuple-element.30), channel_id=1, source_target_pairs={{0,4},{4,8},{8,12},{12,0},{1,5},{5,9},{9,13},{13,1},{2,6},{6,10},{... | collective-permute-start | bytes 393224 | tf_op jit(solution)/shard_map/ppermute | solution.py:120
  188.6 6.0 %collective-permute-start.33 = (bf16[2,32,1024]{2,1,0:T(8,128)(2,1)S(1)}, bf16[2,32,1024]{2,1,0:T(8,128)(2,1)S(1)}, u32[]{:S(2)}, u32[]{:S(2)}) collective-permute-start(bf16[2,32,1024]{2,1,0:T(8,128)(2,1)S(1)} %get-tuple-element.35), channel_id=1, source_target_pairs={{0,3},{1,0},{2,1},{3,2},{4,7},{5,4},{6,5},{7,6},{8,11},{9,8},{10,9... | collective-permute-start | bytes 393224 | tf_op jit(solution)/shard_map/ppermute | solution.py:119
  191.2 6.3 %collective-permute-start.35 = (bf16[2,32,1024]{2,1,0:T(8,128)(2,1)S(1)}, bf16[2,32,1024]{2,1,0:T(8,128)(2,1)S(1)}, u32[]{:S(2)}, u32[]{:S(2)}) collective-permute-start(bf16[2,32,1024]{2,1,0:T(8,128)(2,1)S(1)} %get-tuple-element.36), channel_id=1, source_target_pairs={{0,1},{1,2},{2,3},{3,0},{4,5},{5,6},{6,7},{7,4},{8,9},{9,10},{10,1... | collective-permute-start | bytes 393224 | tf_op jit(solution)/shard_map/ppermute | solution.py:120
  191.5 7.6 %collective-permute-start.25 = (bf16[2,32,2048]{2,1,0:T(8,128)(2,1)S(1)}, bf16[2,32,2048]{2,1,0:T(8,128)(2,1)S(1)}, u32[]{:S(2)}, u32[]{:S(2)}) collective-permute-start(bf16[2,32,2048]{2,1,0:T(8,128)(2,1)S(1)} %pad_maximum_fusion.5), channel_id=1, source_target_pairs={{0,12},{4,0},{8,4},{12,8},{1,13},{5,1},{9,5},{13,9},{2,14},{6,2},{... | collective-permute-start | bytes 786440 | tf_op jit(solution)/shard_map/ppermute | solution.py:125
  194.5 8.2 %collective-permute-start.27 = (bf16[2,32,2048]{2,1,0:T(8,128)(2,1)S(1)}, bf16[2,32,2048]{2,1,0:T(8,128)(2,1)S(1)}, u32[]{:S(2)}, u32[]{:S(2)}) collective-permute-start(bf16[2,32,2048]{2,1,0:T(8,128)(2,1)S(1)} %pad_maximum_fusion.6), channel_id=1, source_target_pairs={{0,4},{4,8},{8,12},{12,0},{1,5},{5,9},{9,13},{13,1},{2,6},{6,10},{... | collective-permute-start | bytes 786440 | tf_op jit(solution)/shard_map/ppermute | solution.py:126
  194.6 8.1 %collective-permute-start.34 = (bf16[2,32,2048]{2,1,0:T(8,128)(2,1)S(1)}, bf16[2,32,2048]{2,1,0:T(8,128)(2,1)S(1)}, u32[]{:S(2)}, u32[]{:S(2)}) collective-permute-start(bf16[2,32,2048]{2,1,0:T(8,128)(2,1)S(1)} %pad_maximum_fusion.7), channel_id=1, source_target_pairs={{0,3},{1,0},{2,1},{3,2},{4,7},{5,4},{6,5},{7,6},{8,11},{9,8},{10,9... | collective-permute-start | bytes 786440 | tf_op jit(solution)/shard_map/ppermute | solution.py:125
  197.6 7.7 %collective-permute-start.36 = (bf16[2,32,2048]{2,1,0:T(8,128)(2,1)S(1)}, bf16[2,32,2048]{2,1,0:T(8,128)(2,1)S(1)}, u32[]{:S(2)}, u32[]{:S(2)}) collective-permute-start(bf16[2,32,2048]{2,1,0:T(8,128)(2,1)S(1)} %pad_maximum_fusion.8), channel_id=1, source_target_pairs={{0,1},{1,2},{2,3},{3,0},{4,5},{5,6},{6,7},{7,4},{8,9},{9,10},{10,1... | collective-permute-start | bytes 786440 | tf_op jit(solution)/shard_map/ppermute | solution.py:126
  205.3 6.6 %collective-permute-start.28 = (bf16[32,2048]{1,0:T(8,128)(2,1)S(1)}, bf16[32,2048]{1,0:T(8,128)(2,1)S(1)}, u32[]{:S(2)}, u32[]{:S(2)}) collective-permute-start(bf16[32,2048]{1,0:T(8,128)(2,1)S(1)} %get-tuple-element.50), channel_id=1, source_target_pairs={{0,16},{16,0},{1,17},{17,1},{2,18},{18,2},{3,19},{19,3},{4,20},{20... | collective-permute-start | bytes 393224 | tf_op jit(solution)/shard_map/ppermute | solution.py:116
  206.3 6.9 %collective-permute-start.37 = (bf16[32,2048]{1,0:T(8,128)(2,1)S(1)}, bf16[32,2048]{1,0:T(8,128)(2,1)S(1)}, u32[]{:S(2)}, u32[]{:S(2)}) collective-permute-start(bf16[32,2048]{1,0:T(8,128)(2,1)S(1)} %get-tuple-element.49), channel_id=1, source_target_pairs={{0,16},{16,0},{1,17},{17,1},{2,18},{18,2},{3,19},{19,3},{4,20},{20... | collective-permute-start | bytes 393224 | tf_op jit(solution)/shard_map/ppermute | solution.py:116
